TPU v7x, 128 devices: a whole 4x4x4 slice. The times are simulated.
128 devices in a mesh: dop: 8 (over y, core), rng: 16 (over x, z).
Axes of the slice: x: 4, y: 4, z: 4, core: 2. Of those that a mesh axis runs over, the one named last changes fastest.
Arguments:
- echoes: bfloat16 [8192, 2, 32, 128], P(('rng', 'dop')), may hold values from -60 to 60
- training: int32 [128, 8192], P('dop', 'rng'), may hold values 0 or 1
- look_index: int32 [64], replicated, may hold values from 0 to 255
Outputs:
- beam_output: float32 [128, 2, 64, 8192], P('dop', None, None, 'rng')
All inputs are finite; a program needn't handle non-finite values. No bound on the sum of `training` on one device may be relied on, other than what follows from the above.
Results may differ from a plain program's by a relative error of at most 0.012.
The roundings to bfloat16 on the way count: a program that leaves them out, or rounds other values in their place, can miss the bound.
Values may be sent and summed in bfloat16 or wider, within the bound.
No kernel may reach another device: no remote copies, remote signals or barrier semaphores. Data moves between devices by JAX's collectives and lax.ppermute only.
A program may use at most 64 MiB of HBM per device.

v0:
```python
import jax
import jax.numpy as jnp
from jax import lax
from jax.sharding import PartitionSpec as P

CH = 32
PULSES = 128
LOOKS = 64
ANGLES = 256
SNAP = 192


loading = 0.1
epsilon = 1e-06
block_pairs = ((0, 0), (0, 1), (0, 2), (1, 1), (1, 2), (2, 2))


def padded(block, sides, width):
    for axis, dim in sides:
        count = lax.axis_size(axis)
        forward = [(i, i + 1) for i in range(count - 1)]
        forward.append((count - 1, 0))
        backward = [(target, source) for source, target in forward]
        low = lax.ppermute(
            lax.slice_in_dim(block, block.shape[dim] - width, None, axis=dim), axis, forward
        )
        high = lax.ppermute(lax.slice_in_dim(block, 0, width, axis=dim), axis, backward)
        block = jnp.concatenate([low, block, high], axis=dim)
    return block


def split_up(array, dim, count):
    dims = array.shape
    blocks = array.reshape(*dims[:dim], count, dims[dim] // count, *dims[dim + 1 :])
    return jnp.moveaxis(blocks, dim, 0)


def sum_at_owner(array, axis, dim):
    blocks = split_up(array, dim, lax.axis_size(axis))
    arrived = lax.all_to_all(blocks, axis, split_axis=0, concat_axis=0, tiled=True)
    return arrived.sum(axis=0)


def in_order(blocks, dim):
    dims = list(blocks.shape[1:])
    dims[dim] *= blocks.shape[0]
    return jnp.moveaxis(blocks, 0, dim).reshape(dims)


def copy_for_each(array, axis):
    count = lax.axis_size(axis)
    return lax.all_to_all(
        jnp.broadcast_to(array[None], (count, *array.shape)), axis, 0, 0, tiled=True
    )


def gather_directly(array, axis, dim):
    return in_order(copy_for_each(array, axis), dim)


def twiddles():
    pulse_ids = jnp.arange(PULSES, dtype=jnp.int32)
    phase_ids = pulse_ids[:, None] * pulse_ids[None, :] % PULSES
    angles = phase_ids.astype(jnp.float32) * (2.0 * jnp.pi / PULSES)
    return jnp.concatenate([jnp.cos(angles), jnp.sin(angles)], axis=0).astype(jnp.bfloat16)


def doppler_spectra(echo_rows, twiddle):
    product = jnp.einsum("kp,rqcp->krqc", twiddle, echo_rows, preferred_element_type=jnp.float32)
    cosine = product[:PULSES]
    sine = product[PULSES:]
    real_part = cosine[:, :, 0] + sine[:, :, 1]
    imag_part = cosine[:, :, 1] - sine[:, :, 0]
    return (
        jnp.stack([real_part, imag_part], axis=2)
        .reshape(PULSES, echo_rows.shape[0], 2 * CH)
        .astype(jnp.bfloat16)
    )


def steering(look_index):
    sines = -1.0 + (2.0 * look_index.astype(jnp.float32) + 1.0) / ANGLES
    channel_ids = jnp.arange(CH).astype(jnp.float32)
    phases = jnp.pi * channel_ids[:, None] * sines[None, :]
    zeros = jnp.zeros((CH, LOOKS), jnp.float32)
    return jnp.stack([zeros, zeros, jnp.cos(phases), jnp.sin(phases), zeros, zeros]).reshape(
        SNAP, LOOKS
    )


def mvdr_weights(upper_blocks, steer):
    bin_count = upper_blocks.shape[0]
    gram_grid = upper_blocks.reshape(bin_count, 6, CH, 2, CH)
    lower_rows = jnp.stack([-gram_grid[:, :, :, 1], gram_grid[:, :, :, 0]], axis=3)
    blocks = jnp.stack([gram_grid, lower_rows], axis=2).reshape(bin_count, 6, 2 * CH, 2 * CH)
    row_list = []
    for left_pos in range(3):
        pieces = []
        for right_pos in range(3):
            if left_pos <= right_pos:
                pieces.append(blocks[:, block_pairs.index((left_pos, right_pos))])
            else:
                pieces.append(
                    jnp.swapaxes(blocks[:, block_pairs.index((right_pos, left_pos))], 1, 2)
                )
        row_list.append(jnp.concatenate(pieces, axis=2))
    matrix = jnp.concatenate(row_list, axis=1)
    power = jnp.trace(matrix, axis1=1, axis2=2) / SNAP + epsilon
    regular = matrix / power[:, None, None] + loading * jnp.eye(SNAP, dtype=jnp.float32)
    factor = jnp.linalg.cholesky(regular)
    targets = jnp.broadcast_to(steer, (bin_count, SNAP, LOOKS))
    forward = lax.linalg.triangular_solve(factor, targets, left_side=True, lower=True)
    solved = lax.linalg.triangular_solve(
        factor, forward, left_side=True, lower=True, transpose_a=True
    )
    gains = jnp.sum(targets * solved, axis=1)
    unit = solved / jnp.sqrt(gains)[:, None, :]
    shaped = unit.reshape(bin_count, 3, 2, CH, LOOKS)
    rotated = jnp.stack([-shaped[:, :, 1], shaped[:, :, 0]], axis=2)
    return jnp.concatenate([unit, rotated.reshape(bin_count, SNAP, LOOKS)], axis=2).astype(
        jnp.bfloat16
    )


def body(echoes, training, look_index):
    spectra = doppler_spectra(echoes, twiddles())
    groups = lax.axis_size("dop")
    bins_here = PULSES // groups
    turned = lax.all_to_all(spectra, "dop", split_axis=0, concat_axis=1, tiled=True)
    edged = padded(turned, (("dop", 0),), 1)
    mask_rows = training.astype(jnp.bfloat16)
    steer = steering(look_index)
    share_bins = bins_here // lax.axis_size("rng")
    bin_count = share_bins * lax.axis_size("rng")
    slab_rows = edged
    weighting = mask_rows[:, :, None]
    products = []
    for left_pos, right_pos in block_pairs:
        masked = slab_rows[left_pos : left_pos + bin_count] * weighting
        products.append(
            jnp.einsum(
                "krn,krm->knm",
                masked,
                slab_rows[right_pos : right_pos + bin_count],
                preferred_element_type=jnp.float32,
            )
        )
    gram_blocks = jnp.stack(products, axis=1).reshape(bin_count, 6, 2, CH, 2, CH)
    flip_sign = jnp.array([1.0, -1.0], jnp.float32).reshape(1, 1, 1, 2, 1)
    upper_half = gram_blocks[:, :, 0] + flip_sign * gram_blocks[:, :, 1][:, :, :, ::-1, :]
    my_gram = sum_at_owner(upper_half.reshape(bin_count, 6 * CH, 2 * CH), "rng", 0)
    weight_piece = gather_directly(mvdr_weights(my_gram, steer), "rng", 0)
    bin_count = weight_piece.shape[0]
    slab_rows = edged
    weight_parts = weight_piece.reshape(bin_count, 3, 2 * CH, 2 * LOOKS)
    summed = jnp.einsum(
        "knj,krn->kjr",
        weight_parts[:, 0],
        slab_rows[0:bin_count],
        preferred_element_type=jnp.float32,
    )
    for position in range(1, 3):
        summed = summed + jnp.einsum(
            "knj,krn->kjr",
            weight_parts[:, position],
            slab_rows[position : position + bin_count],
            preferred_element_type=jnp.float32,
        )
    return summed.reshape(bin_count, 2, LOOKS, slab_rows.shape[1])


def solution(mesh):
    in_specs = (P(("rng", "dop"), None, None, None), P("dop", "rng"), P())
    out_specs = P("dop", None, None, "rng")
    return jax.shard_map(body, mesh=mesh, in_specs=in_specs, out_specs=out_specs, check_vma=False)
```

profile of v0, /device:TPU:24, one launch (start us, length us, event | category | flops | bytes accessed | tf_op | source)
XLA Modules:
  0.0 211.5 jit_solution(4196096061238054398)
XLA Ops:
  0.3 0.9 copy-done
  1.2 0.9 fusion.18
  2.6 3.5 %copy.64 = bf16[128,64,64]{2,1,0:T(8,128)(2,1)S(1)} copy(bf16[128,64,64]{0,1,2:T(8,128)(2,1)S(1)} %bitcast.139) | data formatting | bytes 2097152 | tf_op jit(solution)/shard_map/convert_element_type | solution.py:77
  6.1 2.7 %reshape.523 = bf16[8,2,32768]{2,1,0:T(2,128)(2,1)} reshape(bf16[128,64,64]{2,1,0:T(8,128)(2,1)S(1)} %copy.64) | data formatting | bytes 2097152
  8.7 4.7 %all-to-all-start = ((bf16[8,2,32768]{2,1,0:T(2,128)(2,1)}), bf16[8,2,32768]{2,1,0:T(2,128)(2,1)S(1)}, u32[]{:S(2)}, u32[]{:S(2)}) async-start(bf16[8,2,32768]{2,1,0:T(2,128)(2,1)} %reshape.523), calls=%async_computation | async-start | bytes 2097152 | tf_op jit(solution)/shard_map/all_to_all | solution.py:129
  13.4 13.8 %all-to-all-done = bf16[8,2,32768]{2,1,0:T(2,128)(2,1)S(1)} async-done(((bf16[8,2,32768]{2,1,0:T(2,128)(2,1)}), bf16[8,2,32768]{2,1,0:T(2,128)(2,1)S(1)}, u32[]{:S(2)}, u32[]{:S(2)}) %all-to-all-start) | async-done | bytes 1048608 | tf_op jit(solution)/shard_map/all_to_all | solution.py:129
  27.3 1.4 reshape.524
  28.7 2.8 %copy.66 = bf16[16,8,64,64]{2,1,3,0:T(8,128)(2,1)} copy(bf16[16,8,64,64]{3,2,0,1:T(8,128)(2,1)S(1)} %bitcast.137) | data formatting | bytes 2097152 | tf_op jit(solution)/shard_map/all_to_all | solution.py:129
  31.6 3.2 %all_to_all.22 = bf16[16,512,64]{1,2,0:T(8,128)(2,1)S(1)} reshape(bf16[16,8,64,64]{2,1,3,0:T(8,128)(2,1)} %copy.66) | data formatting | bytes 2097152 | tf_op jit(solution)/shard_map/all_to_all | solution.py:129
  35.0 1.7 collective-permute-start.1
  36.7 0.4 fusion.5
  37.2 0.6 stack.51
  37.8 0.8 collective-permute-done
  38.6 1.2 fusion.11
  39.8 1.6 stack.48
  41.4 1.2 fusion.9
  42.7 1.0 constant_dynamic-update-slice_fusion.5
  43.7 1.6 stack.49
  45.4 1.3 fusion.7
  46.6 2.6 %stack.50 = f32[16,1,2,32,2,32]{5,4,3,2,0,1:T(2,128)} reshape(f32[16,64,64]{2,1,0:T(8,128)} %fusion.7) | data formatting | bytes 524288 | tf_op jit(solution)/shard_map/stack | solution.py:148
  49.3 1.2 fusion.3
  50.5 2.7 %stack.52 = f32[16,1,2,32,2,32]{5,4,3,2,0,1:T(2,128)} reshape(f32[16,64,64]{2,1,0:T(8,128)} %fusion.3) | data formatting | bytes 524288 | tf_op jit(solution)/shard_map/stack | solution.py:148
  53.1 1.3 fusion.1
  54.4 2.7 %stack.53 = f32[16,1,2,32,2,32]{5,4,3,2,0,1:T(2,128)} reshape(f32[16,64,64]{2,1,0:T(8,128)} %fusion.1) | data formatting | bytes 524288 | tf_op jit(solution)/shard_map/stack | solution.py:148
  57.0 1.1 constant_dynamic-update-slice_fusion.4
  58.1 2.3 %constant_dynamic-update-slice_fusion.3 = f32[16,6,2,32,2,32]{5,4,3,2,0,1:T(2,128)} fusion(f32[16,6,2,32,2,32]{5,4,3,2,0,1:T(2,128)} %constant_dynamic-update-slice_fusion.4, f32[16,1,2,32,2,32]{5,4,3,2,0,1:T(2,128)} %stack.50), kind=kLoop, calls=%fused_computation.123 | loop fusion | bytes 2097152
  60.5 1.1 constant_dynamic-update-slice_fusion.2
  61.6 1.0 constant_dynamic-update-slice_fusion.1
  62.6 1.1 constant_dynamic-update-slice_fusion
  63.7 8.5 %fusion.57 = (f32[16,6,1,32,2,32]{5,4,3,2,0,1:T(2,128)S(1)}, f32[16,6,1,32,2,32]{5,4,3,2,0,1:T(2,128)}) fusion(f32[16,6,2,32,2,32]{5,4,3,2,0,1:T(2,128)} %constant_dynamic-update-slice_fusion), kind=kLoop, calls=%fused_computation.139 | loop fusion | bytes 3145728 | tf_op jit(solution)/shard_map/slice | solution.py:150
  72.1 1.9 copy.104
  74.0 19.8 %rev.3 = f32[16,6,32,2,32]{4,3,2,1,0:T(2,128)} reverse(f32[16,6,32,2,32]{4,3,2,1,0:T(2,128)} %bitcast.136), dimensions={3} | reverse | bytes 1572864 | tf_op jit(solution)/shard_map/rev | solution.py:150
  93.8 8.6 %fusion = f32[16,6,32,2,32]{4,3,2,1,0:T(2,128)} fusion(f32[16,6,1,32,2,32]{5,4,3,2,0,1:T(2,128)} %get-tuple-element.26, f32[16,6,32,2,32]{4,3,2,1,0:T(2,128)} %rev.3, f32[2]{0:T(128)S(1)} %copy-done.5), kind=kLoop, calls=%fused_computation.3 | loop fusion | flops 393216 | bytes 2359304 | tf_op jit(solution)/shard_map/add | solution.py:150
  102.4 4.3 %reshape_reshape.6 = f32[16,1,192,64]{3,2,0,1:T(8,128)} reshape(f32[16,6,32,2,32]{4,3,2,1,0:T(2,128)} %fusion) | data formatting | bytes 1572864 | tf_op jit(solution)/shard_map/reshape;reshape | solution.py:34
  106.7 3.0 %copy.74 = f32[16,1,192,64]{2,3,1,0:T(8,128)} copy(f32[16,1,192,64]{3,2,0,1:T(8,128)} %reshape_reshape.6) | data formatting | bytes 1572864 | tf_op jit(solution)/shard_map/reshape;reshape | solution.py:34
  109.7 7.9 %all-to-all-start.1 = ((f32[16,1,192,64]{2,3,1,0:T(8,128)}), f32[16,1,192,64]{2,3,1,0:T(8,128)S(1)}, u32[]{:S(2)}, u32[]{:S(2)}) async-start(f32[16,1,192,64]{2,3,1,0:T(8,128)} %copy.74), calls=%async_computation.1 | async-start | bytes 2097152 | tf_op jit(solution)/shard_map/all_to_all | solution.py:40
  117.8 17.5 %all-to-all-done.1 = f32[16,1,192,64]{2,3,1,0:T(8,128)S(1)} async-done(((f32[16,1,192,64]{2,3,1,0:T(8,128)}), f32[16,1,192,64]{2,3,1,0:T(8,128)S(1)}, u32[]{:S(2)}, u32[]{:S(2)}) %all-to-all-start.1) | async-done | bytes 786464 | tf_op jit(solution)/shard_map/all_to_all | solution.py:40
  137.2 0.6 fusion.30
  138.8 11.7 %custom-call.18 = f32[1,128,128]{2,1,0:T(8,128)S(1)} custom-call(f32[1,128,128]{2,1,0:T(8,128)S(1)} %cholesky.120), custom_call_target="Cholesky" | custom-call | tf_op jit(solution)/shard_map/jit(cholesky)/cholesky | solution.py:110
  150.6 9.8 %custom-call.19 = f32[1,1,128,128]{2,3,1,0:T(8,128)S(1)} custom-call(f32[1,1,128,128]{3,2,1,0:T(8,128)S(1)} %get-tuple-element.45), custom_call_target="InvertDiagBlocksLowerTriangular" | custom-call | tf_op jit(solution)/shard_map/jit(cholesky)/cholesky | solution.py:110
  160.8 5.8 %custom-call.20 = f32[1,64,64]{2,1,0:T(8,128)S(1)} custom-call(f32[1,64,64]{2,1,0:T(8,128)S(1)} %fusion.13), custom_call_target="Cholesky" | custom-call | tf_op jit(solution)/shard_map/jit(cholesky)/cholesky | solution.py:110
  166.7 0.7 compare_reduce_fusion
  167.3 0.6 compare_reduce_fusion.1
  169.4 19.9 %custom-call.21 = f32[1,2,128,128]{2,3,1,0:T(8,128)S(1)} custom-call(f32[1,2,128,128]{3,2,1,0:T(8,128)S(1)} %pad_maximum_fusion.14), custom_call_target="InvertDiagBlocksLowerTriangular" | custom-call | tf_op jit(solution)/shard_map/triangular_solve | solution.py:113
  191.5 15.7 %all_to_all.28 = bf16[16,1,192,128]{3,2,1,0:T(8,128)(2,1)S(1)} all-to-all(bf16[16,1,192,128]{3,2,1,0:T(8,128)(2,1)S(1)} %broadcast_in_dim.12), channel_id=1, replica_groups=mesh['dop'=8,'rng'=16] {'rng'}, dimensions={0} | all-to-all | bytes 1572864 | tf_op jit(solution)/shard_map/all_to_all | solution.py:52
  207.2 0.8 fusion.28
  208.0 0.7 fusion.26
  208.7 2.8 %add_add_fusion = f32[16,128,512]{2,1,0:T(8,128)} fusion(f32[16,128,512]{2,1,0:T(8,128)S(1)} %fusion.26, f32[16,128,512]{2,1,0:T(8,128)S(1)} %fusion.28, bf16[1,512,64]{1,2,0:T(8,128)(2,1)S(1)} %collective-permute-done.1, bf16[16,512,64]{1,2,0:T(8,128)(2,1)S(1)} %all_to_all.22, bf16[16,3,64,128]{3,2,1,0:T(8,128)(2,1)S(1)} %bitcast.142), kind=kOutput, calls=%fused_computation | convolution fusion | flops 136839168 | bytes 13959168 | tf_op jit(solution)/shard_map/knj,krn->kjr/dot_general | solution.py:163
  (78 shorter events, 5.9 us)
Async XLA Ops:
  0.0 1.2 copy-start
  2.5 10.9 %copy-start.4 = (s32[16,512]{1,0:T(8,128)S(1)}, s32[16,512]{1,0:T(8,128)}, u32[]{:S(2)}) copy-start(s32[16,512]{1,0:T(8,128)} %param.5) | copy-start | bytes 98308
  8.7 18.6 %all-to-all-start = ((bf16[8,2,32768]{2,1,0:T(2,128)(2,1)}), bf16[8,2,32768]{2,1,0:T(2,128)(2,1)S(1)}, u32[]{:S(2)}, u32[]{:S(2)}) async-start(bf16[8,2,32768]{2,1,0:T(2,128)(2,1)} %reshape.523), calls=%async_computation | async-start | bytes 2097152 | tf_op jit(solution)/shard_map/all_to_all | solution.py:129
  34.9 3.7 %collective-permute-start = (bf16[1,512,64]{1,2,0:T(8,128)(2,1)S(1)}, bf16[1,512,64]{1,2,0:T(8,128)(2,1)S(1)}, u32[]{:S(2)}, u32[]{:S(2)}) collective-permute-start(bf16[1,512,64]{1,2,0:T(8,128)(2,1)S(1)} %copy.90), channel_id=1, source_target_pairs={{0,16},{16,32},{32,48},{48,64},{64,80},{80,96},{96,112},{112,0},{1... | collective-permute-start | bytes 196616 | tf_op jit(solution)/shard_map/ppermute | solution.py:24
  35.0 10.4 %collective-permute-start.1 = (bf16[1,512,64]{1,2,0:T(8,128)(2,1)S(1)}, bf16[1,512,64]{1,2,0:T(8,128)(2,1)S(1)}, u32[]{:S(2)}, u32[]{:S(2)}) collective-permute-start(bf16[1,512,64]{1,2,0:T(8,128)(2,1)S(1)} %copy.91), channel_id=1, source_target_pairs={{16,0},{32,16},{48,32},{64,48},{80,64},{96,80},{112,96},{0,112},{1... | collective-permute-start | bytes 196616 | tf_op jit(solution)/shard_map/ppermute | solution.py:27
  57.0 4.5 %copy-start.2 = (f32[16,1,2,32,2,32]{5,4,3,2,0,1:T(2,128)S(1)}, f32[16,1,2,32,2,32]{5,4,3,2,0,1:T(2,128)}, u32[]{:S(2)}) copy-start(f32[16,1,2,32,2,32]{5,4,3,2,0,1:T(2,128)} %stack.52) | copy-start | bytes 786436
  57.0 5.6 %copy-start.3 = (f32[16,1,2,32,2,32]{5,4,3,2,0,1:T(2,128)S(1)}, f32[16,1,2,32,2,32]{5,4,3,2,0,1:T(2,128)}, u32[]{:S(2)}) copy-start(f32[16,1,2,32,2,32]{5,4,3,2,0,1:T(2,128)} %stack.53) | copy-start | bytes 786436
  74.0 19.8 %copy-start.5 = (f32[2]{0:T(128)S(1)}, f32[2]{0:T(128)}, u32[]{:S(2)}) copy-start(f32[2]{0:T(128)} %constant.146.clone) | copy-start | bytes 28
  102.4 15.2 %copy-start.6 = (s32[64]{0:T(128)S(1)}, s32[64]{0:T(128)}, u32[]{:S(2)}) copy-start(s32[64]{0:T(128)} %param.6) | copy-start | bytes 772
  109.7 25.6 %all-to-all-start.1 = ((f32[16,1,192,64]{2,3,1,0:T(8,128)}), f32[16,1,192,64]{2,3,1,0:T(8,128)S(1)}, u32[]{:S(2)}, u32[]{:S(2)}) async-start(f32[16,1,192,64]{2,3,1,0:T(8,128)} %copy.74), calls=%async_computation.1 | async-start | bytes 2097152 | tf_op jit(solution)/shard_map/all_to_all | solution.py:40
  208.0 3.6 %copy-start.1 = (bf16[64,2,32,128]{3,2,1,0:T(8,128)(2,1)S(1)}, bf16[64,2,32,128]{3,2,1,0:T(8,128)(2,1)}, u32[]{:S(2)}) copy-start(bf16[64,2,32,128]{3,2,1,0:T(8,128)(2,1)} %param.4) | copy-start | bytes 3145732
where the time goes:
time: 213 us; the launch traced here: 212 us
  local copies, waits for them, and re-layouts  73.3 us (34%)
  other arithmetic  60.2 us (28%)
  waiting for transfers between devices  32.1 us (15%)
  blocking collectives  15.7 us (7%)
  starting transfers between devices  14.3 us (7%)
  matrix products  13.5 us (6%)
  between operations  2.45 us (1%)
    another operation x7, other arithmetic, mvdr_weights(): factor = jnp.linalg.cholesky(regular)  28.7 us
    another operation x6, other arithmetic, mvdr_weights(): lax.linalg.triangular_solve(factor, forward, left_side=True, lower=True,...  20.1 us
    rev x1, local copies, waits for them, and re-layouts, body(): gram_blocks[:, :, 1][:, :, :, ::-1, :]  19.8 us
    all_to_all x1, waiting for transfers between devices, sum_at_owner(): lax.all_to_all(blocks, axis, split_axis=0, concat_axis=0, tiled=True)  17.5 us
    all_to_all x1, blocking collectives, copy_for_each(): lax.all_to_all(jnp.broadcast_to(array[None], (count, *array.shape)), axis...  15.7 us
    all_to_all x1, waiting for transfers between devices, body(): lax.all_to_all(spectra, 'dop', split_axis=0, concat_axis=1, tiled=True)  13.8 us
    unnamed x22, local copies, waits for them, and re-layouts  13.5 us
    another operation x7, local copies, waits for them, and re-layouts, body(): jnp.stack(products, axis=1).reshape(bin_count, 6, 2, CH, 2, CH)  12.9 us
  transfers between devices with their start and end apart: 4, of which 3 were waited for; matrix products, arithmetic and copies ran while one was open for 4% of the time, Pallas kernels for 0%

commit v1 on v0

--- a/solution.py
+++ b/solution.py
@@ -88,23 +88,50 @@
     )
 
 
-def mvdr_weights(upper_blocks, steer):
-    bin_count = upper_blocks.shape[0]
-    gram_grid = upper_blocks.reshape(bin_count, 6, CH, 2, CH)
-    lower_rows = jnp.stack([-gram_grid[:, :, :, 1], gram_grid[:, :, :, 0]], axis=3)
-    blocks = jnp.stack([gram_grid, lower_rows], axis=2).reshape(bin_count, 6, 2 * CH, 2 * CH)
-    row_list = []
+def rotate(values):
+    return jnp.concatenate([-values[..., CH:], values[..., :CH]], axis=-1)
+
+
+def upper_blocks(edged, mask_rows):
+    bin_count = edged.shape[0] - 2
+    rotated = rotate(edged)
+    snap = jnp.concatenate([edged[b : b + bin_count] for b in range(3)], axis=-1)
+    turned_snap = jnp.concatenate([rotated[b : b + bin_count] for b in range(3)], axis=-1)
+    both = jnp.concatenate([snap, turned_snap], axis=1)
+    weighting = jnp.concatenate([mask_rows, mask_rows], axis=1)[:, :, None]
+    masked = both * weighting
+    pieces = []
     for left_pos in range(3):
-        pieces = []
-        for right_pos in range(3):
-            if left_pos <= right_pos:
-                pieces.append(blocks[:, block_pairs.index((left_pos, right_pos))])
-            else:
-                pieces.append(
-                    jnp.swapaxes(blocks[:, block_pairs.index((right_pos, left_pos))], 1, 2)
-                )
-        row_list.append(jnp.concatenate(pieces, axis=2))
-    matrix = jnp.concatenate(row_list, axis=1)
+        pieces.append(
+            jnp.einsum(
+                "krn,krm->knm",
+                masked[:, :, left_pos * 2 * CH : left_pos * 2 * CH + CH],
+                both[:, :, left_pos * 2 * CH :],
+                preferred_element_type=jnp.float32,
+            )
+        )
+    return jnp.concatenate(pieces, axis=-1)
+
+
+def full_from_upper(upper):
+    width = 2 * CH
+
+    def block(left_pos, right_pos):
+        if left_pos > right_pos:
+            return jnp.swapaxes(block(right_pos, left_pos), 1, 2)
+        start = block_pairs.index((left_pos, right_pos)) * width
+        piece = upper[:, :, start : start + width]
+        same, cross = piece[..., :CH], piece[..., CH:]
+        return jnp.concatenate(
+            [jnp.concatenate([same, cross], -1), jnp.concatenate([-cross, same], -1)], 1
+        )
+
+    rows = [jnp.concatenate([block(b, c) for c in range(3)], -1) for b in range(3)]
+    return jnp.concatenate(rows, 1)
+
+
+def unit_vectors(matrix, steer):
+    bin_count = matrix.shape[0]
     power = jnp.trace(matrix, axis1=1, axis2=2) / SNAP + epsilon
     regular = matrix / power[:, None, None] + loading * jnp.eye(SNAP, dtype=jnp.float32)
     factor = jnp.linalg.cholesky(regular)
@@ -114,59 +141,31 @@
         factor, forward, left_side=True, lower=True, transpose_a=True
     )
     gains = jnp.sum(targets * solved, axis=1)
-    unit = solved / jnp.sqrt(gains)[:, None, :]
-    shaped = unit.reshape(bin_count, 3, 2, CH, LOOKS)
-    rotated = jnp.stack([-shaped[:, :, 1], shaped[:, :, 0]], axis=2)
-    return jnp.concatenate([unit, rotated.reshape(bin_count, SNAP, LOOKS)], axis=2).astype(
-        jnp.bfloat16
-    )
+    return (solved / jnp.sqrt(gains)[:, None, :]).astype(jnp.bfloat16)
 
 
 def body(echoes, training, look_index):
     spectra = doppler_spectra(echoes, twiddles())
-    groups = lax.axis_size("dop")
-    bins_here = PULSES // groups
     turned = lax.all_to_all(spectra, "dop", split_axis=0, concat_axis=1, tiled=True)
     edged = padded(turned, (("dop", 0),), 1)
-    mask_rows = training.astype(jnp.bfloat16)
-    steer = steering(look_index)
-    share_bins = bins_here // lax.axis_size("rng")
-    bin_count = share_bins * lax.axis_size("rng")
-    slab_rows = edged
-    weighting = mask_rows[:, :, None]
-    products = []
-    for left_pos, right_pos in block_pairs:
-        masked = slab_rows[left_pos : left_pos + bin_count] * weighting
-        products.append(
-            jnp.einsum(
-                "krn,krm->knm",
-                masked,
-                slab_rows[right_pos : right_pos + bin_count],
-                preferred_element_type=jnp.float32,
-            )
-        )
-    gram_blocks = jnp.stack(products, axis=1).reshape(bin_count, 6, 2, CH, 2, CH)
-    flip_sign = jnp.array([1.0, -1.0], jnp.float32).reshape(1, 1, 1, 2, 1)
-    upper_half = gram_blocks[:, :, 0] + flip_sign * gram_blocks[:, :, 1][:, :, :, ::-1, :]
-    my_gram = sum_at_owner(upper_half.reshape(bin_count, 6 * CH, 2 * CH), "rng", 0)
-    weight_piece = gather_directly(mvdr_weights(my_gram, steer), "rng", 0)
-    bin_count = weight_piece.shape[0]
-    slab_rows = edged
-    weight_parts = weight_piece.reshape(bin_count, 3, 2 * CH, 2 * LOOKS)
-    summed = jnp.einsum(
-        "knj,krn->kjr",
-        weight_parts[:, 0],
-        slab_rows[0:bin_count],
-        preferred_element_type=jnp.float32,
-    )
-    for position in range(1, 3):
-        summed = summed + jnp.einsum(
+    bin_count = edged.shape[0] - 2
+    upper = upper_blocks(edged, training.astype(jnp.bfloat16))
+    my_upper = lax.psum_scatter(upper, "rng", scatter_dimension=0, tiled=True)
+    my_unit = unit_vectors(full_from_upper(my_upper), steering(look_index))
+    unit = lax.all_gather(my_unit, "rng", axis=0, tiled=True)
+    shaped = unit.reshape(bin_count, 3, 2, CH, LOOKS)
+    rotated = jnp.stack([-shaped[:, :, 1], shaped[:, :, 0]], axis=2).reshape(bin_count, SNAP, LOOKS)
+    weights = jnp.concatenate([unit, rotated], axis=2)
+    summed = None
+    for position in range(3):
+        term = jnp.einsum(
             "knj,krn->kjr",
-            weight_parts[:, position],
-            slab_rows[position : position + bin_count],
+            weights[:, position * 2 * CH : (position + 1) * 2 * CH],
+            edged[position : position + bin_count],
             preferred_element_type=jnp.float32,
         )
-    return summed.reshape(bin_count, 2, LOOKS, slab_rows.shape[1])
+        summed = term if summed is None else summed + term
+    return summed.reshape(bin_count, 2, LOOKS, edged.shape[1])
 
 
 def solution(mesh):

time: 213 us -> 245 us (1.15)
  waiting for transfers between devices: 32.1 us -> 107 us
  local copies, waits for them, and re-layouts: 73.3 us -> 22 us
  between operations: 2.45 us -> 15.8 us
  starting transfers between devices: 14.3 us -> 6.43 us
  blocking collectives: 15.7 us -> 23.3 us
    unnamed x0 -> x2, waiting for transfers between devices: none -> 90.8 us
    all_gather x0 -> x1, blocking collectives: none -> 23.3 us  [body(): unit = lax.all_gather(my_unit, 'rng', axis=0, tiled=True)]
    another operation x18 -> x6, local copies, waits for them, and re-layouts: 20.6 us -> 0.11 us  [the longest x1 0.08 us: unit_vectors(): targets = jnp.broadcast_to(steer, (bin_count, SNAP, LOOKS))]
    rev x1 -> x0, local copies, waits for them, and re-layouts: 19.8 us -> none  [body(): gram_blocks[:, :, 1][:, :, :, ::-1, :]]
    all_to_all x1 -> x0, waiting for transfers between devices: 17.5 us -> none  [sum_at_owner(): lax.all_to_all(blocks, axis, split_axis=0, concat_axis=0, tiled=True)]
    all_to_all x1 -> x0, blocking collectives: 15.7 us -> none  [copy_for_each(): lax.all_to_all(jnp.broadcast_to(array[None], (count, *array.shape)), axis...]
    add x2 -> x1, other arithmetic: 8.73 us -> 0.12 us  [unit_vectors(): matrix / power[:, None, None] + loading * jnp.eye(SNAP, dtype=jnp.float32)]
    slice x2 -> x0, local copies, waits for them, and re-layouts: 8.46 us -> none  [the longest x1 8.46 us: body(): gram_blocks[:, :, 1][:, :, :, ::-1, :]]
  transfers between devices with their start and end apart: 4 -> 4, of which waited for: 3 -> 3; matrix products, arithmetic and copies ran while one was open for 4% -> 2% of each run, Pallas kernels for 0% -> 0%
where the time goes in v1:
time: 245 us; the launch traced here: 244 us
  waiting for transfers between devices  107 us (44%)
  other arithmetic  58.7 us (24%)
  blocking collectives  23.3 us (10%)
  local copies, waits for them, and re-layouts  22 us (9%)
  between operations  15.8 us (6%)
  matrix products  11.3 us (5%)
  starting transfers between devices  6.43 us (3%)
    unnamed x2, waiting for transfers between devices  90.8 us
    another operation x7, other arithmetic, unit_vectors(): factor = jnp.linalg.cholesky(regular)  28.7 us
    all_gather x1, blocking collectives, body(): unit = lax.all_gather(my_unit, 'rng', axis=0, tiled=True)  23.3 us
    another operation x6, other arithmetic, unit_vectors(): lax.linalg.triangular_solve(factor, forward, left_side=True, lower=True,...  20 us
    all_to_all x1, waiting for transfers between devices, body(): lax.all_to_all(spectra, 'dop', split_axis=0, concat_axis=1, tiled=True)  13.9 us
    unnamed x29, local copies, waits for them, and re-layouts  8.59 us
    all_to_all x2, local copies, waits for them, and re-layouts, body(): lax.all_to_all(spectra, 'dop', split_axis=0, concat_axis=1, tiled=True)  6.02 us
  transfers between devices with their start and end apart: 4, of which 3 were waited for; matrix products, arithmetic and copies ran while one was open for 2% of the time, Pallas kernels for 0%

profile of v1, /device:TPU:24, one launch (start us, length us, event | category | flops | bytes accessed | tf_op | source)
XLA Modules:
  0.0 244.3 jit_solution(15445949804251667537)
XLA Ops:
  6.5 0.3 sine_convert_fusion
  6.8 0.9 copy-done
  7.8 0.9 fusion.17
  8.7 0.3 fusion.16
  9.0 1.1 pad_maximum_fusion.3
  10.0 4.7 %copy.97 = bf16[128,64,64]{2,1,0:T(8,128)(2,1)S(1)} copy(bf16[128,64,64]{0,1,2:T(8,128)(2,1)} %bitcast.103) | data formatting | bytes 2097152 | tf_op jit(solution)/shard_map/convert_element_type | solution.py:77
  14.8 2.7 %reshape.480 = bf16[8,2,32768]{2,1,0:T(2,128)(2,1)} reshape(bf16[128,64,64]{2,1,0:T(8,128)(2,1)S(1)} %copy.97) | data formatting | bytes 2097152
  17.4 4.7 %all-to-all-start = ((bf16[8,2,32768]{2,1,0:T(2,128)(2,1)}), bf16[8,2,32768]{2,1,0:T(2,128)(2,1)}, u32[]{:S(2)}, u32[]{:S(2)}) async-start(bf16[8,2,32768]{2,1,0:T(2,128)(2,1)} %reshape.480), calls=%async_computation | async-start | bytes 2097152 | tf_op jit(solution)/shard_map/all_to_all | solution.py:149
  22.2 13.9 %all-to-all-done = bf16[8,2,32768]{2,1,0:T(2,128)(2,1)} async-done(((bf16[8,2,32768]{2,1,0:T(2,128)(2,1)}), bf16[8,2,32768]{2,1,0:T(2,128)(2,1)}, u32[]{:S(2)}, u32[]{:S(2)}) %all-to-all-start) | async-done | bytes 1048608 | tf_op jit(solution)/shard_map/all_to_all | solution.py:149
  36.1 3.1 %reshape.481 = bf16[128,64,64]{2,1,0:T(8,128)(2,1)S(1)} reshape(bf16[8,2,32768]{2,1,0:T(2,128)(2,1)} %all-to-all-done) | data formatting | bytes 2097152
  39.4 2.8 %copy.99 = bf16[16,8,64,64]{2,1,3,0:T(8,128)(2,1)} copy(bf16[16,8,64,64]{3,2,0,1:T(8,128)(2,1)S(1)} %bitcast.102) | data formatting | bytes 2097152 | tf_op jit(solution)/shard_map/all_to_all | solution.py:149
  42.2 3.2 %all_to_all.16 = bf16[16,512,64]{1,2,0:T(8,128)(2,1)S(1)} reshape(bf16[16,8,64,64]{2,1,3,0:T(8,128)(2,1)} %copy.99) | data formatting | bytes 2097152 | tf_op jit(solution)/shard_map/all_to_all | solution.py:149
  45.5 1.7 collective-permute-start.1
  47.2 1.9 collective-permute-done.1
  49.1 0.3 pad_maximum_fusion.1
  49.5 0.3 fusion.10
  49.8 2.6 %broadcast_multiply_fusion = (bf16[16,1024,192]{1,2,0:T(8,128)(2,1)S(1)}, bf16[16,1024,192]{1,2,0:T(8,128)(2,1)S(1)}) fusion(bf16[16,1024]{1,0:T(8,128)(2,1)S(1)} %pad_maximum_fusion.13, bf16[18,512,32]{1,2,0:T(8,128)(2,1)S(1)} %get-tuple-element.34, bf16[18,512,32]{1,2,0:T(8,128)(2,1)S(1)} %get-tuple-element.33, ...), kind=kLoop, calls=%fused_computation.6 | loop fusion | flops 53477376 | bytes 19038208 | tf_op jit(solution)/shard_map/mul | solution.py:102
  52.5 2.0 fusion.13
  54.5 1.5 fusion.2
  56.1 0.7 fusion.4
  56.7 1.2 pad_maximum_fusion.4
  58.2 0.6 dynamic-slice.5
  58.8 90.8 %all-reduce.6.cloned.1.call-done = f32[16,32,384]{2,1,0:T(8,128)} async-done(((f32[16,32,384]{2,1,0:T(8,128)}), f32[16,32,384]{2,1,0:T(8,128)}) %all-reduce.6.cloned.1.call-update) | async-done | bytes 786448
  149.7 1.8 constant_dynamic-slice_fusion.12
  152.0 1.6 constant_dynamic-slice_fusion.13
  154.7 0.6 fusion.28
  156.3 11.7 %custom-call.18 = f32[1,128,128]{2,1,0:T(8,128)S(1)} custom-call(f32[1,128,128]{2,1,0:T(8,128)S(1)} %cholesky.120), custom_call_target="Cholesky" | custom-call | tf_op jit(solution)/shard_map/jit(cholesky)/cholesky | solution.py:137
  168.1 9.8 %custom-call.19 = f32[1,1,128,128]{2,3,1,0:T(8,128)S(1)} custom-call(f32[1,1,128,128]{3,2,1,0:T(8,128)S(1)} %get-tuple-element.59), custom_call_target="InvertDiagBlocksLowerTriangular" | custom-call | tf_op jit(solution)/shard_map/jit(cholesky)/cholesky | solution.py:137
  177.9 0.2 bitcast_dynamic-update-slice_fusion
  178.1 0.2 fusion.6
  178.2 5.8 %custom-call.20 = f32[1,64,64]{2,1,0:T(8,128)S(1)} custom-call(f32[1,64,64]{2,1,0:T(8,128)S(1)} %fusion.6), custom_call_target="Cholesky" | custom-call | tf_op jit(solution)/shard_map/jit(cholesky)/cholesky | solution.py:137
  184.1 0.7 compare_reduce_fusion
  184.8 0.6 compare_reduce_fusion.1
  186.8 19.9 %custom-call.21 = f32[1,2,128,128]{2,3,1,0:T(8,128)S(1)} custom-call(f32[1,2,128,128]{3,2,1,0:T(8,128)S(1)} %pad_maximum_fusion.10), custom_call_target="InvertDiagBlocksLowerTriangular" | custom-call | tf_op jit(solution)/shard_map/triangular_solve | solution.py:140
  206.7 0.3 fusion.33
  207.0 0.2 fusion.8
  207.2 0.2 fusion.43
  207.5 0.2 fusion.42
  207.7 0.2 convolution_subtract_fusion
  207.9 0.2 convolution_bitcast_fusion
  208.3 23.3 %all_gather.3 = bf16[16,192,64]{1,2,0:T(8,128)(2,1)S(1)} all-gather(bf16[1,192,64]{1,2,0:T(8,128)(2,1)S(1)} %divide_convert_fusion), channel_id=1, replica_groups=mesh['dop'=8,'rng'=16] {'rng'}, dimensions={0}, use_global_device_ids=true | all-gather | bytes 417792 | tf_op jit(solution)/shard_map/all_gather | solution.py:155
  231.6 0.4 copy.117
  232.1 0.2 pad_maximum_fusion.5
  232.3 0.8 fusion.20
  233.1 0.2 copy-done.2
  233.4 0.8 fusion.23
  234.2 0.4 copy-done.4
  234.6 2.9 %add_add_fusion = f32[16,128,512]{2,1,0:T(8,128)} fusion(f32[16,128,512]{2,1,0:T(8,128)S(1)} %fusion.23, f32[16,128,512]{2,1,0:T(8,128)S(1)} %fusion.20, bf16[16,512,64]{1,2,0:T(8,128)(2,1)S(1)} %copy-done.4, bf16[16,192,64]{2,1,0:T(8,128)(2,1)S(1)} %bitcast.100, bf16[16,192,64]{2,1,0:T(8,128)(2,1)S(1)} %copy.117), kind=kOutput, calls=%fused_computation.5 | convolution fusion | flops 136839168 | bytes 14417920 | tf_op jit(solution)/shard_map/knj,krn->kjr/dot_general | solution.py:161
  (71 shorter events, 3.0 us)
Async XLA Ops:
  6.5 1.2 copy-start
  10.0 12.1 %copy-start.5 = (s32[16,512]{1,0:T(8,128)S(1)}, s32[16,512]{1,0:T(8,128)}, u32[]{:S(2)}) copy-start(s32[16,512]{1,0:T(8,128)} %param.4) | copy-start | bytes 98308
  17.4 18.7 %all-to-all-start = ((bf16[8,2,32768]{2,1,0:T(2,128)(2,1)}), bf16[8,2,32768]{2,1,0:T(2,128)(2,1)}, u32[]{:S(2)}, u32[]{:S(2)}) async-start(bf16[8,2,32768]{2,1,0:T(2,128)(2,1)} %reshape.480), calls=%async_computation | async-start | bytes 2097152 | tf_op jit(solution)/shard_map/all_to_all | solution.py:149
  22.1 127.6 %all-reduce.6.cloned.1.call-start = ((), (), s32[]{:S(2)}) async-start(), calls=%async_computation.1 | async-start | bytes 1572864
  39.3 7.9 %collective-permute-start = (bf16[1,512,64]{1,2,0:T(8,128)(2,1)S(1)}, bf16[1,512,64]{1,2,0:T(8,128)(2,1)S(1)}, u32[]{:S(2)}, u32[]{:S(2)}) collective-permute-start(bf16[1,512,64]{1,2,0:T(8,128)(2,1)S(1)} %copy.120), channel_id=1, source_target_pairs={{0,16},{16,32},{32,48},{48,64},{64,80},{80,96},{96,112},{112,0},{1... | collective-permute-start | bytes 196616 | tf_op jit(solution)/shard_map/ppermute | solution.py:24
  45.5 3.6 %collective-permute-start.1 = (bf16[1,512,64]{1,2,0:T(8,128)(2,1)S(1)}, bf16[1,512,64]{1,2,0:T(8,128)(2,1)S(1)}, u32[]{:S(2)}, u32[]{:S(2)}) collective-permute-start(bf16[1,512,64]{1,2,0:T(8,128)(2,1)S(1)} %copy.121), channel_id=1, source_target_pairs={{16,0},{32,16},{48,32},{64,48},{80,64},{96,80},{112,96},{0,112},{1... | collective-permute-start | bytes 196616 | tf_op jit(solution)/shard_map/ppermute | solution.py:27
  49.4 3.0 %copy-start.1 = (bf16[16,512,64]{1,2,0:T(8,128)(2,1)}, bf16[16,512,64]{1,2,0:T(8,128)(2,1)S(1)}, u32[]{:S(2)}) copy-start(bf16[16,512,64]{1,2,0:T(8,128)(2,1)S(1)} %get-tuple-element.37) | copy-start | bytes 3145732
  49.4 3.0 %copy-start.3 = (bf16[16,512,64]{1,2,0:T(8,128)(2,1)}, bf16[16,512,64]{1,2,0:T(8,128)(2,1)S(1)}, u32[]{:S(2)}) copy-start(bf16[16,512,64]{1,2,0:T(8,128)(2,1)S(1)} %get-tuple-element.35) | copy-start | bytes 3145732
  56.0 1.9 copy-start.6
  56.0 2.2 copy-start.7
  232.1 1.2 copy-start.2
  233.4 1.2 copy-start.4
Sparse Core Ops, SparseCore 0:
  58.0 91.5 all-reduce.5

commit v2 on v1

--- a/solution.py
+++ b/solution.py
@@ -150,9 +150,9 @@
     edged = padded(turned, (("dop", 0),), 1)
     bin_count = edged.shape[0] - 2
     upper = upper_blocks(edged, training.astype(jnp.bfloat16))
-    my_upper = lax.psum_scatter(upper, "rng", scatter_dimension=0, tiled=True)
+    my_upper = sum_at_owner(upper, "rng", 0)
     my_unit = unit_vectors(full_from_upper(my_upper), steering(look_index))
-    unit = lax.all_gather(my_unit, "rng", axis=0, tiled=True)
+    unit = gather_directly(my_unit, "rng", 0)
     shaped = unit.reshape(bin_count, 3, 2, CH, LOOKS)
     rotated = jnp.stack([-shaped[:, :, 1], shaped[:, :, 0]], axis=2).reshape(bin_count, SNAP, LOOKS)
     weights = jnp.concatenate([unit, rotated], axis=2)

time: 245 us -> 151 us (0.62)
  waiting for transfers between devices: 107 us -> 29.4 us
  between operations: 15.8 us -> 2.4 us
  starting transfers between devices: 6.43 us -> 14.3 us
  blocking collectives: 23.3 us -> 16.8 us
  local copies, waits for them, and re-layouts: 22 us -> 19.3 us
    unnamed x2 -> x0, waiting for transfers between devices: 90.8 us -> none
    all_gather x1 -> x0, blocking collectives: 23.3 us -> none  [body(): unit = lax.all_gather(my_unit, 'rng', axis=0, tiled=True)]
    all_to_all x0 -> x1, blocking collectives: none -> 16.8 us  [copy_for_each(): lax.all_to_all(jnp.broadcast_to(array[None], (count, *array.shape)), axis...]
    all_to_all x0 -> x1, waiting for transfers between devices: none -> 13.5 us  [sum_at_owner(): lax.all_to_all(blocks, axis, split_axis=0, concat_axis=0, tiled=True)]
    all_to_all x0 -> x1, starting transfers between devices: none -> 7.88 us  [sum_at_owner(): lax.all_to_all(blocks, axis, split_axis=0, concat_axis=0, tiled=True)]
    unnamed x29 -> x17, local copies, waits for them, and re-layouts: 8.59 us -> 7.32 us
where the time goes in v2:
time: 151 us; the launch traced here: 150 us
  other arithmetic  56.6 us (37%)
  waiting for transfers between devices  29.4 us (19%)
  local copies, waits for them, and re-layouts  19.3 us (13%)
  blocking collectives  16.8 us (11%)
  starting transfers between devices  14.3 us (9%)
  matrix products  11.4 us (8%)
  between operations  2.4 us (2%)
    another operation x7, other arithmetic, unit_vectors(): factor = jnp.linalg.cholesky(regular)  28.8 us
    another operation x6, other arithmetic, unit_vectors(): lax.linalg.triangular_solve(factor, forward, left_side=True, lower=True,...  19.8 us
    all_to_all x1, blocking collectives, copy_for_each(): lax.all_to_all(jnp.broadcast_to(array[None], (count, *array.shape)), axis...  16.8 us
    all_to_all x1, waiting for transfers between devices, body(): lax.all_to_all(spectra, 'dop', split_axis=0, concat_axis=1, tiled=True)  13.9 us
    all_to_all x1, waiting for transfers between devices, sum_at_owner(): lax.all_to_all(blocks, axis, split_axis=0, concat_axis=0, tiled=True)  13.5 us
    all_to_all x1, starting transfers between devices, sum_at_owner(): lax.all_to_all(blocks, axis, split_axis=0, concat_axis=0, tiled=True)  7.88 us
    unnamed x17, local copies, waits for them, and re-layouts  7.32 us
    all_to_all x2, local copies, waits for them, and re-layouts, body(): lax.all_to_all(spectra, 'dop', split_axis=0, concat_axis=1, tiled=True)  6.02 us
  transfers between devices with their start and end apart: 4, of which 3 were waited for; matrix products, arithmetic and copies ran while one was open for 2% of the time, Pallas kernels for 0%

profile of v2, /device:TPU:24, one launch (start us, length us, event | category | flops | bytes accessed | tf_op | source)
XLA Modules:
  0.0 150.2 jit_solution(7828188025039128477)
XLA Ops:
  0.0 0.3 sine_convert_fusion
  0.3 0.9 copy-done
  1.2 0.9 fusion.17
  2.1 0.3 fusion.16
  2.4 1.1 pad_maximum_fusion.3
  3.5 4.7 %copy.44 = bf16[128,64,64]{2,1,0:T(8,128)(2,1)S(1)} copy(bf16[128,64,64]{0,1,2:T(8,128)(2,1)} %bitcast.112) | data formatting | bytes 2097152 | tf_op jit(solution)/shard_map/convert_element_type | solution.py:77
  8.2 2.7 %reshape.473 = bf16[8,2,32768]{2,1,0:T(2,128)(2,1)} reshape(bf16[128,64,64]{2,1,0:T(8,128)(2,1)S(1)} %copy.44) | data formatting | bytes 2097152
  10.9 4.7 %all-to-all-start = ((bf16[8,2,32768]{2,1,0:T(2,128)(2,1)}), bf16[8,2,32768]{2,1,0:T(2,128)(2,1)}, u32[]{:S(2)}, u32[]{:S(2)}) async-start(bf16[8,2,32768]{2,1,0:T(2,128)(2,1)} %reshape.473), calls=%async_computation | async-start | bytes 2097152 | tf_op jit(solution)/shard_map/all_to_all | solution.py:149
  15.6 13.9 %all-to-all-done = bf16[8,2,32768]{2,1,0:T(2,128)(2,1)} async-done(((bf16[8,2,32768]{2,1,0:T(2,128)(2,1)}), bf16[8,2,32768]{2,1,0:T(2,128)(2,1)}, u32[]{:S(2)}, u32[]{:S(2)}) %all-to-all-start) | async-done | bytes 1048608 | tf_op jit(solution)/shard_map/all_to_all | solution.py:149
  29.6 3.1 %reshape.474 = bf16[128,64,64]{2,1,0:T(8,128)(2,1)S(1)} reshape(bf16[8,2,32768]{2,1,0:T(2,128)(2,1)} %all-to-all-done) | data formatting | bytes 2097152
  32.8 2.8 %copy.46 = bf16[16,8,64,64]{2,1,3,0:T(8,128)(2,1)} copy(bf16[16,8,64,64]{3,2,0,1:T(8,128)(2,1)S(1)} %bitcast.111) | data formatting | bytes 2097152 | tf_op jit(solution)/shard_map/all_to_all | solution.py:149
  35.7 3.2 %all_to_all.22 = bf16[16,512,64]{1,2,0:T(8,128)(2,1)S(1)} reshape(bf16[16,8,64,64]{2,1,3,0:T(8,128)(2,1)} %copy.46) | data formatting | bytes 2097152 | tf_op jit(solution)/shard_map/all_to_all | solution.py:149
  39.0 1.7 %collective-permute-start.1 = (bf16[1,512,64]{1,2,0:T(8,128)(2,1)S(1)}, bf16[1,512,64]{1,2,0:T(8,128)(2,1)S(1)}, u32[]{:S(2)}, u32[]{:S(2)}) collective-permute-start(bf16[1,512,64]{1,2,0:T(8,128)(2,1)S(1)} %copy.61), channel_id=1, source_target_pairs={{16,0},{32,16},{48,32},{64,48},{80,64},{96,80},{112,96},{0,112},{1... | collective-permute-start | bytes 196616 | tf_op jit(solution)/shard_map/ppermute | solution.py:27
  40.7 1.9 %collective-permute-done.1 = bf16[1,512,64]{1,2,0:T(8,128)(2,1)S(1)} collective-permute-done((bf16[1,512,64]{1,2,0:T(8,128)(2,1)S(1)}, bf16[1,512,64]{1,2,0:T(8,128)(2,1)S(1)}, u32[]{:S(2)}, u32[]{:S(2)}) %collective-permute-start.1) | collective-permute-done | bytes 65568 | tf_op jit(solution)/shard_map/ppermute | solution.py:27
  42.6 0.3 pad_maximum_fusion.1
  43.0 0.3 fusion.10
  43.3 2.4 %broadcast_multiply_fusion = (bf16[16,1024,192]{1,2,0:T(8,128)(2,1)S(1)}, bf16[16,1024,192]{1,2,0:T(8,128)(2,1)S(1)}) fusion(bf16[16,1024]{1,0:T(8,128)(2,1)S(1)} %pad_maximum_fusion.11, bf16[18,512,32]{1,2,0:T(8,128)(2,1)S(1)} %get-tuple-element.34, bf16[18,512,32]{1,2,0:T(8,128)(2,1)S(1)} %get-tuple-element.33, ...), kind=kLoop, calls=%fused_computation.6 | loop fusion | flops 53477376 | bytes 19038208 | tf_op jit(solution)/shard_map/mul | solution.py:102
  45.8 2.0 %fusion.13 = f32[16,32,192]{2,1,0:T(8,128)S(1)} fusion(bf16[16,1024,192]{1,2,0:T(8,128)(2,1)S(1)} %get-tuple-element.26, bf16[16,1024,192]{1,2,0:T(8,128)(2,1)S(1)} %get-tuple-element.25), kind=kOutput, calls=%fused_computation.23 | convolution fusion | flops 201326592 | bytes 7733248 | tf_op jit(solution)/shard_map/krn,krm->knm/dot_general | solution.py:106
  47.8 1.5 %fusion.2 = f32[16,32,128]{2,1,0:T(8,128)S(1)} fusion(bf16[16,1024,192]{1,2,0:T(8,128)(2,1)S(1)} %get-tuple-element.26, bf16[16,1024,192]{1,2,0:T(8,128)(2,1)S(1)} %get-tuple-element.25), kind=kOutput, calls=%fused_computation.3 | convolution fusion | flops 134217728 | bytes 5505024 | tf_op jit(solution)/shard_map/krn,krm->knm/dot_general | solution.py:106
  49.3 0.7 fusion.4
  50.0 1.2 maximum_bitcast_fusion
  51.2 7.9 %all-to-all-start.1 = ((f32[16,1,32,384]{3,2,1,0:T(8,128)}), f32[16,1,32,384]{3,2,1,0:T(8,128)S(1)}, u32[]{:S(2)}, u32[]{:S(2)}) async-start(f32[16,1,32,384]{3,2,1,0:T(8,128)} %maximum_bitcast_fusion), calls=%async_computation.1 | async-start | bytes 1572864 | tf_op jit(solution)/shard_map/all_to_all | solution.py:40
  59.2 0.1 multiply_cosine_fusion
  59.3 13.5 %all-to-all-done.1 = f32[16,1,32,384]{3,2,1,0:T(8,128)S(1)} async-done(((f32[16,1,32,384]{3,2,1,0:T(8,128)}), f32[16,1,32,384]{3,2,1,0:T(8,128)S(1)}, u32[]{:S(2)}, u32[]{:S(2)}) %all-to-all-start.1) | async-done | bytes 786464 | tf_op jit(solution)/shard_map/all_to_all | solution.py:40
  73.9 0.6 fusion.28
  75.2 0.2 fusion.27
  75.5 11.7 %custom-call.18 = f32[1,128,128]{2,1,0:T(8,128)S(1)} custom-call(f32[1,128,128]{2,1,0:T(8,128)S(1)} %cholesky.120), custom_call_target="Cholesky" | custom-call | tf_op jit(solution)/shard_map/jit(cholesky)/cholesky | solution.py:137
  87.3 9.8 %custom-call.19 = f32[1,1,128,128]{2,3,1,0:T(8,128)S(1)} custom-call(f32[1,1,128,128]{3,2,1,0:T(8,128)S(1)} %get-tuple-element.41), custom_call_target="InvertDiagBlocksLowerTriangular" | custom-call | tf_op jit(solution)/shard_map/jit(cholesky)/cholesky | solution.py:137
  97.1 0.2 bitcast_dynamic-update-slice_fusion
  97.3 0.2 fusion.6
  97.5 5.8 %custom-call.20 = f32[1,64,64]{2,1,0:T(8,128)S(1)} custom-call(f32[1,64,64]{2,1,0:T(8,128)S(1)} %fusion.6), custom_call_target="Cholesky" | custom-call | tf_op jit(solution)/shard_map/jit(cholesky)/cholesky | solution.py:137
  103.4 0.7 compare_reduce_fusion
  104.1 0.7 compare_reduce_fusion.1
  106.2 19.7 %custom-call.21 = f32[1,2,128,128]{2,3,1,0:T(8,128)S(1)} custom-call(f32[1,2,128,128]{3,2,1,0:T(8,128)S(1)} %pad_maximum_fusion.9), custom_call_target="InvertDiagBlocksLowerTriangular" | custom-call | tf_op jit(solution)/shard_map/triangular_solve | solution.py:140
  125.8 0.3 fusion.34
  126.1 0.2 fusion.8
  126.3 0.2 fusion.46
  126.6 0.2 fusion.45
  126.8 0.2 convolution_subtract_fusion
  127.0 0.2 fusion.44
  127.6 16.8 %all_to_all.28 = bf16[16,1,192,64]{2,3,1,0:T(8,128)(2,1)S(1)} all-to-all(bf16[16,1,192,64]{2,3,1,0:T(8,128)(2,1)S(1)} %broadcast_in_dim.12), channel_id=1, replica_groups=mesh['dop'=8,'rng'=16] {'rng'}, dimensions={0} | all-to-all | bytes 786432 | tf_op jit(solution)/shard_map/all_to_all | solution.py:52
  144.4 0.4 copy.56
  144.9 0.2 pad_maximum_fusion.4
  145.1 0.8 fusion.20
  145.9 0.2 copy-done.2
  146.1 0.8 fusion.23
  147.0 0.4 copy-done.4
  147.4 2.9 %add_add_fusion = f32[16,128,512]{2,1,0:T(8,128)} fusion(f32[16,128,512]{2,1,0:T(8,128)S(1)} %fusion.23, f32[16,128,512]{2,1,0:T(8,128)S(1)} %fusion.20, bf16[16,512,64]{1,2,0:T(8,128)(2,1)S(1)} %copy-done.4, bf16[16,192,64]{2,1,0:T(8,128)(2,1)S(1)} %bitcast.109, bf16[16,192,64]{2,1,0:T(8,128)(2,1)S(1)} %bitcast.106), kind=kOutput, calls=%fused_computation.5 | convolution fusion | flops 136839168 | bytes 14417920 | tf_op jit(solution)/shard_map/knj,krn->kjr/dot_general | solution.py:161
  (57 shorter events, 2.2 us)
Async XLA Ops:
  0.0 1.2 copy-start
  3.5 12.1 %copy-start.5 = (s32[16,512]{1,0:T(8,128)S(1)}, s32[16,512]{1,0:T(8,128)}, u32[]{:S(2)}) copy-start(s32[16,512]{1,0:T(8,128)} %param.4) | copy-start | bytes 98308
  10.9 18.7 %all-to-all-start = ((bf16[8,2,32768]{2,1,0:T(2,128)(2,1)}), bf16[8,2,32768]{2,1,0:T(2,128)(2,1)}, u32[]{:S(2)}, u32[]{:S(2)}) async-start(bf16[8,2,32768]{2,1,0:T(2,128)(2,1)} %reshape.473), calls=%async_computation | async-start | bytes 2097152 | tf_op jit(solution)/shard_map/all_to_all | solution.py:149
  32.8 7.9 %collective-permute-start = (bf16[1,512,64]{1,2,0:T(8,128)(2,1)S(1)}, bf16[1,512,64]{1,2,0:T(8,128)(2,1)S(1)}, u32[]{:S(2)}, u32[]{:S(2)}) collective-permute-start(bf16[1,512,64]{1,2,0:T(8,128)(2,1)S(1)} %copy.60), channel_id=1, source_target_pairs={{0,16},{16,32},{32,48},{48,64},{64,80},{80,96},{96,112},{112,0},{1... | collective-permute-start | bytes 196616 | tf_op jit(solution)/shard_map/ppermute | solution.py:24
  39.0 3.6 %collective-permute-start.1 = (bf16[1,512,64]{1,2,0:T(8,128)(2,1)S(1)}, bf16[1,512,64]{1,2,0:T(8,128)(2,1)S(1)}, u32[]{:S(2)}, u32[]{:S(2)}) collective-permute-start(bf16[1,512,64]{1,2,0:T(8,128)(2,1)S(1)} %copy.61), channel_id=1, source_target_pairs={{16,0},{32,16},{48,32},{64,48},{80,64},{96,80},{112,96},{0,112},{1... | collective-permute-start | bytes 196616 | tf_op jit(solution)/shard_map/ppermute | solution.py:27
  42.9 2.9 %copy-start.1 = (bf16[16,512,64]{1,2,0:T(8,128)(2,1)}, bf16[16,512,64]{1,2,0:T(8,128)(2,1)S(1)}, u32[]{:S(2)}) copy-start(bf16[16,512,64]{1,2,0:T(8,128)(2,1)S(1)} %get-tuple-element.37) | copy-start | bytes 3145732
  42.9 2.9 %copy-start.3 = (bf16[16,512,64]{1,2,0:T(8,128)(2,1)}, bf16[16,512,64]{1,2,0:T(8,128)(2,1)S(1)}, u32[]{:S(2)}) copy-start(bf16[16,512,64]{1,2,0:T(8,128)(2,1)S(1)} %get-tuple-element.35) | copy-start | bytes 3145732
  49.3 9.8 %copy-start.6 = (s32[64]{0:T(128)S(1)}, s32[64]{0:T(128)}, u32[]{:S(2)}) copy-start(s32[64]{0:T(128)} %param.5) | copy-start | bytes 772
  51.2 21.6 %all-to-all-start.1 = ((f32[16,1,32,384]{3,2,1,0:T(8,128)}), f32[16,1,32,384]{3,2,1,0:T(8,128)S(1)}, u32[]{:S(2)}, u32[]{:S(2)}) async-start(f32[16,1,32,384]{3,2,1,0:T(8,128)} %maximum_bitcast_fusion), calls=%async_computation.1 | async-start | bytes 1572864 | tf_op jit(solution)/shard_map/all_to_all | solution.py:40
  144.9 1.2 copy-start.2
  146.1 1.2 copy-start.4

commit v3 on v2

--- a/solution.py
+++ b/solution.py
@@ -2,6 +2,8 @@
 import jax.numpy as jnp
 from jax import lax
 from jax.sharding import PartitionSpec as P
+from jax.experimental import pallas as pl
+from jax.experimental.pallas import tpu as pltpu
 
 CH = 32
 PULSES = 128
@@ -130,16 +132,47 @@
     return jnp.concatenate(rows, 1)
 
 
+def eliminate(aug_ref, out_ref, work_ref):
+    rows, cols = work_ref.shape
+    work_ref[...] = aug_ref[0]
+    lane_ids = lax.broadcasted_iota(jnp.int32, (1, cols), 1)
+    row_ids = lax.broadcasted_iota(jnp.int32, (rows, 1), 0)
+
+    def step(j, carry):
+        current = work_ref[...]
+        pivot_row = work_ref[pl.ds(j, 1), :]
+        lane_hit = lane_ids == j
+        column = jnp.sum(jnp.where(lane_hit, current, 0.0), axis=1, keepdims=True)
+        pivot = jnp.sum(jnp.where(lane_hit, pivot_row, 0.0), axis=1, keepdims=True)
+        scaled = pivot_row / pivot
+        work_ref[...] = jnp.where(row_ids == j, scaled, current - column * scaled)
+        return carry
+
+    lax.fori_loop(0, rows, step, 0)
+    out_ref[0] = work_ref[...]
+
+
+def solve_systems(matrix, targets):
+    count, size, _ = matrix.shape
+    aug = jnp.concatenate([matrix, targets], axis=2)
+    spec = pl.BlockSpec((1, size, aug.shape[2]), lambda i: (i, 0, 0))
+    out = pl.pallas_call(
+        eliminate,
+        grid=(count,),
+        in_specs=[spec],
+        out_specs=spec,
+        out_shape=jax.ShapeDtypeStruct(aug.shape, jnp.float32),
+        scratch_shapes=[pltpu.VMEM((size, aug.shape[2]), jnp.float32)],
+    )(aug)
+    return out[:, :, size:]
+
+
 def unit_vectors(matrix, steer):
     bin_count = matrix.shape[0]
     power = jnp.trace(matrix, axis1=1, axis2=2) / SNAP + epsilon
     regular = matrix / power[:, None, None] + loading * jnp.eye(SNAP, dtype=jnp.float32)
-    factor = jnp.linalg.cholesky(regular)
     targets = jnp.broadcast_to(steer, (bin_count, SNAP, LOOKS))
-    forward = lax.linalg.triangular_solve(factor, targets, left_side=True, lower=True)
-    solved = lax.linalg.triangular_solve(
-        factor, forward, left_side=True, lower=True, transpose_a=True
-    )
+    solved = solve_systems(regular, targets)
     gains = jnp.sum(targets * solved, axis=1)
     return (solved / jnp.sqrt(gains)[:, None, :]).astype(jnp.bfloat16)
 

time: 151 us -> 126 us (0.83)
  other arithmetic: 56.6 us -> 10.7 us
  Pallas kernels: 0 us -> 24.6 us
  matrix products: 11.4 us -> 9.67 us
    another operation x15 -> x2, other arithmetic: 49.2 us -> 0.58 us  [the longest x7 28.8 us: unit_vectors(): factor = jnp.linalg.cholesky(regular)]
    pallas_call x0 -> x1, Pallas kernels: none -> 24.6 us  [solve_systems(): pl.pallas_call(eliminate, grid=(count,), in_specs=[spec], out_specs=spec,...]
    another operation x8 -> x0, matrix products: 1.7 us -> none  [the longest x3 0.69 us: unit_vectors(): lax.linalg.triangular_solve(factor, targets, left_side=True, lower=True)]
where the time goes in v3:
time: 126 us; the launch traced here: 125 us
  waiting for transfers between devices  29.4 us (23%)
  Pallas kernels  24.6 us (20%)
  local copies, waits for them, and re-layouts  19.1 us (15%)
  blocking collectives  16.8 us (13%)
  starting transfers between devices  14.3 us (11%)
  other arithmetic  10.7 us (8%)
  matrix products  9.67 us (8%)
    pallas_call x1, Pallas kernels, solve_systems(): pl.pallas_call(eliminate, grid=(count,), in_specs=[spec], out_specs=spec,...  24.6 us
    all_to_all x1, blocking collectives, copy_for_each(): lax.all_to_all(jnp.broadcast_to(array[None], (count, *array.shape)), axis...  16.8 us
    all_to_all x1, waiting for transfers between devices, body(): lax.all_to_all(spectra, 'dop', split_axis=0, concat_axis=1, tiled=True)  14 us
    all_to_all x1, waiting for transfers between devices, sum_at_owner(): lax.all_to_all(blocks, axis, split_axis=0, concat_axis=0, tiled=True)  13.5 us
    all_to_all x1, starting transfers between devices, sum_at_owner(): lax.all_to_all(blocks, axis, split_axis=0, concat_axis=0, tiled=True)  7.87 us
    unnamed x17, local copies, waits for them, and re-layouts  7.32 us
    all_to_all x2, local copies, waits for them, and re-layouts, body(): lax.all_to_all(spectra, 'dop', split_axis=0, concat_axis=1, tiled=True)  6.02 us
    convert_element_type x1, local copies, waits for them, and re-layouts, doppler_spectra(): return jnp.stack([real_part, imag_part], axis=2).reshape(PULSES, echo_row...  4.72 us
  transfers between devices with their start and end apart: 4, of which 3 were waited for; matrix products, arithmetic and copies ran while one was open for 2% of the time, Pallas kernels for 0%

profile of v3, /device:TPU:24, one launch (start us, length us, event | category | flops | bytes accessed | tf_op | source)
XLA Modules:
  0.0 125.5 jit_solution(2962176492339904157)
XLA Ops:
  0.0 0.3 sine_convert_fusion
  0.3 0.9 copy-done
  1.2 0.9 fusion.14
  2.1 0.3 fusion.13
  2.4 1.1 pad_maximum_fusion.3
  3.5 4.7 %copy.34 = bf16[128,64,64]{2,1,0:T(8,128)(2,1)S(1)} copy(bf16[128,64,64]{0,1,2:T(8,128)(2,1)} %bitcast.54) | data formatting | bytes 2097152 | tf_op jit(solution)/shard_map/convert_element_type | solution.py:79
  8.2 2.7 %reshape.215 = bf16[8,2,32768]{2,1,0:T(2,128)(2,1)} reshape(bf16[128,64,64]{2,1,0:T(8,128)(2,1)S(1)} %copy.34) | data formatting | bytes 2097152
  10.9 4.7 %all-to-all-start = ((bf16[8,2,32768]{2,1,0:T(2,128)(2,1)}), bf16[8,2,32768]{2,1,0:T(2,128)(2,1)}, u32[]{:S(2)}, u32[]{:S(2)}) async-start(bf16[8,2,32768]{2,1,0:T(2,128)(2,1)} %reshape.215), calls=%async_computation | async-start | bytes 2097152 | tf_op jit(solution)/shard_map/all_to_all | solution.py:182
  15.6 14.0 %all-to-all-done = bf16[8,2,32768]{2,1,0:T(2,128)(2,1)} async-done(((bf16[8,2,32768]{2,1,0:T(2,128)(2,1)}), bf16[8,2,32768]{2,1,0:T(2,128)(2,1)}, u32[]{:S(2)}, u32[]{:S(2)}) %all-to-all-start) | async-done | bytes 1048608 | tf_op jit(solution)/shard_map/all_to_all | solution.py:182
  29.6 3.1 %reshape.216 = bf16[128,64,64]{2,1,0:T(8,128)(2,1)S(1)} reshape(bf16[8,2,32768]{2,1,0:T(2,128)(2,1)} %all-to-all-done) | data formatting | bytes 2097152
  32.7 0.1 copy.48
  32.8 2.8 %copy.36 = bf16[16,8,64,64]{2,1,3,0:T(8,128)(2,1)} copy(bf16[16,8,64,64]{3,2,0,1:T(8,128)(2,1)S(1)} %bitcast.53) | data formatting | bytes 2097152 | tf_op jit(solution)/shard_map/all_to_all | solution.py:182
  35.7 3.2 %all_to_all.22 = bf16[16,512,64]{1,2,0:T(8,128)(2,1)S(1)} reshape(bf16[16,8,64,64]{2,1,3,0:T(8,128)(2,1)} %copy.36) | data formatting | bytes 2097152 | tf_op jit(solution)/shard_map/all_to_all | solution.py:182
  38.9 0.1 copy.49
  39.0 1.7 %collective-permute-start.1 = (bf16[1,512,64]{1,2,0:T(8,128)(2,1)S(1)}, bf16[1,512,64]{1,2,0:T(8,128)(2,1)S(1)}, u32[]{:S(2)}, u32[]{:S(2)}) collective-permute-start(bf16[1,512,64]{1,2,0:T(8,128)(2,1)S(1)} %copy.49), channel_id=1, source_target_pairs={{16,0},{32,16},{48,32},{64,48},{80,64},{96,80},{112,96},{0,112},{1... | collective-permute-start | bytes 196616 | tf_op jit(solution)/shard_map/ppermute | solution.py:29
  40.7 1.9 %collective-permute-done.1 = bf16[1,512,64]{1,2,0:T(8,128)(2,1)S(1)} collective-permute-done((bf16[1,512,64]{1,2,0:T(8,128)(2,1)S(1)}, bf16[1,512,64]{1,2,0:T(8,128)(2,1)S(1)}, u32[]{:S(2)}, u32[]{:S(2)}) %collective-permute-start.1) | collective-permute-done | bytes 65568 | tf_op jit(solution)/shard_map/ppermute | solution.py:29
  42.6 0.3 pad_maximum_fusion.1
  43.0 0.3 fusion.7
  43.3 2.4 %broadcast_multiply_fusion = (bf16[16,1024,192]{1,2,0:T(8,128)(2,1)S(1)}, bf16[16,1024,192]{1,2,0:T(8,128)(2,1)S(1)}) fusion(bf16[16,1024]{1,0:T(8,128)(2,1)S(1)} %pad_maximum_fusion.11, bf16[18,512,32]{1,2,0:T(8,128)(2,1)S(1)} %get-tuple-element.14, bf16[18,512,32]{1,2,0:T(8,128)(2,1)S(1)} %get-tuple-element.13, ...), kind=kLoop, calls=%fused_computation.6 | loop fusion | flops 53477376 | bytes 19038208 | tf_op jit(solution)/shard_map/mul | solution.py:104
  45.8 2.0 %fusion.10 = f32[16,32,192]{2,1,0:T(8,128)S(1)} fusion(bf16[16,1024,192]{1,2,0:T(8,128)(2,1)S(1)} %get-tuple-element.6, bf16[16,1024,192]{1,2,0:T(8,128)(2,1)S(1)} %get-tuple-element.5), kind=kOutput, calls=%fused_computation.17 | convolution fusion | flops 201326592 | bytes 7733248 | tf_op jit(solution)/shard_map/krn,krm->knm/dot_general | solution.py:108
  47.8 1.5 %fusion.2 = f32[16,32,128]{2,1,0:T(8,128)S(1)} fusion(bf16[16,1024,192]{1,2,0:T(8,128)(2,1)S(1)} %get-tuple-element.6, bf16[16,1024,192]{1,2,0:T(8,128)(2,1)S(1)} %get-tuple-element.5), kind=kOutput, calls=%fused_computation.3 | convolution fusion | flops 134217728 | bytes 5505024 | tf_op jit(solution)/shard_map/krn,krm->knm/dot_general | solution.py:108
  49.3 0.7 fusion.4
  50.0 1.2 maximum_bitcast_fusion
  51.2 7.9 %all-to-all-start.1 = ((f32[16,1,32,384]{3,2,1,0:T(8,128)}), f32[16,1,32,384]{3,2,1,0:T(8,128)S(1)}, u32[]{:S(2)}, u32[]{:S(2)}) async-start(f32[16,1,32,384]{3,2,1,0:T(8,128)} %maximum_bitcast_fusion), calls=%async_computation.1 | async-start | bytes 1572864 | tf_op jit(solution)/shard_map/all_to_all | solution.py:42
  59.1 0.1 multiply_cosine_fusion
  59.3 13.5 %all-to-all-done.1 = f32[16,1,32,384]{3,2,1,0:T(8,128)S(1)} async-done(((f32[16,1,32,384]{3,2,1,0:T(8,128)}), f32[16,1,32,384]{3,2,1,0:T(8,128)S(1)}, u32[]{:S(2)}, u32[]{:S(2)}) %all-to-all-start.1) | async-done | bytes 786464 | tf_op jit(solution)/shard_map/all_to_all | solution.py:42
  72.9 0.1 slice_negate_fusion.7
  73.2 0.1 maximum_bitcast_fusion.7
  73.4 0.1 maximum_bitcast_fusion.8
  73.6 0.1 maximum_bitcast_fusion.3
  73.7 0.1 maximum_bitcast_fusion.4
  73.8 0.1 maximum_bitcast_fusion.5
  73.9 0.7 fusion.25
  75.2 0.2 fusion.24
  75.4 0.8 pad_maximum_fusion.9.aug_ref
  76.1 24.6 %shard_map.37 = f32[1,192,256]{2,1,0:T(8,128)} custom-call(f32[1,192,256]{2,1,0:T(8,128)} %pad_maximum_fusion.9.aug_ref), custom_call_target="tpu_custom_call" | custom-call | tf_op jit(solution)/shard_map/pallas_call | solution.py:159
  100.7 1.0 multiply_reduce_fusion
  101.7 1.0 fusion.34
  102.7 0.1 copy.43
  102.9 16.8 %all_to_all.28 = bf16[16,1,192,64]{2,3,1,0:T(8,128)(2,1)S(1)} all-to-all(bf16[16,1,192,64]{2,3,1,0:T(8,128)(2,1)S(1)} %broadcast_in_dim.13), channel_id=1, replica_groups=mesh['dop'=8,'rng'=16] {'rng'}, dimensions={0} | all-to-all | bytes 786432 | tf_op jit(solution)/shard_map/all_to_all | solution.py:54
  119.7 0.4 copy.44
  120.1 0.1 slice_negate_fusion.1
  120.2 0.2 pad_maximum_fusion.4
  120.4 0.8 fusion.17
  121.2 0.2 copy-done.2
  121.4 0.8 fusion.20
  122.2 0.4 copy-done.4
  122.6 2.9 %add_add_fusion = f32[16,128,512]{2,1,0:T(8,128)} fusion(f32[16,128,512]{2,1,0:T(8,128)S(1)} %fusion.20, f32[16,128,512]{2,1,0:T(8,128)S(1)} %fusion.17, bf16[16,512,64]{1,2,0:T(8,128)(2,1)S(1)} %copy-done.4, bf16[16,192,64]{2,1,0:T(8,128)(2,1)S(1)} %bitcast.51, bf16[16,192,64]{2,1,0:T(8,128)(2,1)S(1)} %bitcast.48), kind=kOutput, calls=%fused_computation.5 | convolution fusion | flops 136839168 | bytes 14417920 | tf_op jit(solution)/shard_map/knj,krn->kjr/dot_general | solution.py:194
  (31 shorter events, 0.7 us)
Async XLA Ops:
  0.0 1.2 copy-start
  3.5 12.1 %copy-start.5 = (s32[16,512]{1,0:T(8,128)S(1)}, s32[16,512]{1,0:T(8,128)}, u32[]{:S(2)}) copy-start(s32[16,512]{1,0:T(8,128)} %param.4) | copy-start | bytes 98308
  10.9 18.7 %all-to-all-start = ((bf16[8,2,32768]{2,1,0:T(2,128)(2,1)}), bf16[8,2,32768]{2,1,0:T(2,128)(2,1)}, u32[]{:S(2)}, u32[]{:S(2)}) async-start(bf16[8,2,32768]{2,1,0:T(2,128)(2,1)} %reshape.215), calls=%async_computation | async-start | bytes 2097152 | tf_op jit(solution)/shard_map/all_to_all | solution.py:182
  32.8 7.9 %collective-permute-start = (bf16[1,512,64]{1,2,0:T(8,128)(2,1)S(1)}, bf16[1,512,64]{1,2,0:T(8,128)(2,1)S(1)}, u32[]{:S(2)}, u32[]{:S(2)}) collective-permute-start(bf16[1,512,64]{1,2,0:T(8,128)(2,1)S(1)} %copy.48), channel_id=1, source_target_pairs={{0,16},{16,32},{32,48},{48,64},{64,80},{80,96},{96,112},{112,0},{1... | collective-permute-start | bytes 196616 | tf_op jit(solution)/shard_map/ppermute | solution.py:26
  39.0 3.6 %collective-permute-start.1 = (bf16[1,512,64]{1,2,0:T(8,128)(2,1)S(1)}, bf16[1,512,64]{1,2,0:T(8,128)(2,1)S(1)}, u32[]{:S(2)}, u32[]{:S(2)}) collective-permute-start(bf16[1,512,64]{1,2,0:T(8,128)(2,1)S(1)} %copy.49), channel_id=1, source_target_pairs={{16,0},{32,16},{48,32},{64,48},{80,64},{96,80},{112,96},{0,112},{1... | collective-permute-start | bytes 196616 | tf_op jit(solution)/shard_map/ppermute | solution.py:29
  42.9 2.9 %copy-start.1 = (bf16[16,512,64]{1,2,0:T(8,128)(2,1)}, bf16[16,512,64]{1,2,0:T(8,128)(2,1)S(1)}, u32[]{:S(2)}) copy-start(bf16[16,512,64]{1,2,0:T(8,128)(2,1)S(1)} %get-tuple-element.17) | copy-start | bytes 3145732
  42.9 2.9 %copy-start.3 = (bf16[16,512,64]{1,2,0:T(8,128)(2,1)}, bf16[16,512,64]{1,2,0:T(8,128)(2,1)S(1)}, u32[]{:S(2)}) copy-start(bf16[16,512,64]{1,2,0:T(8,128)(2,1)S(1)} %get-tuple-element.15) | copy-start | bytes 3145732
  49.3 9.8 %copy-start.6 = (s32[64]{0:T(128)S(1)}, s32[64]{0:T(128)}, u32[]{:S(2)}) copy-start(s32[64]{0:T(128)} %param.5) | copy-start | bytes 772
  51.2 21.6 %all-to-all-start.1 = ((f32[16,1,32,384]{3,2,1,0:T(8,128)}), f32[16,1,32,384]{3,2,1,0:T(8,128)S(1)}, u32[]{:S(2)}, u32[]{:S(2)}) async-start(f32[16,1,32,384]{3,2,1,0:T(8,128)} %maximum_bitcast_fusion), calls=%async_computation.1 | async-start | bytes 1572864 | tf_op jit(solution)/shard_map/all_to_all | solution.py:42
  120.2 1.2 copy-start.2
  121.4 1.2 copy-start.4

commit v4 on v3

--- a/solution.py
+++ b/solution.py
@@ -60,22 +60,23 @@
     return in_order(copy_for_each(array, axis), dim)
 
 
-def twiddles():
+def twiddles(bin_ids):
     pulse_ids = jnp.arange(PULSES, dtype=jnp.int32)
-    phase_ids = pulse_ids[:, None] * pulse_ids[None, :] % PULSES
+    phase_ids = bin_ids[:, None] * pulse_ids[None, :] % PULSES
     angles = phase_ids.astype(jnp.float32) * (2.0 * jnp.pi / PULSES)
     return jnp.concatenate([jnp.cos(angles), jnp.sin(angles)], axis=0).astype(jnp.bfloat16)
 
 
 def doppler_spectra(echo_rows, twiddle):
     product = jnp.einsum("kp,rqcp->krqc", twiddle, echo_rows, preferred_element_type=jnp.float32)
-    cosine = product[:PULSES]
-    sine = product[PULSES:]
+    half = twiddle.shape[0] // 2
+    cosine = product[:half]
+    sine = product[half:]
     real_part = cosine[:, :, 0] + sine[:, :, 1]
     imag_part = cosine[:, :, 1] - sine[:, :, 0]
     return (
         jnp.stack([real_part, imag_part], axis=2)
-        .reshape(PULSES, echo_rows.shape[0], 2 * CH)
+        .reshape(half, echo_rows.shape[0], 2 * CH)
         .astype(jnp.bfloat16)
     )
 
@@ -112,7 +113,7 @@
                 preferred_element_type=jnp.float32,
             )
         )
-    return jnp.concatenate(pieces, axis=-1)
+    return snap, jnp.concatenate(pieces, axis=-1)
 
 
 def full_from_upper(upper):
@@ -178,26 +179,22 @@
 
 
 def body(echoes, training, look_index):
-    spectra = doppler_spectra(echoes, twiddles())
-    turned = lax.all_to_all(spectra, "dop", split_axis=0, concat_axis=1, tiled=True)
-    edged = padded(turned, (("dop", 0),), 1)
-    bin_count = edged.shape[0] - 2
-    upper = upper_blocks(edged, training.astype(jnp.bfloat16))
+    groups = lax.axis_size("dop")
+    bins_here = PULSES // groups
+    wanted = (jnp.arange(groups)[:, None] * bins_here + jnp.arange(bins_here + 2)[None, :] - 1) % PULSES
+    spectra = doppler_spectra(echoes, twiddles(wanted.reshape(-1).astype(jnp.int32)))
+    sent = spectra.reshape(groups, bins_here + 2, echoes.shape[0], 2 * CH)
+    arrived = lax.all_to_all(sent, "dop", 0, 0)
+    edged = jnp.moveaxis(arrived, 0, 1).reshape(bins_here + 2, groups * echoes.shape[0], 2 * CH)
+    bin_count = bins_here
+    snap, upper = upper_blocks(edged, training.astype(jnp.bfloat16))
     my_upper = sum_at_owner(upper, "rng", 0)
     my_unit = unit_vectors(full_from_upper(my_upper), steering(look_index))
     unit = gather_directly(my_unit, "rng", 0)
     shaped = unit.reshape(bin_count, 3, 2, CH, LOOKS)
     rotated = jnp.stack([-shaped[:, :, 1], shaped[:, :, 0]], axis=2).reshape(bin_count, SNAP, LOOKS)
     weights = jnp.concatenate([unit, rotated], axis=2)
-    summed = None
-    for position in range(3):
-        term = jnp.einsum(
-            "knj,krn->kjr",
-            weights[:, position * 2 * CH : (position + 1) * 2 * CH],
-            edged[position : position + bin_count],
-            preferred_element_type=jnp.float32,
-        )
-        summed = term if summed is None else summed + term
+    summed = jnp.einsum("knj,krn->kjr", weights, snap, preferred_element_type=jnp.float32)
     return summed.reshape(bin_count, 2, LOOKS, edged.shape[1])
 
 

time: 126 us -> 157 us (1.25); the launches traced: 125 us -> 154 us
  local copies, waits for them, and re-layouts: 19.1 us -> 47.1 us
  other arithmetic: 10.7 us -> 16.1 us
  blocking collectives: 16.8 us -> 13.5 us
  starting transfers between devices: 14.3 us -> 12.6 us
    slice x3 -> x7, local copies, waits for them, and re-layouts: 0.21 us -> 26.1 us  [upper_blocks(): snap = jnp.concatenate([edged[b:b + bin_count] for b in range(3)], axis=-1)]
    all_to_all x2 -> x0, local copies, waits for them, and re-layouts: 6.02 us -> none  [body(): lax.all_to_all(spectra, 'dop', split_axis=0, concat_axis=1, tiled=True)]
    convert_element_type x1 -> x0, local copies, waits for them, and re-layouts: 4.72 us -> none  [doppler_spectra(): return jnp.stack([real_part, imag_part], axis=2).reshape(PULSES, echo_row...]
    another operation x1 -> x2, local copies, waits for them, and re-layouts: 0.01 us -> 3.8 us  [the longest x1 3.79 us: doppler_spectra(): jnp.stack([real_part, imag_part], axis=2)]
    unnamed x17 -> x16, local copies, waits for them, and re-layouts: 7.32 us -> 11.1 us
    all_to_all x1, blocking collectives: 16.8 us -> 13.5 us  [copy_for_each(): lax.all_to_all(jnp.broadcast_to(array[None], (count, *array.shape)), axis...]
    transpose x0 -> x2, local copies, waits for them, and re-layouts: none -> 2.86 us  [body(): jnp.moveaxis(arrived, 0, 1)]
    reshape x0 -> x1, local copies, waits for them, and re-layouts: none -> 2.4 us  [body(): jnp.moveaxis(arrived, 0, 1)]
  transfers between devices with their start and end apart: 4 -> 2, of which waited for: 3 -> 2; matrix products, arithmetic and copies ran while one was open for 2% -> 0% of each run, Pallas kernels for 0% -> 0%
where the time goes in v4:
time: 157 us; the launch traced here: 154 us
  local copies, waits for them, and re-layouts  47.1 us (30%)
  waiting for transfers between devices  29.1 us (19%)
  Pallas kernels  24.6 us (16%)
  other arithmetic  16.1 us (10%)
  blocking collectives  13.5 us (9%)
  starting transfers between devices  12.6 us (8%)
  matrix products  10.6 us (7%)
    slice x7, local copies, waits for them, and re-layouts, upper_blocks(): snap = jnp.concatenate([edged[b:b + bin_count] for b in range(3)], axis=-1)  26.1 us
    pallas_call x1, Pallas kernels, solve_systems(): pl.pallas_call(eliminate, grid=(count,), in_specs=[spec], out_specs=spec,...  24.6 us
    all_to_all x1, waiting for transfers between devices, body(): arrived = lax.all_to_all(sent, 'dop', 0, 0)  15.4 us
    all_to_all x1, waiting for transfers between devices, sum_at_owner(): lax.all_to_all(blocks, axis, split_axis=0, concat_axis=0, tiled=True)  13.8 us
    all_to_all x1, blocking collectives, copy_for_each(): lax.all_to_all(jnp.broadcast_to(array[None], (count, *array.shape)), axis...  13.5 us
    unnamed x16, local copies, waits for them, and re-layouts  11.1 us
    all_to_all x1, starting transfers between devices, sum_at_owner(): lax.all_to_all(blocks, axis, split_axis=0, concat_axis=0, tiled=True)  7.88 us
    dot_general x1, matrix products, body(): jnp.einsum('knj,krn->kjr', weights, snap, preferred_element_type=jnp.floa...  5.19 us
  transfers between devices with their start and end apart: 2, of which 2 were waited for; matrix products, arithmetic and copies ran while one was open for 0% of the time, Pallas kernels for 0%

profile of v4, /device:TPU:24, one launch (start us, length us, event | category | flops | bytes accessed | tf_op | source)
XLA Modules:
  0.0 154.5 jit_solution(12768317005486149588)
XLA Ops:
  0.2 0.4 cosine_convert_fusion
  0.6 0.7 copy-done
  1.2 1.1 fusion.14
  2.4 1.3 fusion.7
  3.6 1.8 %pad_maximum_fusion.1 = bf16[144,64,2,32]{0,1,3,2:T(8,128)(2,1)} fusion(bf16[144,64,1,32]{0,1,3,2:T(8,128)(2,1)S(1)} %get-tuple-element.8, bf16[144,64,1,32]{0,1,3,2:T(8,128)(2,1)S(1)} %get-tuple-element.7), kind=kLoop, calls=%fused_computation.12 | loop fusion | flops 589824 | bytes 2359296 | tf_op jit(solution)/shard_map/stack | solution.py:78
  5.4 3.8 %copy.39 = bf16[144,64,2,32]{1,3,2,0:T(8,128)(2,1)S(1)} copy(bf16[144,64,2,32]{0,1,3,2:T(8,128)(2,1)} %pad_maximum_fusion.1) | data formatting | bytes 2359296 | tf_op jit(solution)/shard_map/stack | solution.py:78
  9.2 2.8 %reshape.255 = bf16[8,2,36864]{2,1,0:T(2,128)(2,1)} reshape(bf16[8,18,64,64]{3,2,1,0:T(8,128)(2,1)S(1)} %bitcast.55) | data formatting | bytes 2359296
  12.0 4.7 %all-to-all-start = ((bf16[8,2,36864]{2,1,0:T(2,128)(2,1)}), bf16[8,2,36864]{2,1,0:T(2,128)(2,1)}, u32[]{:S(2)}, u32[]{:S(2)}) async-start(bf16[8,2,36864]{2,1,0:T(2,128)(2,1)} %reshape.255), calls=%async_computation | async-start | bytes 2359296 | tf_op jit(solution)/shard_map/all_to_all | solution.py:187
  16.7 15.4 %all-to-all-done = bf16[8,2,36864]{2,1,0:T(2,128)(2,1)} async-done(((bf16[8,2,36864]{2,1,0:T(2,128)(2,1)}), bf16[8,2,36864]{2,1,0:T(2,128)(2,1)}, u32[]{:S(2)}, u32[]{:S(2)}) %all-to-all-start) | async-done | bytes 1179680 | tf_op jit(solution)/shard_map/all_to_all | solution.py:187
  32.1 3.3 %reshape.256 = bf16[8,18,64,64]{3,2,1,0:T(8,128)(2,1)S(1)} reshape(bf16[8,2,36864]{2,1,0:T(2,128)(2,1)} %all-to-all-done) | data formatting | bytes 2359296
  35.3 0.8 bitcast_bitcast_fusion
  36.2 3.8 %fusion.35 = (bf16[16,8,64,64]{2,3,0,1:T(8,128)(2,1)}, bf16[16,8,64,64]{2,3,0,1:T(8,128)(2,1)}, bf16[16,8,64,64]{2,3,0,1:T(8,128)(2,1)S(1)}) fusion(bf16[18,8,64,64]{2,3,0,1:T(8,128)(2,1)S(1)} %bitcast_bitcast_fusion), kind=kLoop, calls=%fused_computation.86 | loop fusion | bytes 6291456 | tf_op jit(solution)/shard_map/slice | solution.py:101
  40.0 2.0 %copy.43 = bf16[18,8,64,64]{2,1,3,0:T(8,128)(2,1)S(1)} copy(bf16[18,8,64,64]{2,3,0,1:T(8,128)(2,1)S(1)} %bitcast_bitcast_fusion) | data formatting | bytes 2359296 | tf_op jit(solution)/shard_map/transpose | solution.py:188
  42.0 3.1 %copy.40 = bf16[16,8,64,64]{2,1,3,0:T(8,128)(2,1)} copy(bf16[16,8,64,64]{2,3,0,1:T(8,128)(2,1)S(1)} %get-tuple-element.11) | data formatting | bytes 2097152 | tf_op jit(solution)/shard_map/slice | solution.py:101
  45.2 3.2 %slice.149 = bf16[16,512,64]{1,2,0:T(8,128)(2,1)S(1)} reshape(bf16[16,8,64,64]{2,1,3,0:T(8,128)(2,1)} %copy.40) | data formatting | bytes 2097152 | tf_op jit(solution)/shard_map/slice | solution.py:101
  48.4 1.1 constant_dynamic-update-slice_fusion.2
  49.5 0.9 copy-done.2
  50.3 3.1 %copy.41 = bf16[16,8,64,64]{2,1,3,0:T(8,128)(2,1)} copy(bf16[16,8,64,64]{2,3,0,1:T(8,128)(2,1)S(1)} %copy-done.2) | data formatting | bytes 2097152 | tf_op jit(solution)/shard_map/slice | solution.py:101
  53.5 4.0 %slice.151 = bf16[16,512,64]{1,2,0:T(8,128)(2,1)} reshape(bf16[16,8,64,64]{2,1,3,0:T(8,128)(2,1)} %copy.41) | data formatting | bytes 2097152 | tf_op jit(solution)/shard_map/slice | solution.py:101
  57.5 4.7 %copy.42 = bf16[16,8,64,64]{2,1,3,0:T(8,128)(2,1)} copy(bf16[16,8,64,64]{2,3,0,1:T(8,128)(2,1)} %get-tuple-element.9) | data formatting | bytes 2097152 | tf_op jit(solution)/shard_map/slice | solution.py:101
  62.2 4.0 %slice.153 = bf16[16,512,64]{1,2,0:T(8,128)(2,1)} reshape(bf16[16,8,64,64]{2,1,3,0:T(8,128)(2,1)} %copy.42) | data formatting | bytes 2097152 | tf_op jit(solution)/shard_map/slice | solution.py:101
  66.3 2.4 %reshape.249 = bf16[18,512,64]{1,2,0:T(8,128)(2,1)} reshape(bf16[18,8,64,64]{2,1,3,0:T(8,128)(2,1)S(1)} %copy.43) | data formatting | bytes 2359296 | tf_op jit(solution)/shard_map/reshape | solution.py:188
  68.7 1.4 slice_negate_fusion
  70.1 2.4 %constant_dynamic-update-slice_fusion.1 = bf16[16,512,192]{1,2,0:T(8,128)(2,1)} fusion(bf16[16,512,192]{1,2,0:T(8,128)(2,1)} %constant_dynamic-update-slice_fusion.2, bf16[16,512,64]{1,2,0:T(8,128)(2,1)} %slice.151), kind=kLoop, calls=%fused_computation.74 | loop fusion | bytes 2097152
  72.5 1.3 fusion.9
  73.7 4.1 %broadcast_multiply_fusion = (bf16[16,1024,192]{1,2,0:T(8,128)(2,1)S(1)}, bf16[16,1024,192]{1,2,0:T(8,128)(2,1)S(1)}) fusion(bf16[16,1024]{1,0:T(8,128)(2,1)S(1)} %pad_maximum_fusion.5, bf16[18,512,32]{1,2,0:T(8,128)(2,1)S(1)} %get-tuple-element.15, bf16[18,512,32]{1,2,0:T(8,128)(2,1)S(1)} %get-tuple-element.14, ...), kind=kLoop, calls=%fused_computation.5 | loop fusion | flops 40894464 | bytes 19038208 | tf_op jit(solution)/shard_map/mul | solution.py:105
  77.8 2.0 %fusion.12 = f32[16,32,192]{2,1,0:T(8,128)S(1)} fusion(bf16[16,1024,192]{1,2,0:T(8,128)(2,1)S(1)} %get-tuple-element.6, bf16[16,1024,192]{1,2,0:T(8,128)(2,1)S(1)} %get-tuple-element.5), kind=kOutput, calls=%fused_computation.21 | convolution fusion | flops 201326592 | bytes 7733248 | tf_op jit(solution)/shard_map/krn,krm->knm/dot_general | solution.py:109
  79.9 1.5 fusion.2
  81.4 0.7 fusion.4
  82.1 1.2 maximum_bitcast_fusion
  83.2 7.9 %all-to-all-start.1 = ((f32[16,1,32,384]{3,2,1,0:T(8,128)}), f32[16,1,32,384]{3,2,1,0:T(8,128)S(1)}, u32[]{:S(2)}, u32[]{:S(2)}) async-start(f32[16,1,32,384]{3,2,1,0:T(8,128)} %maximum_bitcast_fusion), calls=%async_computation.1 | async-start | bytes 1572864 | tf_op jit(solution)/shard_map/all_to_all | solution.py:42
  91.2 0.1 multiply_cosine_fusion
  91.3 13.8 %all-to-all-done.1 = f32[16,1,32,384]{3,2,1,0:T(8,128)S(1)} async-done(((f32[16,1,32,384]{3,2,1,0:T(8,128)}), f32[16,1,32,384]{3,2,1,0:T(8,128)S(1)}, u32[]{:S(2)}, u32[]{:S(2)}) %all-to-all-start.1) | async-done | bytes 786464 | tf_op jit(solution)/shard_map/all_to_all | solution.py:42
  105.2 0.1 slice_negate_fusion.7
  105.5 0.1 maximum_bitcast_fusion.7
  105.8 0.1 maximum_bitcast_fusion.3
  106.0 0.1 maximum_bitcast_fusion.4
  106.2 0.6 fusion.21
  107.5 0.2 fusion.20
  107.6 0.8 pad_maximum_fusion.3.aug_ref
  108.4 24.6 %shard_map.37 = f32[1,192,256]{2,1,0:T(8,128)} custom-call(f32[1,192,256]{2,1,0:T(8,128)} %pad_maximum_fusion.3.aug_ref), custom_call_target="tpu_custom_call" | custom-call | tf_op jit(solution)/shard_map/pallas_call | solution.py:160
  133.0 1.0 multiply_reduce_fusion
  134.0 1.0 fusion.30
  135.0 0.1 copy.49
  135.1 13.5 %all_to_all.15 = bf16[16,1,192,64]{2,3,1,0:T(8,128)(2,1)S(1)} all-to-all(bf16[16,1,192,64]{2,3,1,0:T(8,128)(2,1)S(1)} %broadcast_in_dim.13), channel_id=1, replica_groups=mesh['dop'=8,'rng'=16] {'rng'}, dimensions={0} | all-to-all | bytes 786432 | tf_op jit(solution)/shard_map/all_to_all | solution.py:54
  148.6 0.4 copy.50
  149.1 0.2 pad_maximum_fusion.2
  149.3 5.2 %fusion.16 = f32[16,128,512]{2,1,0:T(8,128)} fusion(bf16[16,512,192]{1,2,0:T(8,128)(2,1)} %get-tuple-element.40, bf16[16,192,64]{2,1,0:T(8,128)(2,1)S(1)} %bitcast.58, bf16[16,192,64]{2,1,0:T(8,128)(2,1)S(1)} %bitcast.57), kind=kOutput, calls=%fused_computation.27 | convolution fusion | flops 404226048 | bytes 8126464 | tf_op jit(solution)/shard_map/knj,krn->kjr/dot_general | solution.py:197
  (31 shorter events, 1.0 us)
Async XLA Ops:
  0.0 1.2 copy-start
  9.2 7.5 %copy-start.4 = (s32[16,512]{1,0:T(8,128)S(1)}, s32[16,512]{1,0:T(8,128)}, u32[]{:S(2)}) copy-start(s32[16,512]{1,0:T(8,128)} %param.4) | copy-start | bytes 98308
  12.0 20.1 %all-to-all-start = ((bf16[8,2,36864]{2,1,0:T(2,128)(2,1)}), bf16[8,2,36864]{2,1,0:T(2,128)(2,1)}, u32[]{:S(2)}, u32[]{:S(2)}) async-start(bf16[8,2,36864]{2,1,0:T(2,128)(2,1)} %reshape.255), calls=%async_computation | async-start | bytes 2359296 | tf_op jit(solution)/shard_map/all_to_all | solution.py:187
  48.4 2.0 %copy-start.2 = (bf16[16,8,64,64]{2,3,0,1:T(8,128)(2,1)S(1)}, bf16[16,8,64,64]{2,3,0,1:T(8,128)(2,1)}, u32[]{:S(2)}) copy-start(bf16[16,8,64,64]{2,3,0,1:T(8,128)(2,1)} %get-tuple-element.10) | copy-start | bytes 3145732
  68.7 3.8 %copy-start.3 = (bf16[16,512,64]{1,2,0:T(8,128)(2,1)S(1)}, bf16[16,512,64]{1,2,0:T(8,128)(2,1)}, u32[]{:S(2)}) copy-start(bf16[16,512,64]{1,2,0:T(8,128)(2,1)} %slice.153) | copy-start | bytes 3145732
  81.4 9.8 %copy-start.5 = (s32[64]{0:T(128)S(1)}, s32[64]{0:T(128)}, u32[]{:S(2)}) copy-start(s32[64]{0:T(128)} %param.5) | copy-start | bytes 772
  83.2 21.9 %all-to-all-start.1 = ((f32[16,1,32,384]{3,2,1,0:T(8,128)}), f32[16,1,32,384]{3,2,1,0:T(8,128)S(1)}, u32[]{:S(2)}, u32[]{:S(2)}) async-start(f32[16,1,32,384]{3,2,1,0:T(8,128)} %maximum_bitcast_fusion), calls=%async_computation.1 | async-start | bytes 1572864 | tf_op jit(solution)/shard_map/all_to_all | solution.py:42
  149.3 5.2 %copy-start.1 = (bf16[64,2,32,128]{3,2,1,0:T(8,128)(2,1)S(1)}, bf16[64,2,32,128]{3,2,1,0:T(8,128)(2,1)}, u32[]{:S(2)}) copy-start(bf16[64,2,32,128]{3,2,1,0:T(8,128)(2,1)} %param.3) | copy-start | bytes 3145732

commit v5 on v3

--- a/solution.py
+++ b/solution.py
@@ -58,6 +58,38 @@
 
 def gather_directly(array, axis, dim):
     return in_order(copy_for_each(array, axis), dim)
+
+
+def ring_groups(count, inner):
+    outer = count // inner
+    along_inner = [[o * inner + i for i in range(inner)] for o in range(outer)]
+    along_outer = [[o * inner + i for o in range(outer)] for i in range(inner)]
+    return along_inner, along_outer
+
+
+def sum_in_stages(array, axis, inner):
+    count = lax.axis_size(axis)
+    outer = count // inner
+    along_inner, along_outer = ring_groups(count, inner)
+    blocks = array.reshape(outer, inner, array.shape[0] // count, *array.shape[1:])
+    first = lax.all_to_all(blocks, axis, 1, 1, axis_index_groups=along_inner).sum(axis=1)
+    second = lax.all_to_all(first, axis, 0, 0, axis_index_groups=along_outer).sum(axis=0)
+    return second
+
+
+def gather_in_stages(array, axis, inner):
+    count = lax.axis_size(axis)
+    outer = count // inner
+    along_inner, along_outer = ring_groups(count, inner)
+    first = lax.all_to_all(
+        jnp.broadcast_to(array[None], (outer, *array.shape)), axis, 0, 0,
+        axis_index_groups=along_outer,
+    )
+    second = lax.all_to_all(
+        jnp.broadcast_to(first[None], (inner, *first.shape)), axis, 0, 0,
+        axis_index_groups=along_inner,
+    )
+    return jnp.swapaxes(second, 0, 1).reshape(count * array.shape[0], *array.shape[1:])
 
 
 def twiddles():
@@ -183,9 +215,9 @@
     edged = padded(turned, (("dop", 0),), 1)
     bin_count = edged.shape[0] - 2
     upper = upper_blocks(edged, training.astype(jnp.bfloat16))
-    my_upper = sum_at_owner(upper, "rng", 0)
+    my_upper = sum_in_stages(upper, "rng", 4)
     my_unit = unit_vectors(full_from_upper(my_upper), steering(look_index))
-    unit = gather_directly(my_unit, "rng", 0)
+    unit = gather_in_stages(my_unit, "rng", 4)
     shaped = unit.reshape(bin_count, 3, 2, CH, LOOKS)
     rotated = jnp.stack([-shaped[:, :, 1], shaped[:, :, 0]], axis=2).reshape(bin_count, SNAP, LOOKS)
     weights = jnp.concatenate([unit, rotated], axis=2)

time: 126 us -> 139 us (1.10); the launches traced: 125 us -> 136 us
  waiting for transfers between devices: 29.4 us -> 33.8 us
  blocking collectives: 16.8 us -> 20.4 us
  starting transfers between devices: 14.3 us -> 16 us
    all_to_all x1 -> x2, waiting for transfers between devices: 13.5 us -> 17.9 us  [the longest x1 11.5 us: sum_in_stages(): lax.all_to_all(blocks, axis, 1, 1, axis_index_groups=along_inner)]
    all_to_all x1 -> x2, blocking collectives: 16.8 us -> 20.4 us  [the longest x1 11.7 us: gather_in_stages(): lax.all_to_all(jnp.broadcast_to(first[None], (inner, *first.shape)), axis...]
    all_to_all x1 -> x2, starting transfers between devices: 7.87 us -> 9.6 us  [the longest x1 5.3 us: sum_in_stages(): lax.all_to_all(blocks, axis, 1, 1, axis_index_groups=along_inner)]
  transfers between devices with their start and end apart: 4 -> 5, of which waited for: 3 -> 4; matrix products, arithmetic and copies ran while one was open for 2% -> 2% of each run, Pallas kernels for 0% -> 0%
where the time goes in v5:
time: 139 us; the launch traced here: 136 us
  waiting for transfers between devices  33.8 us (24%)
  Pallas kernels  24.6 us (18%)
  blocking collectives  20.4 us (15%)
  local copies, waits for them, and re-layouts  20.1 us (14%)
  starting transfers between devices  16 us (12%)
  other arithmetic  10.5 us (8%)
  matrix products  9.66 us (7%)
    pallas_call x1, Pallas kernels, solve_systems(): pl.pallas_call(eliminate, grid=(count,), in_specs=[spec], out_specs=spec,...  24.6 us
    all_to_all x1, waiting for transfers between devices, body(): lax.all_to_all(spectra, 'dop', split_axis=0, concat_axis=1, tiled=True)  14 us
    all_to_all x1, blocking collectives, gather_in_stages(): lax.all_to_all(jnp.broadcast_to(first[None], (inner, *first.shape)), axis...  11.7 us
    all_to_all x1, waiting for transfers between devices, sum_in_stages(): lax.all_to_all(blocks, axis, 1, 1, axis_index_groups=along_inner)  11.5 us
    all_to_all x1, blocking collectives, gather_in_stages(): lax.all_to_all(jnp.broadcast_to(array[None], (outer, *array.shape)), axis...  8.67 us
    unnamed x17, local copies, waits for them, and re-layouts  7.32 us
    all_to_all x1, waiting for transfers between devices, sum_in_stages(): lax.all_to_all(first, axis, 0, 0, axis_index_groups=along_outer).sum(axis=0)  6.45 us
    all_to_all x2, local copies, waits for them, and re-layouts, body(): lax.all_to_all(spectra, 'dop', split_axis=0, concat_axis=1, tiled=True)  6.02 us
  transfers between devices with their start and end apart: 5, of which 4 were waited for; matrix products, arithmetic and copies ran while one was open for 2% of the time, Pallas kernels for 0%

profile of v5, /device:TPU:24, one launch (start us, length us, event | category | flops | bytes accessed | tf_op | source)
XLA Modules:
  0.0 136.1 jit_solution(7261243414662854178)
XLA Ops:
  0.0 0.3 sine_convert_fusion
  0.3 0.9 copy-done
  1.2 0.9 fusion.14
  2.1 0.3 fusion.13
  2.4 1.1 pad_maximum_fusion.3
  3.5 4.7 %copy.32 = bf16[128,64,64]{2,1,0:T(8,128)(2,1)S(1)} copy(bf16[128,64,64]{0,1,2:T(8,128)(2,1)} %bitcast.56) | data formatting | bytes 2097152 | tf_op jit(solution)/shard_map/convert_element_type | solution.py:111
  8.2 2.7 %reshape.219 = bf16[8,2,32768]{2,1,0:T(2,128)(2,1)} reshape(bf16[128,64,64]{2,1,0:T(8,128)(2,1)S(1)} %copy.32) | data formatting | bytes 2097152
  10.9 4.7 %all-to-all-start = ((bf16[8,2,32768]{2,1,0:T(2,128)(2,1)}), bf16[8,2,32768]{2,1,0:T(2,128)(2,1)}, u32[]{:S(2)}, u32[]{:S(2)}) async-start(bf16[8,2,32768]{2,1,0:T(2,128)(2,1)} %reshape.219), calls=%async_computation | async-start | bytes 2097152 | tf_op jit(solution)/shard_map/all_to_all | solution.py:214
  15.6 14.0 %all-to-all-done = bf16[8,2,32768]{2,1,0:T(2,128)(2,1)} async-done(((bf16[8,2,32768]{2,1,0:T(2,128)(2,1)}), bf16[8,2,32768]{2,1,0:T(2,128)(2,1)}, u32[]{:S(2)}, u32[]{:S(2)}) %all-to-all-start) | async-done | bytes 1048608 | tf_op jit(solution)/shard_map/all_to_all | solution.py:214
  29.6 3.1 %reshape.220 = bf16[128,64,64]{2,1,0:T(8,128)(2,1)S(1)} reshape(bf16[8,2,32768]{2,1,0:T(2,128)(2,1)} %all-to-all-done) | data formatting | bytes 2097152
  32.7 0.1 copy.45
  32.8 2.8 %copy.34 = bf16[16,8,64,64]{2,1,3,0:T(8,128)(2,1)} copy(bf16[16,8,64,64]{3,2,0,1:T(8,128)(2,1)S(1)} %bitcast.55) | data formatting | bytes 2097152 | tf_op jit(solution)/shard_map/all_to_all | solution.py:214
  35.7 3.2 %all_to_all.28 = bf16[16,512,64]{1,2,0:T(8,128)(2,1)S(1)} reshape(bf16[16,8,64,64]{2,1,3,0:T(8,128)(2,1)} %copy.34) | data formatting | bytes 2097152 | tf_op jit(solution)/shard_map/all_to_all | solution.py:214
  38.9 0.1 copy.46
  39.0 1.7 %collective-permute-start.1 = (bf16[1,512,64]{1,2,0:T(8,128)(2,1)S(1)}, bf16[1,512,64]{1,2,0:T(8,128)(2,1)S(1)}, u32[]{:S(2)}, u32[]{:S(2)}) collective-permute-start(bf16[1,512,64]{1,2,0:T(8,128)(2,1)S(1)} %copy.46), channel_id=1, source_target_pairs={{16,0},{32,16},{48,32},{64,48},{80,64},{96,80},{112,96},{0,112},{1... | collective-permute-start | bytes 196616 | tf_op jit(solution)/shard_map/ppermute | solution.py:29
  40.7 1.9 %collective-permute-done.1 = bf16[1,512,64]{1,2,0:T(8,128)(2,1)S(1)} collective-permute-done((bf16[1,512,64]{1,2,0:T(8,128)(2,1)S(1)}, bf16[1,512,64]{1,2,0:T(8,128)(2,1)S(1)}, u32[]{:S(2)}, u32[]{:S(2)}) %collective-permute-start.1) | collective-permute-done | bytes 65568 | tf_op jit(solution)/shard_map/ppermute | solution.py:29
  42.6 0.3 pad_maximum_fusion.1
  43.0 0.3 fusion.7
  43.3 2.4 %broadcast_multiply_fusion = (bf16[16,1024,192]{1,2,0:T(8,128)(2,1)S(1)}, bf16[16,1024,192]{1,2,0:T(8,128)(2,1)S(1)}) fusion(bf16[16,1024]{1,0:T(8,128)(2,1)S(1)} %pad_maximum_fusion.12, bf16[18,512,32]{1,2,0:T(8,128)(2,1)S(1)} %get-tuple-element.14, bf16[18,512,32]{1,2,0:T(8,128)(2,1)S(1)} %get-tuple-element.13, ...), kind=kLoop, calls=%fused_computation.6 | loop fusion | flops 53477376 | bytes 19038208 | tf_op jit(solution)/shard_map/mul | solution.py:136
  45.8 2.0 %fusion.10 = f32[16,32,192]{2,1,0:T(8,128)S(1)} fusion(bf16[16,1024,192]{1,2,0:T(8,128)(2,1)S(1)} %get-tuple-element.6, bf16[16,1024,192]{1,2,0:T(8,128)(2,1)S(1)} %get-tuple-element.5), kind=kOutput, calls=%fused_computation.17 | convolution fusion | flops 201326592 | bytes 7733248 | tf_op jit(solution)/shard_map/krn,krm->knm/dot_general | solution.py:140
  47.8 1.5 %fusion.2 = f32[16,32,128]{2,1,0:T(8,128)S(1)} fusion(bf16[16,1024,192]{1,2,0:T(8,128)(2,1)S(1)} %get-tuple-element.6, bf16[16,1024,192]{1,2,0:T(8,128)(2,1)S(1)} %get-tuple-element.5), kind=kOutput, calls=%fused_computation.3 | convolution fusion | flops 134217728 | bytes 5505024 | tf_op jit(solution)/shard_map/krn,krm->knm/dot_general | solution.py:140
  49.3 0.7 fusion.4
  50.0 0.3 pad_maximum_fusion.4
  50.3 1.0 copy.37
  51.3 5.3 %all-to-all-start.1 = ((f32[4,4,1,32,384]{4,3,0,2,1:T(8,128)}), f32[4,4,1,32,384]{4,3,0,2,1:T(8,128)S(1)}, u32[]{:S(2)}, u32[]{:S(2)}) async-start(f32[4,4,1,32,384]{4,3,0,2,1:T(8,128)} %copy.37), calls=%async_computation.1 | async-start | bytes 1572864 | tf_op jit(solution)/shard_map/all_to_all | solution.py:75
  56.6 11.5 %all-to-all-done.1 = f32[4,4,1,32,384]{4,3,0,2,1:T(8,128)S(1)} async-done(((f32[4,4,1,32,384]{4,3,0,2,1:T(8,128)}), f32[4,4,1,32,384]{4,3,0,2,1:T(8,128)S(1)}, u32[]{:S(2)}, u32[]{:S(2)}) %all-to-all-start.1) | async-done | bytes 786464 | tf_op jit(solution)/shard_map/all_to_all | solution.py:75
  68.1 0.7 reduce_sum.41
  68.8 4.3 %all-to-all-start.2 = ((f32[4,1,32,384]{3,2,1,0:T(8,128)}), f32[4,1,32,384]{3,2,1,0:T(8,128)S(1)}, u32[]{:S(2)}, u32[]{:S(2)}) async-start(f32[4,1,32,384]{3,2,1,0:T(8,128)} %bitcast.9), calls=%async_computation.2 | async-start | bytes 393216 | tf_op jit(solution)/shard_map/all_to_all | solution.py:76
  73.1 0.1 multiply_cosine_fusion
  73.3 6.5 %all-to-all-done.2 = f32[4,1,32,384]{3,2,1,0:T(8,128)S(1)} async-done(((f32[4,1,32,384]{3,2,1,0:T(8,128)}), f32[4,1,32,384]{3,2,1,0:T(8,128)S(1)}, u32[]{:S(2)}, u32[]{:S(2)}) %all-to-all-start.2) | async-done | bytes 196640 | tf_op jit(solution)/shard_map/all_to_all | solution.py:76
  79.8 0.1 slice_negate_fusion.7
  80.5 0.1 maximum_bitcast_fusion.2
  80.6 0.1 maximum_bitcast_fusion.3
  80.8 0.7 fusion.25
  82.2 0.2 fusion.24
  82.4 0.8 pad_maximum_fusion.10.aug_ref
  83.1 24.6 %shard_map.37 = f32[1,192,256]{2,1,0:T(8,128)} custom-call(f32[1,192,256]{2,1,0:T(8,128)} %pad_maximum_fusion.10.aug_ref), custom_call_target="tpu_custom_call" | custom-call | tf_op jit(solution)/shard_map/pallas_call | solution.py:191
  107.7 1.0 multiply_reduce_fusion
  108.7 1.0 fusion.34
  109.8 8.7 %all_to_all.38 = bf16[4,1,192,64]{2,3,1,0:T(8,128)(2,1)S(1)} all-to-all(bf16[4,1,192,64]{2,3,1,0:T(8,128)(2,1)S(1)} %broadcast_in_dim.17), channel_id=1, replica_groups={{0,4,8,12},{1,5,9,13},{2,6,10,14},{3,7,11,15},{16,20,24,28},{17,21,25,2..., dimensions={0} | all-to-all | bytes 196608 | tf_op jit(solution)/shard_map/all_to_all | solution.py:84
  118.6 11.7 %all_to_all.39 = bf16[4,4,1,192,64]{3,4,2,1,0:T(8,128)(2,1)S(1)} all-to-all(bf16[4,4,1,192,64]{3,4,2,1,0:T(8,128)(2,1)S(1)} %broadcast_in_dim.19), channel_id=1, replica_groups={{0,1,2,3},{4,5,6,7},{8,9,10,11},{12,13,14,15},{16,17,18,19},{20,21,22,2..., dimensions={0} | all-to-all | bytes 786432 | tf_op jit(solution)/shard_map/all_to_all | solution.py:88
  130.3 0.4 copy.42
  130.8 0.2 pad_maximum_fusion.5
  131.0 0.8 fusion.17
  131.8 0.2 copy-done.2
  132.0 0.8 fusion.20
  132.8 0.4 copy-done.4
  133.2 2.9 %add_add_fusion = f32[16,128,512]{2,1,0:T(8,128)} fusion(f32[16,128,512]{2,1,0:T(8,128)S(1)} %fusion.20, f32[16,128,512]{2,1,0:T(8,128)S(1)} %fusion.17, bf16[16,512,64]{1,2,0:T(8,128)(2,1)S(1)} %copy-done.4, bf16[16,192,64]{2,1,0:T(8,128)(2,1)S(1)} %bitcast.53, bf16[16,192,64]{2,1,0:T(8,128)(2,1)S(1)} %bitcast.50), kind=kOutput, calls=%fused_computation.5 | convolution fusion | flops 136839168 | bytes 14417920 | tf_op jit(solution)/shard_map/knj,krn->kjr/dot_general | solution.py:226
  (37 shorter events, 1.1 us)
Async XLA Ops:
  0.0 1.2 copy-start
  3.5 12.1 %copy-start.5 = (s32[16,512]{1,0:T(8,128)S(1)}, s32[16,512]{1,0:T(8,128)}, u32[]{:S(2)}) copy-start(s32[16,512]{1,0:T(8,128)} %param.4) | copy-start | bytes 98308
  10.9 18.7 %all-to-all-start = ((bf16[8,2,32768]{2,1,0:T(2,128)(2,1)}), bf16[8,2,32768]{2,1,0:T(2,128)(2,1)}, u32[]{:S(2)}, u32[]{:S(2)}) async-start(bf16[8,2,32768]{2,1,0:T(2,128)(2,1)} %reshape.219), calls=%async_computation | async-start | bytes 2097152 | tf_op jit(solution)/shard_map/all_to_all | solution.py:214
  32.8 7.9 %collective-permute-start = (bf16[1,512,64]{1,2,0:T(8,128)(2,1)S(1)}, bf16[1,512,64]{1,2,0:T(8,128)(2,1)S(1)}, u32[]{:S(2)}, u32[]{:S(2)}) collective-permute-start(bf16[1,512,64]{1,2,0:T(8,128)(2,1)S(1)} %copy.45), channel_id=1, source_target_pairs={{0,16},{16,32},{32,48},{48,64},{64,80},{80,96},{96,112},{112,0},{1... | collective-permute-start | bytes 196616 | tf_op jit(solution)/shard_map/ppermute | solution.py:26
  39.0 3.6 %collective-permute-start.1 = (bf16[1,512,64]{1,2,0:T(8,128)(2,1)S(1)}, bf16[1,512,64]{1,2,0:T(8,128)(2,1)S(1)}, u32[]{:S(2)}, u32[]{:S(2)}) collective-permute-start(bf16[1,512,64]{1,2,0:T(8,128)(2,1)S(1)} %copy.46), channel_id=1, source_target_pairs={{16,0},{32,16},{48,32},{64,48},{80,64},{96,80},{112,96},{0,112},{1... | collective-permute-start | bytes 196616 | tf_op jit(solution)/shard_map/ppermute | solution.py:29
  42.9 2.9 %copy-start.1 = (bf16[16,512,64]{1,2,0:T(8,128)(2,1)}, bf16[16,512,64]{1,2,0:T(8,128)(2,1)S(1)}, u32[]{:S(2)}) copy-start(bf16[16,512,64]{1,2,0:T(8,128)(2,1)S(1)} %get-tuple-element.17) | copy-start | bytes 3145732
  42.9 2.9 %copy-start.3 = (bf16[16,512,64]{1,2,0:T(8,128)(2,1)}, bf16[16,512,64]{1,2,0:T(8,128)(2,1)S(1)}, u32[]{:S(2)}) copy-start(bf16[16,512,64]{1,2,0:T(8,128)(2,1)S(1)} %get-tuple-element.15) | copy-start | bytes 3145732
  49.3 7.3 %copy-start.6 = (s32[64]{0:T(128)S(1)}, s32[64]{0:T(128)}, u32[]{:S(2)}) copy-start(s32[64]{0:T(128)} %param.5) | copy-start | bytes 772
  51.3 16.8 %all-to-all-start.1 = ((f32[4,4,1,32,384]{4,3,0,2,1:T(8,128)}), f32[4,4,1,32,384]{4,3,0,2,1:T(8,128)S(1)}, u32[]{:S(2)}, u32[]{:S(2)}) async-start(f32[4,4,1,32,384]{4,3,0,2,1:T(8,128)} %copy.37), calls=%async_computation.1 | async-start | bytes 1572864 | tf_op jit(solution)/shard_map/all_to_all | solution.py:75
  68.8 10.9 %all-to-all-start.2 = ((f32[4,1,32,384]{3,2,1,0:T(8,128)}), f32[4,1,32,384]{3,2,1,0:T(8,128)S(1)}, u32[]{:S(2)}, u32[]{:S(2)}) async-start(f32[4,1,32,384]{3,2,1,0:T(8,128)} %bitcast.9), calls=%async_computation.2 | async-start | bytes 393216 | tf_op jit(solution)/shard_map/all_to_all | solution.py:76
  130.8 1.2 copy-start.2
  132.0 1.2 copy-start.4

commit v6 on v4

--- a/solution.py
+++ b/solution.py
@@ -113,7 +113,7 @@
                 preferred_element_type=jnp.float32,
             )
         )
-    return snap, jnp.concatenate(pieces, axis=-1)
+    return jnp.concatenate(pieces, axis=-1)
 
 
 def full_from_upper(upper):
@@ -133,11 +133,16 @@
     return jnp.concatenate(rows, 1)
 
 
-def eliminate(aug_ref, out_ref, work_ref):
+def eliminate(matrix_ref, steer_ref, unit_ref, work_ref):
     rows, cols = work_ref.shape
-    work_ref[...] = aug_ref[0]
+    matrix = matrix_ref[0]
+    steer = steer_ref[...]
     lane_ids = lax.broadcasted_iota(jnp.int32, (1, cols), 1)
     row_ids = lax.broadcasted_iota(jnp.int32, (rows, 1), 0)
+    diagonal = row_ids == lane_ids[:, :rows]
+    power = jnp.sum(jnp.where(diagonal, matrix, 0.0)) / SNAP + epsilon
+    work_ref[:, :rows] = matrix / power + jnp.where(diagonal, loading, 0.0)
+    work_ref[:, rows:] = steer
 
     def step(j, carry):
         current = work_ref[...]
@@ -150,32 +155,24 @@
         return carry
 
     lax.fori_loop(0, rows, step, 0)
-    out_ref[0] = work_ref[...]
-
-
-def solve_systems(matrix, targets):
+    solved = work_ref[:, rows:]
+    gains = jnp.sum(steer * solved, axis=0, keepdims=True)
+    unit_ref[0] = (solved / jnp.sqrt(gains)).astype(unit_ref.dtype)
+
+
+def unit_vectors(matrix, steer):
     count, size, _ = matrix.shape
-    aug = jnp.concatenate([matrix, targets], axis=2)
-    spec = pl.BlockSpec((1, size, aug.shape[2]), lambda i: (i, 0, 0))
-    out = pl.pallas_call(
+    return pl.pallas_call(
         eliminate,
         grid=(count,),
-        in_specs=[spec],
-        out_specs=spec,
-        out_shape=jax.ShapeDtypeStruct(aug.shape, jnp.float32),
-        scratch_shapes=[pltpu.VMEM((size, aug.shape[2]), jnp.float32)],
-    )(aug)
-    return out[:, :, size:]
-
-
-def unit_vectors(matrix, steer):
-    bin_count = matrix.shape[0]
-    power = jnp.trace(matrix, axis1=1, axis2=2) / SNAP + epsilon
-    regular = matrix / power[:, None, None] + loading * jnp.eye(SNAP, dtype=jnp.float32)
-    targets = jnp.broadcast_to(steer, (bin_count, SNAP, LOOKS))
-    solved = solve_systems(regular, targets)
-    gains = jnp.sum(targets * solved, axis=1)
-    return (solved / jnp.sqrt(gains)[:, None, :]).astype(jnp.bfloat16)
+        in_specs=[
+            pl.BlockSpec((1, size, size), lambda i: (i, 0, 0)),
+            pl.BlockSpec((size, LOOKS), lambda i: (0, 0)),
+        ],
+        out_specs=pl.BlockSpec((1, size, LOOKS), lambda i: (i, 0, 0)),
+        out_shape=jax.ShapeDtypeStruct((count, size, LOOKS), jnp.bfloat16),
+        scratch_shapes=[pltpu.VMEM((size, size + LOOKS), jnp.float32)],
+    )(matrix, steer)
 
 
 def body(echoes, training, look_index):
@@ -183,18 +180,24 @@
     bins_here = PULSES // groups
     wanted = (jnp.arange(groups)[:, None] * bins_here + jnp.arange(bins_here + 2)[None, :] - 1) % PULSES
     spectra = doppler_spectra(echoes, twiddles(wanted.reshape(-1).astype(jnp.int32)))
-    sent = spectra.reshape(groups, bins_here + 2, echoes.shape[0], 2 * CH)
-    arrived = lax.all_to_all(sent, "dop", 0, 0)
-    edged = jnp.moveaxis(arrived, 0, 1).reshape(bins_here + 2, groups * echoes.shape[0], 2 * CH)
+    edged = lax.all_to_all(spectra, "dop", split_axis=0, concat_axis=1, tiled=True)
     bin_count = bins_here
-    snap, upper = upper_blocks(edged, training.astype(jnp.bfloat16))
+    upper = upper_blocks(edged, training.astype(jnp.bfloat16))
     my_upper = sum_at_owner(upper, "rng", 0)
     my_unit = unit_vectors(full_from_upper(my_upper), steering(look_index))
     unit = gather_directly(my_unit, "rng", 0)
     shaped = unit.reshape(bin_count, 3, 2, CH, LOOKS)
     rotated = jnp.stack([-shaped[:, :, 1], shaped[:, :, 0]], axis=2).reshape(bin_count, SNAP, LOOKS)
     weights = jnp.concatenate([unit, rotated], axis=2)
-    summed = jnp.einsum("knj,krn->kjr", weights, snap, preferred_element_type=jnp.float32)
+    summed = None
+    for position in range(3):
+        term = jnp.einsum(
+            "knj,krn->kjr",
+            weights[:, position * 2 * CH : (position + 1) * 2 * CH],
+            edged[position : position + bin_count],
+            preferred_element_type=jnp.float32,
+        )
+        summed = term if summed is None else summed + term
     return summed.reshape(bin_count, 2, LOOKS, edged.shape[1])
 
 

time: 157 us -> 150 us (0.955)
  local copies, waits for them, and re-layouts: 47.1 us -> 44.9 us
  waiting for transfers between devices: 29.1 us -> 27.1 us
  other arithmetic: 16.1 us -> 14.3 us
    all_to_all x0 -> x2, local copies, waits for them, and re-layouts: none -> 7.02 us  [body(): lax.all_to_all(spectra, 'dop', split_axis=0, concat_axis=1, tiled=True)]
    convert_element_type x0 -> x1, local copies, waits for them, and re-layouts: none -> 5.13 us  [doppler_spectra(): return jnp.stack([real_part, imag_part], axis=2).reshape(half, echo_rows....]
    unnamed x16 -> x25, local copies, waits for them, and re-layouts: 11.1 us -> 6.12 us
    another operation x2 -> x1, local copies, waits for them, and re-layouts: 3.8 us -> 0.01 us  [the longest x1 3.79 us: doppler_spectra(): jnp.stack([real_part, imag_part], axis=2)]
    transpose x2 -> x0, local copies, waits for them, and re-layouts: 2.86 us -> none  [body(): jnp.moveaxis(arrived, 0, 1)]
    reshape x1 -> x0, local copies, waits for them, and re-layouts: 2.4 us -> none  [body(): jnp.moveaxis(arrived, 0, 1)]
    reduce_sum x2 -> x0, other arithmetic: 1.63 us -> none  [the longest x1 1 us: unit_vectors(): gains = jnp.sum(targets * solved, axis=1)]
    dot_general x1 -> x3, matrix products: 5.19 us -> 4.53 us  [body(): jnp.einsum('knj,krn->kjr', weights[:, position * 2 * CH:(position + 1) *...]
  transfers between devices with their start and end apart: 2 -> 2, of which waited for: 2 -> 2; matrix products, arithmetic and copies ran while one was open for 0% -> 1% of each run, Pallas kernels for 0% -> 0%
where the time goes in v6:
time: 150 us; the launch traced here: 148 us
  local copies, waits for them, and re-layouts  44.9 us (30%)
  waiting for transfers between devices  27.1 us (18%)
  Pallas kernels  25 us (17%)
  other arithmetic  14.3 us (10%)
  blocking collectives  13.5 us (9%)
  starting transfers between devices  12.6 us (8%)
  matrix products  9.92 us (7%)
    slice x7, local copies, waits for them, and re-layouts, upper_blocks(): snap = jnp.concatenate([edged[b:b + bin_count] for b in range(3)], axis=-1)  25 us
    pallas_call x1, Pallas kernels, unit_vectors(): pl.pallas_call(eliminate, grid=(count,), in_specs=[pl.BlockSpec((1, size,...  25 us
    all_to_all x1, waiting for transfers between devices, body(): lax.all_to_all(spectra, 'dop', split_axis=0, concat_axis=1, tiled=True)  13.9 us
    all_to_all x1, blocking collectives, copy_for_each(): lax.all_to_all(jnp.broadcast_to(array[None], (count, *array.shape)), axis...  13.5 us
    all_to_all x1, waiting for transfers between devices, sum_at_owner(): lax.all_to_all(blocks, axis, split_axis=0, concat_axis=0, tiled=True)  13.2 us
    all_to_all x1, starting transfers between devices, sum_at_owner(): lax.all_to_all(blocks, axis, split_axis=0, concat_axis=0, tiled=True)  7.88 us
    all_to_all x2, local copies, waits for them, and re-layouts, body(): lax.all_to_all(spectra, 'dop', split_axis=0, concat_axis=1, tiled=True)  7.02 us
    unnamed x25, local copies, waits for them, and re-layouts  6.12 us
  transfers between devices with their start and end apart: 2, of which 2 were waited for; matrix products, arithmetic and copies ran while one was open for 1% of the time, Pallas kernels for 0%

profile of v6, /device:TPU:24, one launch (start us, length us, event | category | flops | bytes accessed | tf_op | source)
XLA Modules:
  0.0 147.6 jit_solution(1175549996460353753)
XLA Ops:
  0.1 0.1 sub.15
  0.2 0.4 cosine_convert_fusion
  0.6 0.7 copy-done
  1.2 1.1 fusion.14
  2.4 1.3 fusion.7
  3.6 1.7 %pad_maximum_fusion.1 = bf16[144,64,2,32]{0,1,3,2:T(8,128)(2,1)} fusion(bf16[144,64,1,32]{0,1,3,2:T(8,128)(2,1)S(1)} %get-tuple-element.8, bf16[144,64,1,32]{0,1,3,2:T(8,128)(2,1)S(1)} %get-tuple-element.7), kind=kLoop, calls=%fused_computation.13 | loop fusion | flops 589824 | bytes 2359296 | tf_op jit(solution)/shard_map/stack | solution.py:78
  5.4 5.1 %copy.60 = bf16[144,64,64]{2,1,0:T(8,128)(2,1)S(1)} copy(bf16[144,64,64]{0,1,2:T(8,128)(2,1)} %bitcast.55) | data formatting | bytes 2359296 | tf_op jit(solution)/shard_map/convert_element_type | solution.py:80
  10.5 2.8 %reshape.159 = bf16[8,2,36864]{2,1,0:T(2,128)(2,1)} reshape(bf16[144,64,64]{2,1,0:T(8,128)(2,1)S(1)} %copy.60) | data formatting | bytes 2359296
  13.3 4.7 %all-to-all-start = ((bf16[8,2,36864]{2,1,0:T(2,128)(2,1)}), bf16[8,2,36864]{2,1,0:T(2,128)(2,1)S(1)}, u32[]{:S(2)}, u32[]{:S(2)}) async-start(bf16[8,2,36864]{2,1,0:T(2,128)(2,1)} %reshape.159), calls=%async_computation | async-start | bytes 2359296 | tf_op jit(solution)/shard_map/all_to_all | solution.py:183
  18.0 0.8 convert_element_type.25
  18.7 0.6 pad_maximum_fusion.6
  19.3 13.9 %all-to-all-done = bf16[8,2,36864]{2,1,0:T(2,128)(2,1)S(1)} async-done(((bf16[8,2,36864]{2,1,0:T(2,128)(2,1)}), bf16[8,2,36864]{2,1,0:T(2,128)(2,1)S(1)}, u32[]{:S(2)}, u32[]{:S(2)}) %all-to-all-start) | async-done | bytes 1179680 | tf_op jit(solution)/shard_map/all_to_all | solution.py:183
  33.3 1.6 %reshape.160 = bf16[144,64,64]{2,1,0:T(8,128)(2,1)S(1)} reshape(bf16[8,2,36864]{2,1,0:T(2,128)(2,1)S(1)} %all-to-all-done) | data formatting | bytes 2359296
  34.8 2.7 %copy.64 = bf16[18,8,64,64]{2,1,3,0:T(8,128)(2,1)} copy(bf16[18,8,64,64]{3,2,0,1:T(8,128)(2,1)S(1)} %bitcast.46) | data formatting | bytes 2359296 | tf_op jit(solution)/shard_map/all_to_all | solution.py:183
  37.5 3.5 %fusion.37 = (bf16[16,8,64,64]{3,2,0,1:T(8,128)(2,1)}, bf16[16,8,64,64]{3,2,0,1:T(8,128)(2,1)}, bf16[16,8,64,64]{3,2,0,1:T(8,128)(2,1)}) fusion(bf16[18,8,64,64]{3,2,0,1:T(8,128)(2,1)S(1)} %bitcast.47), kind=kLoop, calls=%fused_computation.78 | loop fusion | bytes 6291456 | tf_op jit(solution)/shard_map/slice | solution.py:101
  41.0 4.4 %all_to_all.22 = bf16[18,512,64]{1,2,0:T(8,128)(2,1)} reshape(bf16[18,8,64,64]{2,1,3,0:T(8,128)(2,1)} %copy.64) | data formatting | bytes 2359296 | tf_op jit(solution)/shard_map/all_to_all | solution.py:183
  45.3 2.2 %slice_negate_fusion = (bf16[18,512,32]{1,2,0:T(8,128)(2,1)S(1)}, bf16[18,512,32]{1,2,0:T(8,128)(2,1)}) fusion(bf16[18,512,64]{1,2,0:T(8,128)(2,1)} %all_to_all.22), kind=kLoop, calls=%fused_computation.32 | loop fusion | flops 294912 | bytes 2359296 | tf_op jit(solution)/shard_map/neg | solution.py:95
  47.5 2.8 %copy.61 = bf16[16,8,64,64]{2,1,3,0:T(8,128)(2,1)} copy(bf16[16,8,64,64]{3,2,0,1:T(8,128)(2,1)S(1)} %copy-done.3) | data formatting | bytes 2097152 | tf_op jit(solution)/shard_map/slice | solution.py:101
  50.3 3.2 %slice.158 = bf16[16,512,64]{1,2,0:T(8,128)(2,1)S(1)} reshape(bf16[16,8,64,64]{2,1,3,0:T(8,128)(2,1)} %copy.61) | data formatting | bytes 2097152 | tf_op jit(solution)/shard_map/slice | solution.py:101
  53.5 4.1 %copy.62 = bf16[16,8,64,64]{2,1,3,0:T(8,128)(2,1)} copy(bf16[16,8,64,64]{3,2,0,1:T(8,128)(2,1)} %get-tuple-element.9) | data formatting | bytes 2097152 | tf_op jit(solution)/shard_map/slice | solution.py:101
  57.6 3.2 %slice.160 = bf16[16,512,64]{1,2,0:T(8,128)(2,1)S(1)} reshape(bf16[16,8,64,64]{2,1,3,0:T(8,128)(2,1)} %copy.62) | data formatting | bytes 2097152 | tf_op jit(solution)/shard_map/slice | solution.py:101
  60.8 4.2 %copy.63 = bf16[16,8,64,64]{2,1,3,0:T(8,128)(2,1)} copy(bf16[16,8,64,64]{3,2,0,1:T(8,128)(2,1)} %get-tuple-element.10) | data formatting | bytes 2097152 | tf_op jit(solution)/shard_map/slice | solution.py:101
  65.0 4.1 %slice.162 = bf16[16,512,64]{1,2,0:T(8,128)(2,1)} reshape(bf16[16,8,64,64]{2,1,3,0:T(8,128)(2,1)} %copy.63) | data formatting | bytes 2097152 | tf_op jit(solution)/shard_map/slice | solution.py:101
  69.1 0.1 fusion.9
  69.2 3.8 %broadcast_multiply_fusion = (bf16[16,1024,192]{1,2,0:T(8,128)(2,1)S(1)}, bf16[16,1024,192]{1,2,0:T(8,128)(2,1)S(1)}) fusion(bf16[16,1024]{1,0:T(8,128)(2,1)S(1)} %copy-done.5, bf16[18,512,32]{1,2,0:T(8,128)(2,1)S(1)} %copy-done.4, bf16[18,512,32]{1,2,0:T(8,128)(2,1)S(1)} %get-tuple-element.14, bf16[16,512,64]{1,2,0:T(8,128)(2,1)S(1)} %get-tuple-element.13, ...), kind=kLoop, calls=%fused_computation.6 | loop fusion | flops 53477376 | bytes 19038208 | tf_op jit(solution)/shard_map/mul | solution.py:105
  73.0 2.0 %fusion.12 = f32[16,32,192]{2,1,0:T(8,128)S(1)} fusion(bf16[16,1024,192]{1,2,0:T(8,128)(2,1)S(1)} %get-tuple-element.6, bf16[16,1024,192]{1,2,0:T(8,128)(2,1)S(1)} %get-tuple-element.5), kind=kOutput, calls=%fused_computation.22 | convolution fusion | flops 201326592 | bytes 7733248 | tf_op jit(solution)/shard_map/krn,krm->knm/dot_general | solution.py:109
  75.1 1.5 %fusion.2 = f32[16,32,128]{2,1,0:T(8,128)S(1)} fusion(bf16[16,1024,192]{1,2,0:T(8,128)(2,1)S(1)} %get-tuple-element.6, bf16[16,1024,192]{1,2,0:T(8,128)(2,1)S(1)} %get-tuple-element.5), kind=kOutput, calls=%fused_computation.3 | convolution fusion | flops 134217728 | bytes 5505024 | tf_op jit(solution)/shard_map/krn,krm->knm/dot_general | solution.py:109
  76.6 0.7 fusion.4
  77.3 1.2 maximum_bitcast_fusion
  78.4 7.9 %all-to-all-start.1 = ((f32[16,1,32,384]{3,2,1,0:T(8,128)}), f32[16,1,32,384]{3,2,1,0:T(8,128)S(1)}, u32[]{:S(2)}, u32[]{:S(2)}) async-start(f32[16,1,32,384]{3,2,1,0:T(8,128)} %maximum_bitcast_fusion), calls=%async_computation.1 | async-start | bytes 1572864 | tf_op jit(solution)/shard_map/all_to_all | solution.py:42
  86.4 0.1 multiply_cosine_fusion
  86.5 0.6 pad_maximum_fusion.5
  87.2 13.2 %all-to-all-done.1 = f32[16,1,32,384]{3,2,1,0:T(8,128)S(1)} async-done(((f32[16,1,32,384]{3,2,1,0:T(8,128)}), f32[16,1,32,384]{3,2,1,0:T(8,128)S(1)}, u32[]{:S(2)}, u32[]{:S(2)}) %all-to-all-start.1) | async-done | bytes 786464 | tf_op jit(solution)/shard_map/all_to_all | solution.py:42
  100.4 0.1 fusion.39
  101.1 0.1 copy.86
  101.2 0.1 copy.89
  101.3 0.1 maximum_bitcast_fusion.3
  101.4 0.1 maximum_maximum_fusion.1
  101.7 0.8 maximum_maximum_fusion.matrix_ref
  102.5 25.0 %shard_map.37 = bf16[1,192,64]{2,1,0:T(8,128)(2,1)} custom-call(f32[1,192,192]{2,1,0:T(8,128)} %maximum_maximum_fusion.matrix_ref, f32[192,64]{1,0:T(8,128)} %bitcast.58), custom_call_target="tpu_custom_call" | custom-call | tf_op jit(solution)/shard_map/pallas_call | solution.py:165
  127.5 0.9 copy.78
  128.5 13.5 %all_to_all.28 = bf16[16,1,192,64]{2,3,1,0:T(8,128)(2,1)S(1)} all-to-all(bf16[16,1,192,64]{2,3,1,0:T(8,128)(2,1)S(1)} %broadcast_in_dim.5), channel_id=1, replica_groups=mesh['dop'=8,'rng'=16] {'rng'}, dimensions={0} | all-to-all | bytes 786432 | tf_op jit(solution)/shard_map/all_to_all | solution.py:54
  142.0 0.4 copy.79
  142.5 0.2 pad_maximum_fusion.2
  142.6 0.8 fusion.17
  143.5 0.8 fusion.20
  144.3 0.4 copy-done.2
  144.7 2.9 %add_add_fusion = f32[16,128,512]{2,1,0:T(8,128)} fusion(f32[16,128,512]{2,1,0:T(8,128)S(1)} %fusion.20, f32[16,128,512]{2,1,0:T(8,128)S(1)} %fusion.17, bf16[16,512,64]{1,2,0:T(8,128)(2,1)S(1)} %copy-done.2, bf16[16,192,64]{2,1,0:T(8,128)(2,1)S(1)} %bitcast.54, bf16[16,192,64]{2,1,0:T(8,128)(2,1)S(1)} %bitcast.51), kind=kOutput, calls=%fused_computation.5 | convolution fusion | flops 136839168 | bytes 14417920 | tf_op jit(solution)/shard_map/knj,krn->kjr/dot_general | solution.py:194
  (35 shorter events, 1.1 us)
Async XLA Ops:
  0.0 1.2 copy-start
  13.3 20.0 %all-to-all-start = ((bf16[8,2,36864]{2,1,0:T(2,128)(2,1)}), bf16[8,2,36864]{2,1,0:T(2,128)(2,1)S(1)}, u32[]{:S(2)}, u32[]{:S(2)}) async-start(bf16[8,2,36864]{2,1,0:T(2,128)(2,1)} %reshape.159), calls=%async_computation | async-start | bytes 2359296 | tf_op jit(solution)/shard_map/all_to_all | solution.py:183
  41.0 6.5 %copy-start.3 = (bf16[16,8,64,64]{3,2,0,1:T(8,128)(2,1)S(1)}, bf16[16,8,64,64]{3,2,0,1:T(8,128)(2,1)}, u32[]{:S(2)}) copy-start(bf16[16,8,64,64]{3,2,0,1:T(8,128)(2,1)} %get-tuple-element.11) | copy-start | bytes 3145732
  60.8 8.3 %copy-start.4 = (bf16[18,512,32]{1,2,0:T(8,128)(2,1)S(1)}, bf16[18,512,32]{1,2,0:T(8,128)(2,1)}, u32[]{:S(2)}) copy-start(bf16[18,512,32]{1,2,0:T(8,128)(2,1)} %get-tuple-element.15) | copy-start | bytes 1769476
  65.0 4.2 %copy-start.5 = (bf16[16,1024]{1,0:T(8,128)(2,1)S(1)}, bf16[16,1024]{1,0:T(8,128)(2,1)}, u32[]{:S(2)}) copy-start(bf16[16,1024]{1,0:T(8,128)(2,1)} %pad_maximum_fusion.6) | copy-start | bytes 98308
  76.6 9.8 %copy-start.6 = (s32[64]{0:T(128)S(1)}, s32[64]{0:T(128)}, u32[]{:S(2)}) copy-start(s32[64]{0:T(128)} %param.5) | copy-start | bytes 772
  78.4 21.9 %all-to-all-start.1 = ((f32[16,1,32,384]{3,2,1,0:T(8,128)}), f32[16,1,32,384]{3,2,1,0:T(8,128)S(1)}, u32[]{:S(2)}, u32[]{:S(2)}) async-start(f32[16,1,32,384]{3,2,1,0:T(8,128)} %maximum_bitcast_fusion), calls=%async_computation.1 | async-start | bytes 1572864 | tf_op jit(solution)/shard_map/all_to_all | solution.py:42
  143.5 1.2 copy-start.2
  143.5 4.1 %copy-start.1 = (bf16[64,2,32,128]{3,2,1,0:T(8,128)(2,1)S(1)}, bf16[64,2,32,128]{3,2,1,0:T(8,128)(2,1)}, u32[]{:S(2)}) copy-start(bf16[64,2,32,128]{3,2,1,0:T(8,128)(2,1)} %param.3) | copy-start | bytes 3145732

commit v7 on v6

--- a/solution.py
+++ b/solution.py
@@ -60,23 +60,22 @@
     return in_order(copy_for_each(array, axis), dim)
 
 
-def twiddles(bin_ids):
+def twiddles():
     pulse_ids = jnp.arange(PULSES, dtype=jnp.int32)
-    phase_ids = bin_ids[:, None] * pulse_ids[None, :] % PULSES
+    phase_ids = pulse_ids[:, None] * pulse_ids[None, :] % PULSES
     angles = phase_ids.astype(jnp.float32) * (2.0 * jnp.pi / PULSES)
     return jnp.concatenate([jnp.cos(angles), jnp.sin(angles)], axis=0).astype(jnp.bfloat16)
 
 
 def doppler_spectra(echo_rows, twiddle):
     product = jnp.einsum("kp,rqcp->krqc", twiddle, echo_rows, preferred_element_type=jnp.float32)
-    half = twiddle.shape[0] // 2
-    cosine = product[:half]
-    sine = product[half:]
+    cosine = product[:PULSES]
+    sine = product[PULSES:]
     real_part = cosine[:, :, 0] + sine[:, :, 1]
     imag_part = cosine[:, :, 1] - sine[:, :, 0]
     return (
         jnp.stack([real_part, imag_part], axis=2)
-        .reshape(half, echo_rows.shape[0], 2 * CH)
+        .reshape(PULSES, echo_rows.shape[0], 2 * CH)
         .astype(jnp.bfloat16)
     )
 
@@ -176,12 +175,10 @@
 
 
 def body(echoes, training, look_index):
-    groups = lax.axis_size("dop")
-    bins_here = PULSES // groups
-    wanted = (jnp.arange(groups)[:, None] * bins_here + jnp.arange(bins_here + 2)[None, :] - 1) % PULSES
-    spectra = doppler_spectra(echoes, twiddles(wanted.reshape(-1).astype(jnp.int32)))
-    edged = lax.all_to_all(spectra, "dop", split_axis=0, concat_axis=1, tiled=True)
-    bin_count = bins_here
+    spectra = doppler_spectra(echoes, twiddles())
+    turned = lax.all_to_all(spectra, "dop", split_axis=0, concat_axis=1, tiled=True)
+    edged = padded(turned, (("dop", 0),), 1)
+    bin_count = edged.shape[0] - 2
     upper = upper_blocks(edged, training.astype(jnp.bfloat16))
     my_upper = sum_at_owner(upper, "rng", 0)
     my_unit = unit_vectors(full_from_upper(my_upper), steering(look_index))

time: 150 us -> 124 us (0.83); the launches traced: 148 us -> 124 us
  local copies, waits for them, and re-layouts: 44.9 us -> 20.5 us
  other arithmetic: 14.3 us -> 8.3 us
  blocking collectives: 13.5 us -> 16.8 us
  starting transfers between devices: 12.6 us -> 14.3 us
  waiting for transfers between devices: 27.1 us -> 28.8 us
    slice x7 -> x3, local copies, waits for them, and re-layouts: 25 us -> 0.21 us  [the longest x2 0.12 us: padded(): lax.slice_in_dim(block, 0, width, axis=dim)]
    all_to_all x1, blocking collectives: 13.5 us -> 16.8 us  [copy_for_each(): lax.all_to_all(jnp.broadcast_to(array[None], (count, *array.shape)), axis...]
    neg x1, other arithmetic: 2.15 us -> 0.08 us  [rotate(): return jnp.concatenate([-values[..., CH:], values[..., :CH]], axis=-1)]
    unnamed x25 -> x26, local copies, waits for them, and re-layouts: 6.12 us -> 8.02 us
    ppermute x0 -> x2, waiting for transfers between devices: none -> 1.9 us  [the longest x1 1.89 us: padded(): lax.ppermute(lax.slice_in_dim(block, 0, width, axis=dim), axis, backward)]
    ppermute x0 -> x2, starting transfers between devices: none -> 1.74 us  [the longest x1 1.72 us: padded(): lax.ppermute(lax.slice_in_dim(block, 0, width, axis=dim), axis, backward)]
  transfers between devices with their start and end apart: 2 -> 4, of which waited for: 2 -> 3; matrix products, arithmetic and copies ran while one was open for 1% -> 3% of each run, Pallas kernels for 0% -> 0%
where the time goes in v7:
time: 124 us
  waiting for transfers between devices  28.8 us (23%)
  Pallas kernels  25 us (20%)
  local copies, waits for them, and re-layouts  20.5 us (17%)
  blocking collectives  16.8 us (14%)
  starting transfers between devices  14.3 us (12%)
  matrix products  9.67 us (8%)
  other arithmetic  8.3 us (7%)
    pallas_call x1, Pallas kernels, unit_vectors(): pl.pallas_call(eliminate, grid=(count,), in_specs=[pl.BlockSpec((1, size,...  25 us
    all_to_all x1, blocking collectives, copy_for_each(): lax.all_to_all(jnp.broadcast_to(array[None], (count, *array.shape)), axis...  16.8 us
    all_to_all x1, waiting for transfers between devices, body(): lax.all_to_all(spectra, 'dop', split_axis=0, concat_axis=1, tiled=True)  14 us
    all_to_all x1, waiting for transfers between devices, sum_at_owner(): lax.all_to_all(blocks, axis, split_axis=0, concat_axis=0, tiled=True)  12.9 us
    unnamed x26, local copies, waits for them, and re-layouts  8.02 us
    all_to_all x1, starting transfers between devices, sum_at_owner(): lax.all_to_all(blocks, axis, split_axis=0, concat_axis=0, tiled=True)  7.87 us
    all_to_all x2, local copies, waits for them, and re-layouts, body(): lax.all_to_all(spectra, 'dop', split_axis=0, concat_axis=1, tiled=True)  6.02 us
    convert_element_type x1, local copies, waits for them, and re-layouts, doppler_spectra(): return jnp.stack([real_part, imag_part], axis=2).reshape(PULSES, echo_row...  4.72 us
  transfers between devices with their start and end apart: 4, of which 3 were waited for; matrix products, arithmetic and copies ran while one was open for 3% of the time, Pallas kernels for 0%

profile of v7, /device:TPU:24, one launch (start us, length us, event | category | flops | bytes accessed | tf_op | source)
XLA Modules:
  0.0 123.7 jit_solution(7300212804344190899)
XLA Ops:
  0.0 0.3 sine_convert_fusion
  0.3 0.9 copy-done
  1.2 0.9 fusion.14
  2.1 0.3 fusion.13
  2.4 1.1 pad_maximum_fusion.3
  3.5 4.7 %copy.58 = bf16[128,64,64]{2,1,0:T(8,128)(2,1)S(1)} copy(bf16[128,64,64]{0,1,2:T(8,128)(2,1)} %bitcast.45) | data formatting | bytes 2097152 | tf_op jit(solution)/shard_map/convert_element_type | solution.py:79
  8.2 2.7 %reshape.125 = bf16[8,2,32768]{2,1,0:T(2,128)(2,1)} reshape(bf16[128,64,64]{2,1,0:T(8,128)(2,1)S(1)} %copy.58) | data formatting | bytes 2097152
  10.9 4.7 %all-to-all-start = ((bf16[8,2,32768]{2,1,0:T(2,128)(2,1)}), bf16[8,2,32768]{2,1,0:T(2,128)(2,1)}, u32[]{:S(2)}, u32[]{:S(2)}) async-start(bf16[8,2,32768]{2,1,0:T(2,128)(2,1)} %reshape.125), calls=%async_computation | async-start | bytes 2097152 | tf_op jit(solution)/shard_map/all_to_all | solution.py:179
  15.6 14.0 %all-to-all-done = bf16[8,2,32768]{2,1,0:T(2,128)(2,1)} async-done(((bf16[8,2,32768]{2,1,0:T(2,128)(2,1)}), bf16[8,2,32768]{2,1,0:T(2,128)(2,1)}, u32[]{:S(2)}, u32[]{:S(2)}) %all-to-all-start) | async-done | bytes 1048608 | tf_op jit(solution)/shard_map/all_to_all | solution.py:179
  29.6 3.1 %reshape.126 = bf16[128,64,64]{2,1,0:T(8,128)(2,1)S(1)} reshape(bf16[8,2,32768]{2,1,0:T(2,128)(2,1)} %all-to-all-done) | data formatting | bytes 2097152
  32.7 0.1 copy.80
  32.8 2.8 %copy.60 = bf16[16,8,64,64]{2,1,3,0:T(8,128)(2,1)} copy(bf16[16,8,64,64]{3,2,0,1:T(8,128)(2,1)S(1)} %bitcast.44) | data formatting | bytes 2097152 | tf_op jit(solution)/shard_map/all_to_all | solution.py:179
  35.7 3.2 %all_to_all.22 = bf16[16,512,64]{1,2,0:T(8,128)(2,1)S(1)} reshape(bf16[16,8,64,64]{2,1,3,0:T(8,128)(2,1)} %copy.60) | data formatting | bytes 2097152 | tf_op jit(solution)/shard_map/all_to_all | solution.py:179
  38.9 0.1 copy.81
  39.0 1.7 %collective-permute-start.1 = (bf16[1,512,64]{1,2,0:T(8,128)(2,1)S(1)}, bf16[1,512,64]{1,2,0:T(8,128)(2,1)S(1)}, u32[]{:S(2)}, u32[]{:S(2)}) collective-permute-start(bf16[1,512,64]{1,2,0:T(8,128)(2,1)S(1)} %copy.81), channel_id=1, source_target_pairs={{16,0},{32,16},{48,32},{64,48},{80,64},{96,80},{112,96},{0,112},{1... | collective-permute-start | bytes 196616 | tf_op jit(solution)/shard_map/ppermute | solution.py:29
  40.7 1.9 %collective-permute-done.1 = bf16[1,512,64]{1,2,0:T(8,128)(2,1)S(1)} collective-permute-done((bf16[1,512,64]{1,2,0:T(8,128)(2,1)S(1)}, bf16[1,512,64]{1,2,0:T(8,128)(2,1)S(1)}, u32[]{:S(2)}, u32[]{:S(2)}) %collective-permute-start.1) | collective-permute-done | bytes 65568 | tf_op jit(solution)/shard_map/ppermute | solution.py:29
  42.6 0.3 pad_maximum_fusion.1
  42.9 0.1 slice_negate_fusion
  43.0 0.3 fusion.7
  43.3 2.4 %broadcast_multiply_fusion = (bf16[16,1024,192]{1,2,0:T(8,128)(2,1)S(1)}, bf16[16,1024,192]{1,2,0:T(8,128)(2,1)S(1)}) fusion(bf16[16,1024]{1,0:T(8,128)(2,1)S(1)} %pad_maximum_fusion.10, bf16[18,512,32]{1,2,0:T(8,128)(2,1)S(1)} %get-tuple-element.14, bf16[18,512,32]{1,2,0:T(8,128)(2,1)S(1)} %get-tuple-element.13, ...), kind=kLoop, calls=%fused_computation.6 | loop fusion | flops 53477376 | bytes 19038208 | tf_op jit(solution)/shard_map/mul | solution.py:104
  45.8 2.0 %fusion.10 = f32[16,32,192]{2,1,0:T(8,128)S(1)} fusion(bf16[16,1024,192]{1,2,0:T(8,128)(2,1)S(1)} %get-tuple-element.6, bf16[16,1024,192]{1,2,0:T(8,128)(2,1)S(1)} %get-tuple-element.5), kind=kOutput, calls=%fused_computation.17 | convolution fusion | flops 201326592 | bytes 7733248 | tf_op jit(solution)/shard_map/krn,krm->knm/dot_general | solution.py:108
  47.8 1.5 %fusion.2 = f32[16,32,128]{2,1,0:T(8,128)S(1)} fusion(bf16[16,1024,192]{1,2,0:T(8,128)(2,1)S(1)} %get-tuple-element.6, bf16[16,1024,192]{1,2,0:T(8,128)(2,1)S(1)} %get-tuple-element.5), kind=kOutput, calls=%fused_computation.3 | convolution fusion | flops 134217728 | bytes 5505024 | tf_op jit(solution)/shard_map/krn,krm->knm/dot_general | solution.py:108
  49.3 0.7 fusion.4
  50.0 1.2 maximum_bitcast_fusion
  51.2 7.9 %all-to-all-start.1 = ((f32[16,1,32,384]{3,2,1,0:T(8,128)}), f32[16,1,32,384]{3,2,1,0:T(8,128)S(1)}, u32[]{:S(2)}, u32[]{:S(2)}) async-start(f32[16,1,32,384]{3,2,1,0:T(8,128)} %maximum_bitcast_fusion), calls=%async_computation.1 | async-start | bytes 1572864 | tf_op jit(solution)/shard_map/all_to_all | solution.py:42
  59.1 0.1 multiply_cosine_fusion
  59.3 0.6 pad_maximum_fusion.9
  59.9 12.9 %all-to-all-done.1 = f32[16,1,32,384]{3,2,1,0:T(8,128)S(1)} async-done(((f32[16,1,32,384]{3,2,1,0:T(8,128)}), f32[16,1,32,384]{3,2,1,0:T(8,128)S(1)}, u32[]{:S(2)}, u32[]{:S(2)}) %all-to-all-start.1) | async-done | bytes 786464 | tf_op jit(solution)/shard_map/all_to_all | solution.py:42
  72.9 0.1 fusion.39
  73.5 0.1 copy.82
  73.6 0.1 copy.85
  73.7 0.1 copy.88
  73.8 0.1 maximum_bitcast_fusion.3
  73.9 0.1 maximum_bitcast_fusion.4
  73.9 0.1 maximum_maximum_fusion.1
  74.1 0.1 copy.74
  74.3 0.8 maximum_maximum_fusion.matrix_ref
  75.1 25.0 %shard_map.37 = bf16[1,192,64]{2,1,0:T(8,128)(2,1)} custom-call(f32[1,192,192]{2,1,0:T(8,128)} %maximum_maximum_fusion.matrix_ref, f32[192,64]{1,0:T(8,128)} %bitcast.50), custom_call_target="tpu_custom_call" | custom-call | tf_op jit(solution)/shard_map/pallas_call | solution.py:164
  100.1 0.9 copy.75
  101.1 16.8 %all_to_all.28 = bf16[16,1,192,64]{2,3,1,0:T(8,128)(2,1)S(1)} all-to-all(bf16[16,1,192,64]{2,3,1,0:T(8,128)(2,1)S(1)} %broadcast_in_dim.5), channel_id=1, replica_groups=mesh['dop'=8,'rng'=16] {'rng'}, dimensions={0} | all-to-all | bytes 786432 | tf_op jit(solution)/shard_map/all_to_all | solution.py:54
  117.9 0.4 copy.76
  118.3 0.1 slice_negate_fusion.1
  118.4 0.2 pad_maximum_fusion.4
  118.5 0.8 fusion.17
  119.4 0.2 copy-done.2
  119.6 0.8 fusion.20
  120.4 0.4 copy-done.4
  120.8 2.9 %add_add_fusion = f32[16,128,512]{2,1,0:T(8,128)} fusion(f32[16,128,512]{2,1,0:T(8,128)S(1)} %fusion.20, f32[16,128,512]{2,1,0:T(8,128)S(1)} %fusion.17, bf16[16,512,64]{1,2,0:T(8,128)(2,1)S(1)} %copy-done.4, bf16[16,192,64]{2,1,0:T(8,128)(2,1)S(1)} %bitcast.42, bf16[16,192,64]{2,1,0:T(8,128)(2,1)S(1)} %bitcast.39), kind=kOutput, calls=%fused_computation.5 | convolution fusion | flops 136839168 | bytes 14417920 | tf_op jit(solution)/shard_map/knj,krn->kjr/dot_general | solution.py:191
  (35 shorter events, 0.9 us)
Async XLA Ops:
  0.0 1.2 copy-start
  3.5 12.1 %copy-start.5 = (s32[16,512]{1,0:T(8,128)S(1)}, s32[16,512]{1,0:T(8,128)}, u32[]{:S(2)}) copy-start(s32[16,512]{1,0:T(8,128)} %param.4) | copy-start | bytes 98308
  10.9 18.7 %all-to-all-start = ((bf16[8,2,32768]{2,1,0:T(2,128)(2,1)}), bf16[8,2,32768]{2,1,0:T(2,128)(2,1)}, u32[]{:S(2)}, u32[]{:S(2)}) async-start(bf16[8,2,32768]{2,1,0:T(2,128)(2,1)} %reshape.125), calls=%async_computation | async-start | bytes 2097152 | tf_op jit(solution)/shard_map/all_to_all | solution.py:179
  32.8 7.9 %collective-permute-start = (bf16[1,512,64]{1,2,0:T(8,128)(2,1)S(1)}, bf16[1,512,64]{1,2,0:T(8,128)(2,1)S(1)}, u32[]{:S(2)}, u32[]{:S(2)}) collective-permute-start(bf16[1,512,64]{1,2,0:T(8,128)(2,1)S(1)} %copy.80), channel_id=1, source_target_pairs={{0,16},{16,32},{32,48},{48,64},{64,80},{80,96},{96,112},{112,0},{1... | collective-permute-start | bytes 196616 | tf_op jit(solution)/shard_map/ppermute | solution.py:26
  39.0 3.6 %collective-permute-start.1 = (bf16[1,512,64]{1,2,0:T(8,128)(2,1)S(1)}, bf16[1,512,64]{1,2,0:T(8,128)(2,1)S(1)}, u32[]{:S(2)}, u32[]{:S(2)}) collective-permute-start(bf16[1,512,64]{1,2,0:T(8,128)(2,1)S(1)} %copy.81), channel_id=1, source_target_pairs={{16,0},{32,16},{48,32},{64,48},{80,64},{96,80},{112,96},{0,112},{1... | collective-permute-start | bytes 196616 | tf_op jit(solution)/shard_map/ppermute | solution.py:29
  42.9 2.9 %copy-start.1 = (bf16[16,512,64]{1,2,0:T(8,128)(2,1)}, bf16[16,512,64]{1,2,0:T(8,128)(2,1)S(1)}, u32[]{:S(2)}) copy-start(bf16[16,512,64]{1,2,0:T(8,128)(2,1)S(1)} %get-tuple-element.17) | copy-start | bytes 3145732
  42.9 2.9 %copy-start.3 = (bf16[16,512,64]{1,2,0:T(8,128)(2,1)}, bf16[16,512,64]{1,2,0:T(8,128)(2,1)S(1)}, u32[]{:S(2)}) copy-start(bf16[16,512,64]{1,2,0:T(8,128)(2,1)S(1)} %get-tuple-element.15) | copy-start | bytes 3145732
  49.3 9.8 %copy-start.6 = (s32[64]{0:T(128)S(1)}, s32[64]{0:T(128)}, u32[]{:S(2)}) copy-start(s32[64]{0:T(128)} %param.5) | copy-start | bytes 772
  51.2 21.6 %all-to-all-start.1 = ((f32[16,1,32,384]{3,2,1,0:T(8,128)}), f32[16,1,32,384]{3,2,1,0:T(8,128)S(1)}, u32[]{:S(2)}, u32[]{:S(2)}) async-start(f32[16,1,32,384]{3,2,1,0:T(8,128)} %maximum_bitcast_fusion), calls=%async_computation.1 | async-start | bytes 1572864 | tf_op jit(solution)/shard_map/all_to_all | solution.py:42
  118.4 1.2 copy-start.2
  119.6 1.2 copy-start.4

commit v8 on v2

--- a/solution.py
+++ b/solution.py
@@ -2,6 +2,8 @@
 import jax.numpy as jnp
 from jax import lax
 from jax.sharding import PartitionSpec as P
+from jax.experimental import pallas as pl
+from jax.experimental.pallas import tpu as pltpu
 
 CH = 32
 PULSES = 128
@@ -113,35 +115,90 @@
     return jnp.concatenate(pieces, axis=-1)
 
 
-def full_from_upper(upper):
-    width = 2 * CH
-
-    def block(left_pos, right_pos):
+def eliminate(real_ref, imag_ref, steer_re_ref, steer_im_ref, unit_ref, wr_ref, wi_ref):
+    rows, cols = wr_ref.shape
+    gap = cols - LOOKS
+    lane_ids = lax.broadcasted_iota(jnp.int32, (1, cols), 1)
+    row_ids = lax.broadcasted_iota(jnp.int32, (rows, 1), 0)
+    diagonal = row_ids == lax.broadcasted_iota(jnp.int32, (1, rows), 1)
+    same = real_ref[0]
+    power = 2.0 * jnp.sum(jnp.where(diagonal, same, 0.0)) / SNAP + epsilon
+    steer_re = steer_re_ref[...]
+    steer_im = steer_im_ref[...]
+    wr_ref[...] = jnp.zeros(wr_ref.shape, jnp.float32)
+    wi_ref[...] = jnp.zeros(wi_ref.shape, jnp.float32)
+    wr_ref[:, :rows] = same / power + jnp.where(diagonal, loading, 0.0)
+    wi_ref[:, :rows] = imag_ref[0] / power
+    wr_ref[:, gap:] = steer_re
+    wi_ref[:, gap:] = steer_im
+
+    def step(j, carry):
+        cur_r = wr_ref[...]
+        cur_i = wi_ref[...]
+        row_r = wr_ref[pl.ds(j, 1), :]
+        row_i = wi_ref[pl.ds(j, 1), :]
+        hit = lane_ids == j
+        col_r = jnp.sum(jnp.where(hit, cur_r, 0.0), axis=1, keepdims=True)
+        col_i = jnp.sum(jnp.where(hit, cur_i, 0.0), axis=1, keepdims=True)
+        lead_r = jnp.sum(jnp.where(hit, row_r, 0.0), axis=1, keepdims=True)
+        lead_i = jnp.sum(jnp.where(hit, row_i, 0.0), axis=1, keepdims=True)
+        norm = lead_r * lead_r + lead_i * lead_i
+        scaled_r = (row_r * lead_r + row_i * lead_i) / norm
+        scaled_i = (row_i * lead_r - row_r * lead_i) / norm
+        is_row = row_ids == j
+        wr_ref[...] = jnp.where(is_row, scaled_r, cur_r - (col_r * scaled_r - col_i * scaled_i))
+        wi_ref[...] = jnp.where(is_row, scaled_i, cur_i - (col_r * scaled_i + col_i * scaled_r))
+        return carry
+
+    lax.fori_loop(0, rows, step, 0)
+    solved_re = wr_ref[:, gap:]
+    solved_im = wi_ref[:, gap:]
+    root = jnp.sqrt(jnp.sum(steer_re * solved_re + steer_im * solved_im, axis=0, keepdims=True))
+    unit_re = (solved_re / root).astype(unit_ref.dtype)
+    unit_im = (solved_im / root).astype(unit_ref.dtype)
+    for pos in range(rows // CH):
+        unit_ref[0, 2 * pos * CH : (2 * pos + 1) * CH, :] = unit_re[pos * CH : (pos + 1) * CH]
+        unit_ref[0, (2 * pos + 1) * CH : (2 * pos + 2) * CH, :] = unit_im[pos * CH : (pos + 1) * CH]
+
+
+def unit_vectors(same, cross, steer):
+    count, size, _ = same.shape
+    parts = steer.reshape(size // CH, 2, CH, LOOKS)
+    steer_re = parts[:, 0].reshape(size, LOOKS)
+    steer_im = parts[:, 1].reshape(size, LOOKS)
+    width = ((size + 127) // 128) * 128 + LOOKS
+    matrix = pl.BlockSpec((1, size, size), lambda i: (i, 0, 0))
+    vector = pl.BlockSpec((size, LOOKS), lambda i: (0, 0))
+    return pl.pallas_call(
+        eliminate,
+        grid=(count,),
+        in_specs=[matrix, matrix, vector, vector],
+        out_specs=pl.BlockSpec((1, 2 * size, LOOKS), lambda i: (i, 0, 0)),
+        out_shape=jax.ShapeDtypeStruct((count, 2 * size, LOOKS), jnp.bfloat16),
+        scratch_shapes=[pltpu.VMEM((size, width), jnp.float32)] * 2,
+    )(same, cross, steer_re, steer_im)
+
+
+def hermitian_parts(upper):
+    def piece(left_pos, right_pos):
+        start = block_pairs.index((left_pos, right_pos)) * 2 * CH
+        return upper[:, :, start : start + 2 * CH]
+
+    def real_block(left_pos, right_pos):
         if left_pos > right_pos:
-            return jnp.swapaxes(block(right_pos, left_pos), 1, 2)
-        start = block_pairs.index((left_pos, right_pos)) * width
-        piece = upper[:, :, start : start + width]
-        same, cross = piece[..., :CH], piece[..., CH:]
-        return jnp.concatenate(
-            [jnp.concatenate([same, cross], -1), jnp.concatenate([-cross, same], -1)], 1
-        )
-
-    rows = [jnp.concatenate([block(b, c) for c in range(3)], -1) for b in range(3)]
-    return jnp.concatenate(rows, 1)
-
-
-def unit_vectors(matrix, steer):
-    bin_count = matrix.shape[0]
-    power = jnp.trace(matrix, axis1=1, axis2=2) / SNAP + epsilon
-    regular = matrix / power[:, None, None] + loading * jnp.eye(SNAP, dtype=jnp.float32)
-    factor = jnp.linalg.cholesky(regular)
-    targets = jnp.broadcast_to(steer, (bin_count, SNAP, LOOKS))
-    forward = lax.linalg.triangular_solve(factor, targets, left_side=True, lower=True)
-    solved = lax.linalg.triangular_solve(
-        factor, forward, left_side=True, lower=True, transpose_a=True
-    )
-    gains = jnp.sum(targets * solved, axis=1)
-    return (solved / jnp.sqrt(gains)[:, None, :]).astype(jnp.bfloat16)
+            return jnp.swapaxes(real_block(right_pos, left_pos), 1, 2)
+        return piece(left_pos, right_pos)[..., :CH]
+
+    def imag_block(left_pos, right_pos):
+        if left_pos > right_pos:
+            return -jnp.swapaxes(imag_block(right_pos, left_pos), 1, 2)
+        return -piece(left_pos, right_pos)[..., CH:]
+
+    def assemble(block):
+        rows = [jnp.concatenate([block(b, c) for c in range(3)], -1) for b in range(3)]
+        return jnp.concatenate(rows, 1)
+
+    return assemble(real_block), assemble(imag_block)
 
 
 def body(echoes, training, look_index):
@@ -151,7 +208,7 @@
     bin_count = edged.shape[0] - 2
     upper = upper_blocks(edged, training.astype(jnp.bfloat16))
     my_upper = sum_at_owner(upper, "rng", 0)
-    my_unit = unit_vectors(full_from_upper(my_upper), steering(look_index))
+    my_unit = unit_vectors(*hermitian_parts(my_upper), steering(look_index))
     unit = gather_directly(my_unit, "rng", 0)
     shaped = unit.reshape(bin_count, 3, 2, CH, LOOKS)
     rotated = jnp.stack([-shaped[:, :, 1], shaped[:, :, 0]], axis=2).reshape(bin_count, SNAP, LOOKS)

time: 151 us -> 114 us (0.75)
  other arithmetic: 56.6 us -> 7.95 us
  Pallas kernels: 0 us -> 14.6 us
  between operations: 2.4 us -> 0.29 us
  matrix products: 11.4 us -> 9.66 us
    another operation x15 -> x2, other arithmetic: 49.2 us -> 0.58 us  [the longest x7 28.8 us: unit_vectors(): factor = jnp.linalg.cholesky(regular)]
    pallas_call x0 -> x1, Pallas kernels: none -> 14.6 us  [unit_vectors(): pl.pallas_call(eliminate, grid=(count,), in_specs=[matrix, matrix, vector...]
    another operation x8 -> x0, matrix products: 1.7 us -> none  [the longest x3 0.69 us: unit_vectors(): lax.linalg.triangular_solve(factor, targets, left_side=True, lower=True)]
    unnamed x17 -> x20, local copies, waits for them, and re-layouts: 7.32 us -> 7.53 us
  transfers between devices with their start and end apart: 4 -> 4, of which waited for: 3 -> 3; matrix products, arithmetic and copies ran while one was open for 2% -> 3% of each run, Pallas kernels for 0% -> 0%
where the time goes in v8:
time: 114 us; the launch traced here: 113 us
  waiting for transfers between devices  28.7 us (25%)
  local copies, waits for them, and re-layouts  20.7 us (18%)
  blocking collectives  16.8 us (15%)
  Pallas kernels  14.6 us (13%)
  starting transfers between devices  14.3 us (13%)
  matrix products  9.66 us (8%)
  other arithmetic  7.95 us (7%)
    all_to_all x1, blocking collectives, copy_for_each(): lax.all_to_all(jnp.broadcast_to(array[None], (count, *array.shape)), axis...  16.8 us
    pallas_call x1, Pallas kernels, unit_vectors(): pl.pallas_call(eliminate, grid=(count,), in_specs=[matrix, matrix, vector...  14.6 us
    all_to_all x1, waiting for transfers between devices, body(): lax.all_to_all(spectra, 'dop', split_axis=0, concat_axis=1, tiled=True)  13.9 us
    all_to_all x1, waiting for transfers between devices, sum_at_owner(): lax.all_to_all(blocks, axis, split_axis=0, concat_axis=0, tiled=True)  12.9 us
    all_to_all x1, starting transfers between devices, sum_at_owner(): lax.all_to_all(blocks, axis, split_axis=0, concat_axis=0, tiled=True)  7.87 us
    unnamed x20, local copies, waits for them, and re-layouts  7.53 us
    all_to_all x2, local copies, waits for them, and re-layouts, body(): lax.all_to_all(spectra, 'dop', split_axis=0, concat_axis=1, tiled=True)  6.02 us
    convert_element_type x1, local copies, waits for them, and re-layouts, doppler_spectra(): return jnp.stack([real_part, imag_part], axis=2).reshape(PULSES, echo_row...  4.72 us
  transfers between devices with their start and end apart: 4, of which 3 were waited for; matrix products, arithmetic and copies ran while one was open for 3% of the time, Pallas kernels for 0%

profile of v8, /device:TPU:24, one launch (start us, length us, event | category | flops | bytes accessed | tf_op | source)
XLA Modules:
  0.0 113.2 jit_solution(9622763172770840092)
XLA Ops:
  0.0 0.3 sine_convert_fusion
  0.3 0.9 copy-done
  1.2 0.9 fusion.14
  2.1 0.3 fusion.13
  2.4 1.1 pad_maximum_fusion.3
  3.5 4.7 %copy.54 = bf16[128,64,64]{2,1,0:T(8,128)(2,1)S(1)} copy(bf16[128,64,64]{0,1,2:T(8,128)(2,1)} %bitcast.50) | data formatting | bytes 2097152 | tf_op jit(solution)/shard_map/convert_element_type | solution.py:79
  8.2 2.7 %reshape.121 = bf16[8,2,32768]{2,1,0:T(2,128)(2,1)} reshape(bf16[128,64,64]{2,1,0:T(8,128)(2,1)S(1)} %copy.54) | data formatting | bytes 2097152
  10.9 4.7 %all-to-all-start = ((bf16[8,2,32768]{2,1,0:T(2,128)(2,1)}), bf16[8,2,32768]{2,1,0:T(2,128)(2,1)}, u32[]{:S(2)}, u32[]{:S(2)}) async-start(bf16[8,2,32768]{2,1,0:T(2,128)(2,1)} %reshape.121), calls=%async_computation | async-start | bytes 2097152 | tf_op jit(solution)/shard_map/all_to_all | solution.py:206
  15.6 13.9 %all-to-all-done = bf16[8,2,32768]{2,1,0:T(2,128)(2,1)} async-done(((bf16[8,2,32768]{2,1,0:T(2,128)(2,1)}), bf16[8,2,32768]{2,1,0:T(2,128)(2,1)}, u32[]{:S(2)}, u32[]{:S(2)}) %all-to-all-start) | async-done | bytes 1048608 | tf_op jit(solution)/shard_map/all_to_all | solution.py:206
  29.6 3.1 %reshape.122 = bf16[128,64,64]{2,1,0:T(8,128)(2,1)S(1)} reshape(bf16[8,2,32768]{2,1,0:T(2,128)(2,1)} %all-to-all-done) | data formatting | bytes 2097152
  32.7 0.1 copy.74
  32.8 2.8 %copy.56 = bf16[16,8,64,64]{2,1,3,0:T(8,128)(2,1)} copy(bf16[16,8,64,64]{3,2,0,1:T(8,128)(2,1)S(1)} %bitcast.49) | data formatting | bytes 2097152 | tf_op jit(solution)/shard_map/all_to_all | solution.py:206
  35.7 3.2 %all_to_all.22 = bf16[16,512,64]{1,2,0:T(8,128)(2,1)S(1)} reshape(bf16[16,8,64,64]{2,1,3,0:T(8,128)(2,1)} %copy.56) | data formatting | bytes 2097152 | tf_op jit(solution)/shard_map/all_to_all | solution.py:206
  38.9 0.1 copy.75
  39.0 1.7 %collective-permute-start.1 = (bf16[1,512,64]{1,2,0:T(8,128)(2,1)S(1)}, bf16[1,512,64]{1,2,0:T(8,128)(2,1)S(1)}, u32[]{:S(2)}, u32[]{:S(2)}) collective-permute-start(bf16[1,512,64]{1,2,0:T(8,128)(2,1)S(1)} %copy.75), channel_id=1, source_target_pairs={{16,0},{32,16},{48,32},{64,48},{80,64},{96,80},{112,96},{0,112},{1... | collective-permute-start | bytes 196616 | tf_op jit(solution)/shard_map/ppermute | solution.py:29
  40.7 1.9 %collective-permute-done.1 = bf16[1,512,64]{1,2,0:T(8,128)(2,1)S(1)} collective-permute-done((bf16[1,512,64]{1,2,0:T(8,128)(2,1)S(1)}, bf16[1,512,64]{1,2,0:T(8,128)(2,1)S(1)}, u32[]{:S(2)}, u32[]{:S(2)}) %collective-permute-start.1) | collective-permute-done | bytes 65568 | tf_op jit(solution)/shard_map/ppermute | solution.py:29
  42.6 0.3 pad_maximum_fusion.1
  42.9 0.1 slice_negate_fusion
  43.0 0.3 fusion.7
  43.3 2.4 %broadcast_multiply_fusion = (bf16[16,1024,192]{1,2,0:T(8,128)(2,1)S(1)}, bf16[16,1024,192]{1,2,0:T(8,128)(2,1)S(1)}) fusion(bf16[16,1024]{1,0:T(8,128)(2,1)S(1)} %pad_maximum_fusion.10, bf16[18,512,32]{1,2,0:T(8,128)(2,1)S(1)} %get-tuple-element.14, bf16[18,512,32]{1,2,0:T(8,128)(2,1)S(1)} %get-tuple-element.13, ...), kind=kLoop, calls=%fused_computation.6 | loop fusion | flops 53477376 | bytes 19038208 | tf_op jit(solution)/shard_map/mul | solution.py:104
  45.8 2.0 %fusion.10 = f32[16,32,192]{2,1,0:T(8,128)S(1)} fusion(bf16[16,1024,192]{1,2,0:T(8,128)(2,1)S(1)} %get-tuple-element.6, bf16[16,1024,192]{1,2,0:T(8,128)(2,1)S(1)} %get-tuple-element.5), kind=kOutput, calls=%fused_computation.17 | convolution fusion | flops 201326592 | bytes 7733248 | tf_op jit(solution)/shard_map/krn,krm->knm/dot_general | solution.py:108
  47.8 1.5 %fusion.2 = f32[16,32,128]{2,1,0:T(8,128)S(1)} fusion(bf16[16,1024,192]{1,2,0:T(8,128)(2,1)S(1)} %get-tuple-element.6, bf16[16,1024,192]{1,2,0:T(8,128)(2,1)S(1)} %get-tuple-element.5), kind=kOutput, calls=%fused_computation.3 | convolution fusion | flops 134217728 | bytes 5505024 | tf_op jit(solution)/shard_map/krn,krm->knm/dot_general | solution.py:108
  49.3 0.7 fusion.4
  50.0 1.2 %maximum_bitcast_fusion = f32[16,1,32,384]{3,2,1,0:T(8,128)} fusion(f32[16,32,64]{2,1,0:T(8,128)S(1)} %fusion.4, f32[16,32,128]{2,1,0:T(8,128)S(1)} %fusion.2, f32[16,32,192]{2,1,0:T(8,128)S(1)} %fusion.10), kind=kLoop, calls=%fused_computation.28 | loop fusion | flops 393216 | bytes 1572864 | tf_op jit(solution)/shard_map/reshape | solution.py:36
  51.2 7.9 %all-to-all-start.1 = ((f32[16,1,32,384]{3,2,1,0:T(8,128)}), f32[16,1,32,384]{3,2,1,0:T(8,128)S(1)}, u32[]{:S(2)}, u32[]{:S(2)}) async-start(f32[16,1,32,384]{3,2,1,0:T(8,128)} %maximum_bitcast_fusion), calls=%async_computation.1 | async-start | bytes 1572864 | tf_op jit(solution)/shard_map/all_to_all | solution.py:42
  59.1 0.1 multiply_cosine_fusion
  59.3 0.6 fusion.38
  59.9 12.9 %all-to-all-done.1 = f32[16,1,32,384]{3,2,1,0:T(8,128)S(1)} async-done(((f32[16,1,32,384]{3,2,1,0:T(8,128)}), f32[16,1,32,384]{3,2,1,0:T(8,128)S(1)}, u32[]{:S(2)}, u32[]{:S(2)}) %all-to-all-start.1) | async-done | bytes 786464 | tf_op jit(solution)/shard_map/all_to_all | solution.py:42
  72.9 0.1 slice_negate_fusion.4
  73.0 0.1 copy.78
  73.1 0.1 copy.66
  73.1 0.1 copy.67
  73.2 0.1 copy.68
  73.3 0.1 copy.76
  73.4 0.1 copy.64
  73.5 0.8 maximum_maximum_fusion.real_ref
  74.2 0.7 maximum_maximum_fusion.1.imag_ref
  74.9 14.6 %shard_map.37 = bf16[1,192,64]{2,1,0:T(8,128)(2,1)} custom-call(f32[1,96,96]{2,1,0:T(8,128)} %maximum_maximum_fusion.real_ref, f32[1,96,96]{2,1,0:T(8,128)} %maximum_maximum_fusion.1.imag_ref, f32[96,64]{1,0:T(8,128)} %bitcast.57, f32[96,64]{1,0:T(8,128)} %bitcast.56), custom_call_target="tpu_custom_call" | custom-call | tf_op jit(solution)/shard_map/pallas_call | solution.py:172
  89.6 0.9 copy.69
  90.5 16.8 %all_to_all.28 = bf16[16,1,192,64]{2,3,1,0:T(8,128)(2,1)S(1)} all-to-all(bf16[16,1,192,64]{2,3,1,0:T(8,128)(2,1)S(1)} %broadcast_in_dim.5), channel_id=1, replica_groups=mesh['dop'=8,'rng'=16] {'rng'}, dimensions={0} | all-to-all | bytes 786432 | tf_op jit(solution)/shard_map/all_to_all | solution.py:54
  107.4 0.4 copy.70
  107.8 0.1 slice_negate_fusion.1
  107.9 0.2 pad_maximum_fusion.4
  108.0 0.8 fusion.17
  108.9 0.2 copy-done.2
  109.1 0.8 fusion.20
  109.9 0.4 copy-done.4
  110.3 2.9 %add_add_fusion = f32[16,128,512]{2,1,0:T(8,128)} fusion(f32[16,128,512]{2,1,0:T(8,128)S(1)} %fusion.20, f32[16,128,512]{2,1,0:T(8,128)S(1)} %fusion.17, bf16[16,512,64]{1,2,0:T(8,128)(2,1)S(1)} %copy-done.4, bf16[16,192,64]{2,1,0:T(8,128)(2,1)S(1)} %bitcast.47, bf16[16,192,64]{2,1,0:T(8,128)(2,1)S(1)} %bitcast.44), kind=kOutput, calls=%fused_computation.5 | convolution fusion | flops 136839168 | bytes 14417920 | tf_op jit(solution)/shard_map/knj,krn->kjr/dot_general | solution.py:218
  (26 shorter events, 0.3 us)
Async XLA Ops:
  0.0 1.2 %copy-start = (bf16[64,2,32,128]{3,2,1,0:T(8,128)(2,1)S(1)}, bf16[64,2,32,128]{3,2,1,0:T(8,128)(2,1)}, u32[]{:S(2)}) copy-start(bf16[64,2,32,128]{3,2,1,0:T(8,128)(2,1)} %param.3) | copy-start | bytes 3145732
  3.5 12.1 %copy-start.5 = (s32[16,512]{1,0:T(8,128)S(1)}, s32[16,512]{1,0:T(8,128)}, u32[]{:S(2)}) copy-start(s32[16,512]{1,0:T(8,128)} %param.4) | copy-start | bytes 98308
  10.9 18.7 %all-to-all-start = ((bf16[8,2,32768]{2,1,0:T(2,128)(2,1)}), bf16[8,2,32768]{2,1,0:T(2,128)(2,1)}, u32[]{:S(2)}, u32[]{:S(2)}) async-start(bf16[8,2,32768]{2,1,0:T(2,128)(2,1)} %reshape.121), calls=%async_computation | async-start | bytes 2097152 | tf_op jit(solution)/shard_map/all_to_all | solution.py:206
  32.8 7.9 %collective-permute-start = (bf16[1,512,64]{1,2,0:T(8,128)(2,1)S(1)}, bf16[1,512,64]{1,2,0:T(8,128)(2,1)S(1)}, u32[]{:S(2)}, u32[]{:S(2)}) collective-permute-start(bf16[1,512,64]{1,2,0:T(8,128)(2,1)S(1)} %copy.74), channel_id=1, source_target_pairs={{0,16},{16,32},{32,48},{48,64},{64,80},{80,96},{96,112},{112,0},{1... | collective-permute-start | bytes 196616 | tf_op jit(solution)/shard_map/ppermute | solution.py:26
  39.0 3.6 %collective-permute-start.1 = (bf16[1,512,64]{1,2,0:T(8,128)(2,1)S(1)}, bf16[1,512,64]{1,2,0:T(8,128)(2,1)S(1)}, u32[]{:S(2)}, u32[]{:S(2)}) collective-permute-start(bf16[1,512,64]{1,2,0:T(8,128)(2,1)S(1)} %copy.75), channel_id=1, source_target_pairs={{16,0},{32,16},{48,32},{64,48},{80,64},{96,80},{112,96},{0,112},{1... | collective-permute-start | bytes 196616 | tf_op jit(solution)/shard_map/ppermute | solution.py:29
  42.9 2.9 %copy-start.1 = (bf16[16,512,64]{1,2,0:T(8,128)(2,1)}, bf16[16,512,64]{1,2,0:T(8,128)(2,1)S(1)}, u32[]{:S(2)}) copy-start(bf16[16,512,64]{1,2,0:T(8,128)(2,1)S(1)} %get-tuple-element.17) | copy-start | bytes 3145732
  42.9 2.9 %copy-start.3 = (bf16[16,512,64]{1,2,0:T(8,128)(2,1)}, bf16[16,512,64]{1,2,0:T(8,128)(2,1)S(1)}, u32[]{:S(2)}) copy-start(bf16[16,512,64]{1,2,0:T(8,128)(2,1)S(1)} %get-tuple-element.15) | copy-start | bytes 3145732
  49.3 9.8 %copy-start.6 = (s32[64]{0:T(128)S(1)}, s32[64]{0:T(128)}, u32[]{:S(2)}) copy-start(s32[64]{0:T(128)} %param.5) | copy-start | bytes 772
  51.2 21.6 %all-to-all-start.1 = ((f32[16,1,32,384]{3,2,1,0:T(8,128)}), f32[16,1,32,384]{3,2,1,0:T(8,128)S(1)}, u32[]{:S(2)}, u32[]{:S(2)}) async-start(f32[16,1,32,384]{3,2,1,0:T(8,128)} %maximum_bitcast_fusion), calls=%async_computation.1 | async-start | bytes 1572864 | tf_op jit(solution)/shard_map/all_to_all | solution.py:42
  107.8 1.2 %copy-start.2 = (bf16[16,512,64]{1,2,0:T(8,128)(2,1)S(1)}, bf16[16,512,64]{1,2,0:T(8,128)(2,1)}, u32[]{:S(2)}) copy-start(bf16[16,512,64]{1,2,0:T(8,128)(2,1)} %copy-done.1) | copy-start | bytes 3145732
  109.1 1.2 %copy-start.4 = (bf16[16,512,64]{1,2,0:T(8,128)(2,1)S(1)}, bf16[16,512,64]{1,2,0:T(8,128)(2,1)}, u32[]{:S(2)}) copy-start(bf16[16,512,64]{1,2,0:T(8,128)(2,1)} %copy-done.3) | copy-start | bytes 3145732

commit v9 on v8

--- a/solution.py
+++ b/solution.py
@@ -102,17 +102,8 @@
     both = jnp.concatenate([snap, turned_snap], axis=1)
     weighting = jnp.concatenate([mask_rows, mask_rows], axis=1)[:, :, None]
     masked = both * weighting
-    pieces = []
-    for left_pos in range(3):
-        pieces.append(
-            jnp.einsum(
-                "krn,krm->knm",
-                masked[:, :, left_pos * 2 * CH : left_pos * 2 * CH + CH],
-                both[:, :, left_pos * 2 * CH :],
-                preferred_element_type=jnp.float32,
-            )
-        )
-    return jnp.concatenate(pieces, axis=-1)
+    leading = masked.reshape(*masked.shape[:2], 3, 2, CH)[:, :, :, 0].reshape(*masked.shape[:2], 3 * CH)
+    return jnp.einsum("krn,krm->knm", leading, both, preferred_element_type=jnp.float32)
 
 
 def eliminate(real_ref, imag_ref, steer_re_ref, steer_im_ref, unit_ref, wr_ref, wi_ref):
@@ -179,26 +170,10 @@
     )(same, cross, steer_re, steer_im)
 
 
-def hermitian_parts(upper):
-    def piece(left_pos, right_pos):
-        start = block_pairs.index((left_pos, right_pos)) * 2 * CH
-        return upper[:, :, start : start + 2 * CH]
-
-    def real_block(left_pos, right_pos):
-        if left_pos > right_pos:
-            return jnp.swapaxes(real_block(right_pos, left_pos), 1, 2)
-        return piece(left_pos, right_pos)[..., :CH]
-
-    def imag_block(left_pos, right_pos):
-        if left_pos > right_pos:
-            return -jnp.swapaxes(imag_block(right_pos, left_pos), 1, 2)
-        return -piece(left_pos, right_pos)[..., CH:]
-
-    def assemble(block):
-        rows = [jnp.concatenate([block(b, c) for c in range(3)], -1) for b in range(3)]
-        return jnp.concatenate(rows, 1)
-
-    return assemble(real_block), assemble(imag_block)
+def hermitian_parts(rows):
+    split = rows.reshape(rows.shape[0], rows.shape[1], 3, 2, CH)
+    size = rows.shape[1]
+    return split[:, :, :, 0].reshape(-1, size, size), -split[:, :, :, 1].reshape(-1, size, size)
 
 
 def body(echoes, training, look_index):

time: 114 us -> 128 us (1.12)
  the two profiles are of different devices: /device:TPU:24 before, /device:TPU:16 now
where the time goes in v9:
time: 128 us; the launch traced here: 127 us
  waiting for transfers between devices  38.7 us (30%)
  local copies, waits for them, and re-layouts  26.6 us (21%)
  blocking collectives  16.7 us (13%)
  Pallas kernels  14.6 us (11%)
  starting transfers between devices  14.3 us (11%)
  matrix products  8.81 us (7%)
  other arithmetic  7.31 us (6%)
    all_to_all x1, waiting for transfers between devices, sum_at_owner(): lax.all_to_all(blocks, axis, split_axis=0, concat_axis=0, tiled=True)  23.9 us
    all_to_all x1, blocking collectives, copy_for_each(): lax.all_to_all(jnp.broadcast_to(array[None], (count, *array.shape)), axis...  16.7 us
    pallas_call x1, Pallas kernels, unit_vectors(): pl.pallas_call(eliminate, grid=(count,), in_specs=[matrix, matrix, vector...  14.6 us
    all_to_all x1, waiting for transfers between devices, body(): lax.all_to_all(spectra, 'dop', split_axis=0, concat_axis=1, tiled=True)  12.9 us
    unnamed x23, local copies, waits for them, and re-layouts  10.6 us
    all_to_all x1, starting transfers between devices, sum_at_owner(): lax.all_to_all(blocks, axis, split_axis=0, concat_axis=0, tiled=True)  8.05 us
    all_to_all x2, local copies, waits for them, and re-layouts, body(): lax.all_to_all(spectra, 'dop', split_axis=0, concat_axis=1, tiled=True)  5.29 us
    all_to_all x1, starting transfers between devices, body(): lax.all_to_all(spectra, 'dop', split_axis=0, concat_axis=1, tiled=True)  4.8 us
  transfers between devices with their start and end apart: 4, of which 3 were waited for; matrix products, arithmetic and copies ran while one was open for 5% of the time, Pallas kernels for 0%

profile of v9, /device:TPU:16, one launch (start us, length us, event | category | flops | bytes accessed | tf_op | source)
XLA Modules:
  0.0 127.4 jit_solution(535404543069096472)
XLA Ops:
  0.0 0.3 sine_convert_fusion
  0.3 0.9 copy-done
  1.2 0.9 fusion.20
  2.1 0.3 fusion.19
  2.4 1.1 pad_maximum_fusion.7
  3.5 4.7 %copy.45 = bf16[128,64,64]{2,1,0:T(8,128)(2,1)S(1)} copy(bf16[128,64,64]{0,1,2:T(8,128)(2,1)} %bitcast.56) | data formatting | bytes 2097152 | tf_op jit(solution)/shard_map/convert_element_type | solution.py:79
  8.2 2.7 %reshape.146 = bf16[8,2,32768]{2,1,0:T(2,128)(2,1)} reshape(bf16[128,64,64]{2,1,0:T(8,128)(2,1)S(1)} %copy.45) | data formatting | bytes 2097152
  10.9 4.8 %all-to-all-start = ((bf16[8,2,32768]{2,1,0:T(2,128)(2,1)}), bf16[8,2,32768]{2,1,0:T(2,128)(2,1)}, u32[]{:S(2)}, u32[]{:S(2)}) async-start(bf16[8,2,32768]{2,1,0:T(2,128)(2,1)} %reshape.146), calls=%async_computation | async-start | bytes 2097152 | tf_op jit(solution)/shard_map/all_to_all | solution.py:181
  15.7 12.9 %all-to-all-done = bf16[8,2,32768]{2,1,0:T(2,128)(2,1)} async-done(((bf16[8,2,32768]{2,1,0:T(2,128)(2,1)}), bf16[8,2,32768]{2,1,0:T(2,128)(2,1)}, u32[]{:S(2)}, u32[]{:S(2)}) %all-to-all-start) | async-done | bytes 1048608 | tf_op jit(solution)/shard_map/all_to_all | solution.py:181
  28.6 3.1 %reshape.147 = bf16[128,64,64]{2,1,0:T(8,128)(2,1)S(1)} reshape(bf16[8,2,32768]{2,1,0:T(2,128)(2,1)} %all-to-all-done) | data formatting | bytes 2097152
  31.7 0.0 copy-start.1
  31.7 0.1 copy.61
  31.9 0.0 collective-permute-start
  31.9 1.2 copy-done.1
  33.0 3.2 %copy.47 = bf16[16,8,64,64]{2,1,3,0:T(8,128)(2,1)S(1)} copy(bf16[16,8,64,64]{3,2,0,1:T(8,128)(2,1)} %bitcast.53) | data formatting | bytes 2097152 | tf_op jit(solution)/shard_map/all_to_all | solution.py:181
  36.3 2.0 %all_to_all.22 = bf16[16,512,64]{1,2,0:T(8,128)(2,1)} reshape(bf16[16,8,64,64]{2,1,3,0:T(8,128)(2,1)S(1)} %copy.47) | data formatting | bytes 2097152 | tf_op jit(solution)/shard_map/all_to_all | solution.py:181
  38.3 2.0 %concatenate.48 = bf16[16,512,1,2,32]{1,4,3,0,2:T(8,128)(2,1)} reshape(bf16[16,8,64,64]{2,1,3,0:T(8,128)(2,1)S(1)} %copy.47) | data formatting | bytes 2097152 | tf_op jit(solution)/shard_map/concatenate | solution.py:100
  40.4 0.1 copy.62
  40.5 1.4 %collective-permute-start.1 = (bf16[1,512,64]{1,2,0:T(8,128)(2,1)S(1)}, bf16[1,512,64]{1,2,0:T(8,128)(2,1)S(1)}, u32[]{:S(2)}, u32[]{:S(2)}) collective-permute-start(bf16[1,512,64]{1,2,0:T(8,128)(2,1)S(1)} %copy.62), channel_id=1, source_target_pairs={{16,0},{32,16},{48,32},{64,48},{80,64},{96,80},{112,96},{0,112},{1... | collective-permute-start | bytes 196616 | tf_op jit(solution)/shard_map/ppermute | solution.py:29
  41.9 1.9 %collective-permute-done.1 = bf16[1,512,64]{1,2,0:T(8,128)(2,1)S(1)} collective-permute-done((bf16[1,512,64]{1,2,0:T(8,128)(2,1)S(1)}, bf16[1,512,64]{1,2,0:T(8,128)(2,1)S(1)}, u32[]{:S(2)}, u32[]{:S(2)}) %collective-permute-start.1) | collective-permute-done | bytes 65568 | tf_op jit(solution)/shard_map/ppermute | solution.py:29
  43.8 2.2 %pad_maximum_fusion.5 = (bf16[16,512,64]{1,2,0:T(8,128)(2,1)S(1)}, bf16[18,512,64]{1,2,0:T(8,128)(2,1)S(1)}, bf16[16,512,64]{1,2,0:T(8,128)(2,1)S(1)}) fusion(bf16[1,512,64]{1,2,0:T(8,128)(2,1)S(1)} %collective-permute-done.1, bf16[16,512,64]{1,2,0:T(8,128)(2,1)} %all_to_all.22, bf16[18,512,64]{1,2,0:T(8,128)(2,1)S(1)} %constant_dynamic-update-slice_fusion.2, ...), kind=kLoop, calls=%fused_computation.27 | loop fusion | flops 4194304 | bytes 4325376 | tf_op jit(solution)/shard_map/concatenate | solution.py:30
  46.0 0.1 slice_negate_fusion
  46.1 0.4 fusion.17
  46.5 0.3 pad_maximum_fusion.3
  46.8 1.1 copy-done.7
  47.9 0.7 fusion.12
  48.7 0.4 copy.51
  49.1 0.8 copy-done.2
  49.9 3.4 %fusion.13 = f32[16,1,96,192]{3,2,1,0:T(8,128)} fusion(bf16[16,1024,96]{1,2,0:T(8,128)(2,1)S(1)} %bitcast.57, bf16[16,512,64]{1,2,0:T(8,128)(2,1)S(1)} %get-tuple-element.10, bf16[16,512,64]{1,2,0:T(8,128)(2,1)S(1)} %get-tuple-element.11, bf16[16,512,64]{1,2,0:T(8,128)(2,1)S(1)} %get-tuple-element.9, bf16[16,512,64]{1,2,0:T(8,128)(2,1)S(1)} %get-tuple-element.14, ...), kind=kOutput, calls=%fused_computation.19 | convolution fusion | flops 641728512 | bytes 10616832 | tf_op jit(solution)/shard_map/krn,krm->knm/dot_general | solution.py:106
  53.3 8.0 %all-to-all-start.1 = ((f32[16,1,96,192]{3,2,1,0:T(8,128)}), f32[16,1,96,192]{3,2,1,0:T(8,128)}, u32[]{:S(2)}, u32[]{:S(2)}) async-start(f32[16,1,96,192]{3,2,1,0:T(8,128)} %fusion.13), calls=%async_computation.1 | async-start | bytes 3145728 | tf_op jit(solution)/shard_map/all_to_all | solution.py:42
  61.4 0.1 multiply_cosine_fusion
  61.6 0.6 fusion.44
  62.2 23.9 %all-to-all-done.1 = f32[16,1,96,192]{3,2,1,0:T(8,128)} async-done(((f32[16,1,96,192]{3,2,1,0:T(8,128)}), f32[16,1,96,192]{3,2,1,0:T(8,128)}, u32[]{:S(2)}, u32[]{:S(2)}) %all-to-all-start.1) | async-done | bytes 1179680 | tf_op jit(solution)/shard_map/all_to_all | solution.py:42
  86.1 1.5 %bitcast_reduce_fusion = f32[96,192]{1,0:T(8,128)S(1)} fusion(f32[16,1,96,192]{3,2,1,0:T(8,128)} %all-to-all-done.1), kind=kLoop, calls=%fused_computation.18 | loop fusion | flops 276480 | bytes 1253376 | tf_op jit(solution)/shard_map/reduce_sum | solution.py:43
  87.6 0.1 copy.54
  87.8 0.7 copy.55.real_ref
  88.5 0.7 copy.56.imag_ref
  89.2 14.6 %shard_map.37 = bf16[1,192,64]{2,1,0:T(8,128)(2,1)} custom-call(f32[1,96,96]{2,1,0:T(8,128)} %copy.55.real_ref, f32[1,96,96]{2,1,0:T(8,128)} %copy.56.imag_ref, f32[96,64]{1,0:T(8,128)} %bitcast.66, f32[96,64]{1,0:T(8,128)} %bitcast.65), custom_call_target="tpu_custom_call" | custom-call | tf_op jit(solution)/shard_map/pallas_call | solution.py:163
  103.8 0.9 copy.57
  104.8 16.7 %all_to_all.28 = bf16[16,1,192,64]{2,3,1,0:T(8,128)(2,1)S(1)} all-to-all(bf16[16,1,192,64]{2,3,1,0:T(8,128)(2,1)S(1)} %broadcast_in_dim.5), channel_id=1, replica_groups=mesh['dop'=8,'rng'=16] {'rng'}, dimensions={0} | all-to-all | bytes 786432 | tf_op jit(solution)/shard_map/all_to_all | solution.py:54
  121.5 0.4 copy.58
  121.9 0.1 slice_negate_fusion.1
  121.9 0.2 pad_maximum_fusion.8
  122.1 0.8 fusion.23
  123.0 0.4 copy-done.4
  123.3 0.8 fusion.26
  124.2 0.4 copy-done.6
  124.6 2.9 %add_add_fusion = f32[16,128,512]{2,1,0:T(8,128)} fusion(f32[16,128,512]{2,1,0:T(8,128)S(1)} %fusion.26, f32[16,128,512]{2,1,0:T(8,128)S(1)} %fusion.23, bf16[16,512,64]{1,2,0:T(8,128)(2,1)S(1)} %copy-done.6, bf16[16,192,64]{2,1,0:T(8,128)(2,1)S(1)} %bitcast.51, bf16[16,192,64]{2,1,0:T(8,128)(2,1)S(1)} %bitcast.47), kind=kOutput, calls=%fused_computation.12 | convolution fusion | flops 136839168 | bytes 14417920 | tf_op jit(solution)/shard_map/knj,krn->kjr/dot_general | solution.py:193
  (25 shorter events, 0.2 us)
Async XLA Ops:
  0.0 1.2 copy-start
  8.2 7.5 %copy-start.8 = (s32[16,512]{1,0:T(8,128)S(1)}, s32[16,512]{1,0:T(8,128)}, u32[]{:S(2)}) copy-start(s32[16,512]{1,0:T(8,128)} %param.4) | copy-start | bytes 98308
  10.9 17.7 %all-to-all-start = ((bf16[8,2,32768]{2,1,0:T(2,128)(2,1)}), bf16[8,2,32768]{2,1,0:T(2,128)(2,1)}, u32[]{:S(2)}, u32[]{:S(2)}) async-start(bf16[8,2,32768]{2,1,0:T(2,128)(2,1)} %reshape.146), calls=%async_computation | async-start | bytes 2097152 | tf_op jit(solution)/shard_map/all_to_all | solution.py:181
  31.7 1.3 %copy-start.1 = (bf16[128,64,64]{2,1,0:T(8,128)(2,1)}, bf16[128,64,64]{2,1,0:T(8,128)(2,1)S(1)}, u32[]{:S(2)}) copy-start(bf16[128,64,64]{2,1,0:T(8,128)(2,1)S(1)} %reshape.147) | copy-start | bytes 3145732
  31.9 10.0 %collective-permute-start = (bf16[1,512,64]{1,2,0:T(8,128)(2,1)S(1)}, bf16[1,512,64]{1,2,0:T(8,128)(2,1)S(1)}, u32[]{:S(2)}, u32[]{:S(2)}) collective-permute-start(bf16[1,512,64]{1,2,0:T(8,128)(2,1)S(1)} %copy.61), channel_id=1, source_target_pairs={{0,16},{16,32},{32,48},{48,64},{64,80},{80,96},{96,112},{112,0},{1... | collective-permute-start | bytes 196616 | tf_op jit(solution)/shard_map/ppermute | solution.py:26
  40.5 3.3 %collective-permute-start.1 = (bf16[1,512,64]{1,2,0:T(8,128)(2,1)S(1)}, bf16[1,512,64]{1,2,0:T(8,128)(2,1)S(1)}, u32[]{:S(2)}, u32[]{:S(2)}) collective-permute-start(bf16[1,512,64]{1,2,0:T(8,128)(2,1)S(1)} %copy.62), channel_id=1, source_target_pairs={{16,0},{32,16},{48,32},{64,48},{80,64},{96,80},{112,96},{0,112},{1... | collective-permute-start | bytes 196616 | tf_op jit(solution)/shard_map/ppermute | solution.py:29
  46.0 3.1 %copy-start.3 = (bf16[16,512,64]{1,2,0:T(8,128)(2,1)}, bf16[16,512,64]{1,2,0:T(8,128)(2,1)S(1)}, u32[]{:S(2)}) copy-start(bf16[16,512,64]{1,2,0:T(8,128)(2,1)S(1)} %get-tuple-element.16) | copy-start | bytes 3145732
  46.0 3.1 %copy-start.5 = (bf16[16,512,64]{1,2,0:T(8,128)(2,1)}, bf16[16,512,64]{1,2,0:T(8,128)(2,1)S(1)}, u32[]{:S(2)}) copy-start(bf16[16,512,64]{1,2,0:T(8,128)(2,1)S(1)} %get-tuple-element.14) | copy-start | bytes 3145732
  46.5 1.5 %copy-start.7 = (bf16[16,512,1,2,32]{1,4,3,0,2:T(8,128)(2,1)S(1)}, bf16[16,512,1,2,32]{1,4,3,0,2:T(8,128)(2,1)}, u32[]{:S(2)}) copy-start(bf16[16,512,1,2,32]{1,4,3,0,2:T(8,128)(2,1)} %concatenate.48) | copy-start | bytes 3145732
  48.7 1.2 copy-start.2
  53.3 8.1 %copy-start.9 = (s32[64]{0:T(128)S(1)}, s32[64]{0:T(128)}, u32[]{:S(2)}) copy-start(s32[64]{0:T(128)} %param.5) | copy-start | bytes 772
  53.3 32.8 %all-to-all-start.1 = ((f32[16,1,96,192]{3,2,1,0:T(8,128)}), f32[16,1,96,192]{3,2,1,0:T(8,128)}, u32[]{:S(2)}, u32[]{:S(2)}) async-start(f32[16,1,96,192]{3,2,1,0:T(8,128)} %fusion.13), calls=%async_computation.1 | async-start | bytes 3145728 | tf_op jit(solution)/shard_map/all_to_all | solution.py:42
  122.1 1.2 copy-start.4
  123.3 1.2 copy-start.6

commit v10 on v8

--- a/solution.py
+++ b/solution.py
@@ -102,16 +102,18 @@
     both = jnp.concatenate([snap, turned_snap], axis=1)
     weighting = jnp.concatenate([mask_rows, mask_rows], axis=1)[:, :, None]
     masked = both * weighting
+    below = lax.broadcasted_iota(jnp.int32, (CH, CH), 0) > lax.broadcasted_iota(jnp.int32, (CH, CH), 1)
     pieces = []
     for left_pos in range(3):
-        pieces.append(
-            jnp.einsum(
-                "krn,krm->knm",
-                masked[:, :, left_pos * 2 * CH : left_pos * 2 * CH + CH],
-                both[:, :, left_pos * 2 * CH :],
-                preferred_element_type=jnp.float32,
-            )
+        start = left_pos * 2 * CH
+        piece = jnp.einsum(
+            "krn,krm->knm",
+            masked[:, :, start : start + CH],
+            both[:, :, start:],
+            preferred_element_type=jnp.float32,
         )
+        folded = jnp.where(below, piece[..., CH : 2 * CH], piece[..., :CH])
+        pieces.extend([folded, piece[..., 2 * CH :]])
     return jnp.concatenate(pieces, axis=-1)
 
 
@@ -180,19 +182,33 @@
 
 
 def hermitian_parts(upper):
-    def piece(left_pos, right_pos):
-        start = block_pairs.index((left_pos, right_pos)) * 2 * CH
-        return upper[:, :, start : start + 2 * CH]
+    below = lax.broadcasted_iota(jnp.int32, (CH, CH), 0) > lax.broadcasted_iota(jnp.int32, (CH, CH), 1)
+    starts = {}
+    offset = 0
+    for left_pos in range(3):
+        starts[left_pos] = offset
+        offset += CH + (2 - left_pos) * 2 * CH
 
     def real_block(left_pos, right_pos):
         if left_pos > right_pos:
             return jnp.swapaxes(real_block(right_pos, left_pos), 1, 2)
-        return piece(left_pos, right_pos)[..., :CH]
+        start = starts[left_pos]
+        if left_pos == right_pos:
+            folded = upper[:, :, start : start + CH]
+            return jnp.where(below, jnp.swapaxes(folded, 1, 2), folded)
+        start += CH + (right_pos - left_pos - 1) * 2 * CH
+        return upper[:, :, start : start + CH]
 
     def imag_block(left_pos, right_pos):
         if left_pos > right_pos:
             return -jnp.swapaxes(imag_block(right_pos, left_pos), 1, 2)
-        return -piece(left_pos, right_pos)[..., CH:]
+        start = starts[left_pos]
+        if left_pos == right_pos:
+            folded = upper[:, :, start : start + CH]
+            above = jnp.swapaxes(below, 0, 1)
+            return jnp.where(below, -folded, jnp.where(above, jnp.swapaxes(folded, 1, 2), 0.0))
+        start += CH + (right_pos - left_pos - 1) * 2 * CH
+        return -upper[:, :, start + CH : start + 2 * CH]
 
     def assemble(block):
         rows = [jnp.concatenate([block(b, c) for c in range(3)], -1) for b in range(3)]

time: 114 us -> 118 us (1.035)
  local copies, waits for them, and re-layouts: 20.7 us -> 25 us
    concatenate x0 -> x1, local copies, waits for them, and re-layouts: none -> 2.32 us  [upper_blocks(): return jnp.concatenate(pieces, axis=-1)]
    slice x0 -> x4, local copies, waits for them, and re-layouts: none -> 1.85 us  [the longest x2 1.7 us: upper_blocks(): pieces.extend([folded, piece[..., 2 * CH:]])]
    reshape x1 -> x0, other arithmetic: 1.2 us -> none  [split_up(): array.reshape(*dims[:dim], count, dims[dim] // count, *dims[dim + 1:])]
    unnamed x20 -> x19, local copies, waits for them, and re-layouts: 7.53 us -> 7.46 us
where the time goes in v10:
time: 118 us; the launch traced here: 117 us
  waiting for transfers between devices  28.7 us (24%)
  local copies, waits for them, and re-layouts  25 us (21%)
  blocking collectives  16.8 us (14%)
  Pallas kernels  14.6 us (12%)
  starting transfers between devices  14.3 us (12%)
  matrix products  9.66 us (8%)
  other arithmetic  7.69 us (7%)
    all_to_all x1, blocking collectives, copy_for_each(): lax.all_to_all(jnp.broadcast_to(array[None], (count, *array.shape)), axis...  16.8 us
    pallas_call x1, Pallas kernels, unit_vectors(): pl.pallas_call(eliminate, grid=(count,), in_specs=[matrix, matrix, vector...  14.6 us
    all_to_all x1, waiting for transfers between devices, body(): lax.all_to_all(spectra, 'dop', split_axis=0, concat_axis=1, tiled=True)  13.9 us
    all_to_all x1, waiting for transfers between devices, sum_at_owner(): lax.all_to_all(blocks, axis, split_axis=0, concat_axis=0, tiled=True)  12.9 us
    all_to_all x1, starting transfers between devices, sum_at_owner(): lax.all_to_all(blocks, axis, split_axis=0, concat_axis=0, tiled=True)  7.87 us
    unnamed x19, local copies, waits for them, and re-layouts  7.46 us
    all_to_all x2, local copies, waits for them, and re-layouts, body(): lax.all_to_all(spectra, 'dop', split_axis=0, concat_axis=1, tiled=True)  6.02 us
    convert_element_type x1, local copies, waits for them, and re-layouts, doppler_spectra(): return jnp.stack([real_part, imag_part], axis=2).reshape(PULSES, echo_row...  4.72 us
  transfers between devices with their start and end apart: 4, of which 3 were waited for; matrix products, arithmetic and copies ran while one was open for 3% of the time, Pallas kernels for 0%

profile of v10, /device:TPU:24, one launch (start us, length us, event | category | flops | bytes accessed | tf_op | source)
XLA Modules:
  0.0 117.1 jit_solution(3780448665601751455)
XLA Ops:
  0.0 0.3 sine_convert_fusion
  0.3 0.9 copy-done
  1.2 0.9 fusion.14
  2.1 0.3 fusion.13
  2.4 1.1 pad_maximum_fusion.3
  3.5 4.7 %copy.64 = bf16[128,64,64]{2,1,0:T(8,128)(2,1)S(1)} copy(bf16[128,64,64]{0,1,2:T(8,128)(2,1)} %bitcast.59) | data formatting | bytes 2097152 | tf_op jit(solution)/shard_map/convert_element_type | solution.py:79
  8.2 2.7 %reshape.143 = bf16[8,2,32768]{2,1,0:T(2,128)(2,1)} reshape(bf16[128,64,64]{2,1,0:T(8,128)(2,1)S(1)} %copy.64) | data formatting | bytes 2097152
  10.9 4.7 %all-to-all-start = ((bf16[8,2,32768]{2,1,0:T(2,128)(2,1)}), bf16[8,2,32768]{2,1,0:T(2,128)(2,1)}, u32[]{:S(2)}, u32[]{:S(2)}) async-start(bf16[8,2,32768]{2,1,0:T(2,128)(2,1)} %reshape.143), calls=%async_computation | async-start | bytes 2097152 | tf_op jit(solution)/shard_map/all_to_all | solution.py:222
  15.6 13.9 %all-to-all-done = bf16[8,2,32768]{2,1,0:T(2,128)(2,1)} async-done(((bf16[8,2,32768]{2,1,0:T(2,128)(2,1)}), bf16[8,2,32768]{2,1,0:T(2,128)(2,1)}, u32[]{:S(2)}, u32[]{:S(2)}) %all-to-all-start) | async-done | bytes 1048608 | tf_op jit(solution)/shard_map/all_to_all | solution.py:222
  29.6 3.1 %reshape.144 = bf16[128,64,64]{2,1,0:T(8,128)(2,1)S(1)} reshape(bf16[8,2,32768]{2,1,0:T(2,128)(2,1)} %all-to-all-done) | data formatting | bytes 2097152
  32.7 0.1 copy.88
  32.8 2.8 %copy.66 = bf16[16,8,64,64]{2,1,3,0:T(8,128)(2,1)} copy(bf16[16,8,64,64]{3,2,0,1:T(8,128)(2,1)S(1)} %bitcast.58) | data formatting | bytes 2097152 | tf_op jit(solution)/shard_map/all_to_all | solution.py:222
  35.7 3.2 %all_to_all.22 = bf16[16,512,64]{1,2,0:T(8,128)(2,1)S(1)} reshape(bf16[16,8,64,64]{2,1,3,0:T(8,128)(2,1)} %copy.66) | data formatting | bytes 2097152 | tf_op jit(solution)/shard_map/all_to_all | solution.py:222
  38.9 0.1 copy.89
  39.0 1.7 %collective-permute-start.1 = (bf16[1,512,64]{1,2,0:T(8,128)(2,1)S(1)}, bf16[1,512,64]{1,2,0:T(8,128)(2,1)S(1)}, u32[]{:S(2)}, u32[]{:S(2)}) collective-permute-start(bf16[1,512,64]{1,2,0:T(8,128)(2,1)S(1)} %copy.89), channel_id=1, source_target_pairs={{16,0},{32,16},{48,32},{64,48},{80,64},{96,80},{112,96},{0,112},{1... | collective-permute-start | bytes 196616 | tf_op jit(solution)/shard_map/ppermute | solution.py:29
  40.7 1.9 %collective-permute-done.1 = bf16[1,512,64]{1,2,0:T(8,128)(2,1)S(1)} collective-permute-done((bf16[1,512,64]{1,2,0:T(8,128)(2,1)S(1)}, bf16[1,512,64]{1,2,0:T(8,128)(2,1)S(1)}, u32[]{:S(2)}, u32[]{:S(2)}) %collective-permute-start.1) | collective-permute-done | bytes 65568 | tf_op jit(solution)/shard_map/ppermute | solution.py:29
  42.6 0.3 pad_maximum_fusion.1
  42.9 0.1 slice_negate_fusion
  43.0 0.3 fusion.7
  43.3 2.4 %broadcast_multiply_fusion = (bf16[16,1024,192]{1,2,0:T(8,128)(2,1)S(1)}, bf16[16,1024,192]{1,2,0:T(8,128)(2,1)S(1)}) fusion(bf16[16,1024]{1,0:T(8,128)(2,1)S(1)} %pad_maximum_fusion.10, bf16[18,512,32]{1,2,0:T(8,128)(2,1)S(1)} %get-tuple-element.14, bf16[18,512,32]{1,2,0:T(8,128)(2,1)S(1)} %get-tuple-element.13, ...), kind=kLoop, calls=%fused_computation.6 | loop fusion | flops 53477376 | bytes 19038208 | tf_op jit(solution)/shard_map/mul | solution.py:104
  45.8 2.0 %fusion.10 = f32[16,32,192]{2,1,0:T(8,128)S(1)} fusion(bf16[16,1024,192]{1,2,0:T(8,128)(2,1)S(1)} %get-tuple-element.6, bf16[16,1024,192]{1,2,0:T(8,128)(2,1)S(1)} %get-tuple-element.5), kind=kOutput, calls=%fused_computation.17 | convolution fusion | flops 201326592 | bytes 7733248 | tf_op jit(solution)/shard_map/krn,krm->knm/dot_general | solution.py:109
  47.8 1.5 %fusion.2 = f32[16,32,128]{2,1,0:T(8,128)S(1)} fusion(bf16[16,1024,192]{1,2,0:T(8,128)(2,1)S(1)} %get-tuple-element.6, bf16[16,1024,192]{1,2,0:T(8,128)(2,1)S(1)} %get-tuple-element.5), kind=kOutput, calls=%fused_computation.3 | convolution fusion | flops 134217728 | bytes 5505024 | tf_op jit(solution)/shard_map/krn,krm->knm/dot_general | solution.py:109
  49.3 0.7 fusion.4
  50.0 0.9 slice.210
  50.9 0.8 slice.215
  51.7 0.9 slice_select_fusion
  52.6 2.3 %concatenate.67 = f32[16,32,288]{2,1,0:T(8,128)} concatenate(f32[16,32,32]{2,1,0:T(8,128)} %get-tuple-element.47, f32[16,32,128]{2,1,0:T(8,128)} %slice.210, f32[16,32,32]{2,1,0:T(8,128)S(1)} %get-tuple-element.46, f32[16,32,64]{2,1,0:T(8,128)} %slice.215, f32[16,32,32]{2,1,0:T(8,128)S(1)} %get-tuple-element.45), dimensions={2} | concatenate | bytes 1179648 | tf_op jit(solution)/shard_map/concatenate | solution.py:117
  55.0 7.9 %all-to-all-start.1 = ((f32[16,1,32,288]{3,2,1,0:T(8,128)}), f32[16,1,32,288]{3,2,1,0:T(8,128)S(1)}, u32[]{:S(2)}, u32[]{:S(2)}) async-start(f32[16,1,32,288]{3,2,1,0:T(8,128)} %bitcast.60), calls=%async_computation.1 | async-start | bytes 1572864 | tf_op jit(solution)/shard_map/all_to_all | solution.py:42
  62.8 0.1 multiply_cosine_fusion
  63.0 0.6 fusion.41
  63.7 12.9 %all-to-all-done.1 = f32[16,1,32,288]{3,2,1,0:T(8,128)S(1)} async-done(((f32[16,1,32,288]{3,2,1,0:T(8,128)}), f32[16,1,32,288]{3,2,1,0:T(8,128)S(1)}, u32[]{:S(2)}, u32[]{:S(2)}) %all-to-all-start.1) | async-done | bytes 589856 | tf_op jit(solution)/shard_map/all_to_all | solution.py:42
  76.6 0.1 fusion.42
  76.7 0.1 copy.70
  76.9 0.1 fusion.32
  77.0 0.1 copy.79
  77.5 0.7 maximum_maximum_fusion.real_ref
  78.2 0.7 maximum_maximum_fusion.1.imag_ref
  78.9 14.6 %shard_map.37 = bf16[1,192,64]{2,1,0:T(8,128)(2,1)} custom-call(f32[1,96,96]{2,1,0:T(8,128)} %maximum_maximum_fusion.real_ref, f32[1,96,96]{2,1,0:T(8,128)} %maximum_maximum_fusion.1.imag_ref, f32[96,64]{1,0:T(8,128)} %bitcast.68, f32[96,64]{1,0:T(8,128)} %bitcast.67), custom_call_target="tpu_custom_call" | custom-call | tf_op jit(solution)/shard_map/pallas_call | solution.py:174
  93.6 0.9 copy.83
  94.5 16.8 %all_to_all.28 = bf16[16,1,192,64]{2,3,1,0:T(8,128)(2,1)S(1)} all-to-all(bf16[16,1,192,64]{2,3,1,0:T(8,128)(2,1)S(1)} %broadcast_in_dim.43), channel_id=1, replica_groups=mesh['dop'=8,'rng'=16] {'rng'}, dimensions={0} | all-to-all | bytes 786432 | tf_op jit(solution)/shard_map/all_to_all | solution.py:54
  111.3 0.4 copy.84
  111.7 0.1 slice_negate_fusion.1
  111.8 0.2 pad_maximum_fusion.4
  112.0 0.8 fusion.17
  112.8 0.2 copy-done.2
  113.0 0.8 fusion.20
  113.9 0.4 copy-done.4
  114.3 2.9 %add_add_fusion = f32[16,128,512]{2,1,0:T(8,128)} fusion(f32[16,128,512]{2,1,0:T(8,128)S(1)} %fusion.20, f32[16,128,512]{2,1,0:T(8,128)S(1)} %fusion.17, bf16[16,512,64]{1,2,0:T(8,128)(2,1)S(1)} %copy-done.4, bf16[16,192,64]{2,1,0:T(8,128)(2,1)S(1)} %bitcast.56, bf16[16,192,64]{2,1,0:T(8,128)(2,1)S(1)} %bitcast.53), kind=kOutput, calls=%fused_computation.5 | convolution fusion | flops 136839168 | bytes 14417920 | tf_op jit(solution)/shard_map/knj,krn->kjr/dot_general | solution.py:234
  (32 shorter events, 0.7 us)
Async XLA Ops:
  0.0 1.2 %copy-start = (bf16[64,2,32,128]{3,2,1,0:T(8,128)(2,1)S(1)}, bf16[64,2,32,128]{3,2,1,0:T(8,128)(2,1)}, u32[]{:S(2)}) copy-start(bf16[64,2,32,128]{3,2,1,0:T(8,128)(2,1)} %param.3) | copy-start | bytes 3145732
  3.5 12.1 %copy-start.5 = (s32[16,512]{1,0:T(8,128)S(1)}, s32[16,512]{1,0:T(8,128)}, u32[]{:S(2)}) copy-start(s32[16,512]{1,0:T(8,128)} %param.4) | copy-start | bytes 98308
  3.5 12.1 %copy-start.6 = (s32[64]{0:T(128)S(1)}, s32[64]{0:T(128)}, u32[]{:S(2)}) copy-start(s32[64]{0:T(128)} %param.5) | copy-start | bytes 772
  10.9 18.7 %all-to-all-start = ((bf16[8,2,32768]{2,1,0:T(2,128)(2,1)}), bf16[8,2,32768]{2,1,0:T(2,128)(2,1)}, u32[]{:S(2)}, u32[]{:S(2)}) async-start(bf16[8,2,32768]{2,1,0:T(2,128)(2,1)} %reshape.143), calls=%async_computation | async-start | bytes 2097152 | tf_op jit(solution)/shard_map/all_to_all | solution.py:222
  32.8 7.9 %collective-permute-start = (bf16[1,512,64]{1,2,0:T(8,128)(2,1)S(1)}, bf16[1,512,64]{1,2,0:T(8,128)(2,1)S(1)}, u32[]{:S(2)}, u32[]{:S(2)}) collective-permute-start(bf16[1,512,64]{1,2,0:T(8,128)(2,1)S(1)} %copy.88), channel_id=1, source_target_pairs={{0,16},{16,32},{32,48},{48,64},{64,80},{80,96},{96,112},{112,0},{1... | collective-permute-start | bytes 196616 | tf_op jit(solution)/shard_map/ppermute | solution.py:26
  39.0 3.6 %collective-permute-start.1 = (bf16[1,512,64]{1,2,0:T(8,128)(2,1)S(1)}, bf16[1,512,64]{1,2,0:T(8,128)(2,1)S(1)}, u32[]{:S(2)}, u32[]{:S(2)}) collective-permute-start(bf16[1,512,64]{1,2,0:T(8,128)(2,1)S(1)} %copy.89), channel_id=1, source_target_pairs={{16,0},{32,16},{48,32},{64,48},{80,64},{96,80},{112,96},{0,112},{1... | collective-permute-start | bytes 196616 | tf_op jit(solution)/shard_map/ppermute | solution.py:29
  42.9 2.9 %copy-start.1 = (bf16[16,512,64]{1,2,0:T(8,128)(2,1)}, bf16[16,512,64]{1,2,0:T(8,128)(2,1)S(1)}, u32[]{:S(2)}) copy-start(bf16[16,512,64]{1,2,0:T(8,128)(2,1)S(1)} %get-tuple-element.17) | copy-start | bytes 3145732
  42.9 2.9 %copy-start.3 = (bf16[16,512,64]{1,2,0:T(8,128)(2,1)}, bf16[16,512,64]{1,2,0:T(8,128)(2,1)S(1)}, u32[]{:S(2)}) copy-start(bf16[16,512,64]{1,2,0:T(8,128)(2,1)S(1)} %get-tuple-element.15) | copy-start | bytes 3145732
  55.0 21.6 %all-to-all-start.1 = ((f32[16,1,32,288]{3,2,1,0:T(8,128)}), f32[16,1,32,288]{3,2,1,0:T(8,128)S(1)}, u32[]{:S(2)}, u32[]{:S(2)}) async-start(f32[16,1,32,288]{3,2,1,0:T(8,128)} %bitcast.60), calls=%async_computation.1 | async-start | bytes 1572864 | tf_op jit(solution)/shard_map/all_to_all | solution.py:42
  111.8 1.2 %copy-start.2 = (bf16[16,512,64]{1,2,0:T(8,128)(2,1)S(1)}, bf16[16,512,64]{1,2,0:T(8,128)(2,1)}, u32[]{:S(2)}) copy-start(bf16[16,512,64]{1,2,0:T(8,128)(2,1)} %copy-done.1) | copy-start | bytes 3145732
  113.0 1.2 %copy-start.4 = (bf16[16,512,64]{1,2,0:T(8,128)(2,1)S(1)}, bf16[16,512,64]{1,2,0:T(8,128)(2,1)}, u32[]{:S(2)}) copy-start(bf16[16,512,64]{1,2,0:T(8,128)(2,1)} %copy-done.3) | copy-start | bytes 3145732

commit v11 on v8

--- a/solution.py
+++ b/solution.py
@@ -67,18 +67,24 @@
     return jnp.concatenate([jnp.cos(angles), jnp.sin(angles)], axis=0).astype(jnp.bfloat16)
 
 
+def transform(twiddle_ref, echo_ref, out_ref):
+    rows = echo_ref.shape[0]
+    echoes = echo_ref[...]
+    swapped = jnp.stack([echoes[:, 1], -echoes[:, 0]], axis=1)
+    stacked = jnp.concatenate(
+        [echoes.reshape(rows * 2 * CH, PULSES), swapped.reshape(rows * 2 * CH, PULSES)], axis=1
+    )
+    out_ref[...] = lax.dot_general(
+        twiddle_ref[...], stacked, (((1,), (1,)), ((), ())), preferred_element_type=jnp.float32
+    ).astype(out_ref.dtype)
+
 def doppler_spectra(echo_rows, twiddle):
-    product = jnp.einsum("kp,rqcp->krqc", twiddle, echo_rows, preferred_element_type=jnp.float32)
-    cosine = product[:PULSES]
-    sine = product[PULSES:]
-    real_part = cosine[:, :, 0] + sine[:, :, 1]
-    imag_part = cosine[:, :, 1] - sine[:, :, 0]
-    return (
-        jnp.stack([real_part, imag_part], axis=2)
-        .reshape(PULSES, echo_rows.shape[0], 2 * CH)
-        .astype(jnp.bfloat16)
-    )
-
+    rows = echo_rows.shape[0]
+    paired = jnp.concatenate([twiddle[:PULSES], twiddle[PULSES:]], axis=1)
+    return pl.pallas_call(
+        transform,
+        out_shape=jax.ShapeDtypeStruct((PULSES, rows * 2 * CH), jnp.bfloat16),
+    )(paired, echo_rows)
 
 def steering(look_index):
     sines = -1.0 + (2.0 * look_index.astype(jnp.float32) + 1.0) / ANGLES
@@ -204,6 +210,7 @@
 def body(echoes, training, look_index):
     spectra = doppler_spectra(echoes, twiddles())
     turned = lax.all_to_all(spectra, "dop", split_axis=0, concat_axis=1, tiled=True)
+    turned = turned.reshape(turned.shape[0], -1, 2 * CH)
     edged = padded(turned, (("dop", 0),), 1)
     bin_count = edged.shape[0] - 2
     upper = upper_blocks(edged, training.astype(jnp.bfloat16))

time: 114 us -> 100 us (0.88)
  local copies, waits for them, and re-layouts: 20.7 us -> 7.3 us
  Pallas kernels: 14.6 us -> 17.7 us
  blocking collectives: 16.8 us -> 15.1 us
    unnamed x20 -> x13, local copies, waits for them, and re-layouts: 7.53 us -> 0.24 us
    all_to_all x2 -> x1, local copies, waits for them, and re-layouts: 6.02 us -> 0.58 us  [body(): lax.all_to_all(spectra, 'dop', split_axis=0, concat_axis=1, tiled=True)]
    convert_element_type x1 -> x0, local copies, waits for them, and re-layouts: 4.72 us -> none  [doppler_spectra(): return jnp.stack([real_part, imag_part], axis=2).reshape(PULSES, echo_row...]
    reshape x0 -> x2, local copies, waits for them, and re-layouts: none -> 3.12 us  [body(): turned = turned.reshape(turned.shape[0], -1, 2 * CH)]
    pallas_call x0 -> x1, Pallas kernels: none -> 3.05 us  [doppler_spectra(): pl.pallas_call(transform, out_shape=jax.ShapeDtypeStruct((PULSES, rows *...]
    all_to_all x1, waiting for transfers between devices: 12.9 us -> 15 us  [sum_at_owner(): lax.all_to_all(blocks, axis, split_axis=0, concat_axis=0, tiled=True)]
    ppermute x1, waiting for transfers between devices: 1.89 us -> 0.01 us  [padded(): lax.ppermute(lax.slice_in_dim(block, 0, width, axis=dim), axis, backward)]
    all_to_all x1, blocking collectives: 16.8 us -> 15.1 us  [copy_for_each(): lax.all_to_all(jnp.broadcast_to(array[None], (count, *array.shape)), axis...]
  transfers between devices with their start and end apart: 4 -> 4, of which waited for: 3 -> 2; matrix products, arithmetic and copies ran while one was open for 3% -> 6% of each run, Pallas kernels for 0% -> 0%
where the time goes in v11:
time: 100 us; the launch traced here: 99.9 us
  waiting for transfers between devices  28.1 us (28%)
  Pallas kernels  17.7 us (18%)
  blocking collectives  15.1 us (15%)
  starting transfers between devices  14.3 us (14%)
  matrix products  9.13 us (9%)
  other arithmetic  7.97 us (8%)
  local copies, waits for them, and re-layouts  7.3 us (7%)
    all_to_all x1, blocking collectives, copy_for_each(): lax.all_to_all(jnp.broadcast_to(array[None], (count, *array.shape)), axis...  15.1 us
    all_to_all x1, waiting for transfers between devices, sum_at_owner(): lax.all_to_all(blocks, axis, split_axis=0, concat_axis=0, tiled=True)  15 us
    pallas_call x1, Pallas kernels, unit_vectors(): pl.pallas_call(eliminate, grid=(count,), in_specs=[matrix, matrix, vector...  14.6 us
    all_to_all x1, waiting for transfers between devices, body(): lax.all_to_all(spectra, 'dop', split_axis=0, concat_axis=1, tiled=True)  13.1 us
    all_to_all x1, starting transfers between devices, sum_at_owner(): lax.all_to_all(blocks, axis, split_axis=0, concat_axis=0, tiled=True)  7.88 us
    dot_general x3, matrix products, body(): jnp.einsum('knj,krn->kjr', weights[:, position * 2 * CH:(position + 1) *...  4.9 us
    all_to_all x1, starting transfers between devices, body(): lax.all_to_all(spectra, 'dop', split_axis=0, concat_axis=1, tiled=True)  4.69 us
    dot_general x3, matrix products, upper_blocks(): jnp.einsum('krn,krm->knm', masked[:, :, left_pos * 2 * CH:left_pos * 2 *...  4.23 us
  transfers between devices with their start and end apart: 4, of which 2 were waited for; matrix products, arithmetic and copies ran while one was open for 6% of the time, Pallas kernels for 0%

profile of v11, /device:TPU:24, one launch (start us, length us, event | category | flops | bytes accessed | tf_op | source)
XLA Modules:
  0.0 99.9 jit_solution(5215712180736943557)
XLA Ops:
  0.0 0.3 sine_convert_fusion
  0.3 0.6 pad_maximum_fusion.10.twiddle_ref
  0.9 3.0 %shard_map.37 = bf16[128,4096]{1,0:T(8,128)(2,1)} custom-call(bf16[128,256]{1,0:T(8,128)(2,1)} %pad_maximum_fusion.10.twiddle_ref, bf16[64,2,32,128]{3,2,1,0:T(8,128)(2,1)} %echo_ref.1), custom_call_target="tpu_custom_call" | custom-call | tf_op jit(solution)/shard_map/pallas_call | solution.py:84
  4.0 4.7 %all-to-all-start = ((bf16[8,16,4096]{2,1,0:T(8,128)(2,1)}), bf16[8,16,4096]{2,1,0:T(8,128)(2,1)S(1)}, u32[]{:S(2)}, u32[]{:S(2)}) async-start(bf16[8,16,4096]{2,1,0:T(8,128)(2,1)} %bitcast.37), calls=%async_computation | async-start | bytes 2097152 | tf_op jit(solution)/shard_map/all_to_all | solution.py:212
  8.7 0.8 convert_element_type.20
  9.4 13.1 %all-to-all-done = bf16[8,16,4096]{2,1,0:T(8,128)(2,1)S(1)} async-done(((bf16[8,16,4096]{2,1,0:T(8,128)(2,1)}), bf16[8,16,4096]{2,1,0:T(8,128)(2,1)S(1)}, u32[]{:S(2)}, u32[]{:S(2)}) %all-to-all-start) | async-done | bytes 1048608 | tf_op jit(solution)/shard_map/all_to_all | solution.py:212
  22.5 0.6 slice_reduce_fusion
  23.1 0.2 slice.154
  23.3 0.1 copy.57
  23.4 0.0 collective-permute-start
  23.4 0.2 slice.157
  23.6 0.1 copy.60
  23.7 1.7 %collective-permute-start.1 = (bf16[1,512,64]{1,2,0:T(8,128)(2,1)S(1)}, bf16[1,512,64]{1,2,0:T(8,128)(2,1)S(1)}, u32[]{:S(2)}, u32[]{:S(2)}) collective-permute-start(bf16[1,512,64]{1,2,0:T(8,128)(2,1)S(1)} %copy.60), channel_id=1, source_target_pairs={{16,0},{32,16},{48,32},{64,48},{80,64},{96,80},{112,96},{0,112},{1... | collective-permute-start | bytes 196616 | tf_op jit(solution)/shard_map/ppermute | solution.py:29
  25.5 0.6 copy.58
  26.0 2.3 %reshape.121 = bf16[16,512,64]{2,1,0:T(8,128)(2,1)S(1)} reshape(bf16[16,8,4096]{2,1,0:T(8,128)(2,1)S(1)} %copy.58) | data formatting | bytes 2097152 | tf_op jit(solution)/shard_map/reshape | solution.py:213
  28.3 0.8 copy.59
  29.2 0.2 pad_maximum_fusion.1
  29.4 0.1 slice_negate_fusion
  29.4 0.3 fusion.7
  29.7 0.1 pad_maximum_fusion.2
  29.9 2.4 %broadcast_multiply_fusion = (bf16[16,1024,192]{1,2,0:T(8,128)(2,1)S(1)}, bf16[16,1024,192]{1,2,0:T(8,128)(2,1)S(1)}) fusion(bf16[16,1024]{1,0:T(8,128)(2,1)S(1)} %pad_maximum_fusion.11, bf16[18,512,32]{1,2,0:T(8,128)(2,1)S(1)} %get-tuple-element.12, bf16[18,512,32]{1,2,0:T(8,128)(2,1)S(1)} %get-tuple-element.11, ...), kind=kLoop, calls=%fused_computation.6 | loop fusion | flops 53477376 | bytes 19038208 | tf_op jit(solution)/shard_map/mul | solution.py:110
  32.3 2.0 %fusion.10 = f32[16,32,192]{2,1,0:T(8,128)S(1)} fusion(bf16[16,1024,192]{1,2,0:T(8,128)(2,1)S(1)} %get-tuple-element.8, bf16[16,1024,192]{1,2,0:T(8,128)(2,1)S(1)} %get-tuple-element.7), kind=kOutput, calls=%fused_computation.18 | convolution fusion | flops 201326592 | bytes 7733248 | tf_op jit(solution)/shard_map/krn,krm->knm/dot_general | solution.py:114
  34.4 1.5 %fusion.2 = f32[16,32,128]{2,1,0:T(8,128)S(1)} fusion(bf16[16,1024,192]{1,2,0:T(8,128)(2,1)S(1)} %get-tuple-element.8, bf16[16,1024,192]{1,2,0:T(8,128)(2,1)S(1)} %get-tuple-element.7), kind=kOutput, calls=%fused_computation.3 | convolution fusion | flops 134217728 | bytes 5505024 | tf_op jit(solution)/shard_map/krn,krm->knm/dot_general | solution.py:114
  35.9 0.7 fusion.4
  36.6 1.2 %maximum_bitcast_fusion = f32[16,1,32,384]{3,2,1,0:T(8,128)} fusion(f32[16,32,64]{2,1,0:T(8,128)S(1)} %fusion.4, f32[16,32,128]{2,1,0:T(8,128)S(1)} %fusion.2, f32[16,32,192]{2,1,0:T(8,128)S(1)} %fusion.10), kind=kLoop, calls=%fused_computation.22 | loop fusion | flops 393216 | bytes 1572864 | tf_op jit(solution)/shard_map/reshape | solution.py:36
  37.8 7.9 %all-to-all-start.1 = ((f32[16,1,32,384]{3,2,1,0:T(8,128)}), f32[16,1,32,384]{3,2,1,0:T(8,128)S(1)}, u32[]{:S(2)}, u32[]{:S(2)}) async-start(f32[16,1,32,384]{3,2,1,0:T(8,128)} %maximum_bitcast_fusion), calls=%async_computation.1 | async-start | bytes 1572864 | tf_op jit(solution)/shard_map/all_to_all | solution.py:42
  45.7 0.1 multiply_cosine_fusion
  45.9 0.6 fusion.30
  46.5 15.0 %all-to-all-done.1 = f32[16,1,32,384]{3,2,1,0:T(8,128)S(1)} async-done(((f32[16,1,32,384]{3,2,1,0:T(8,128)}), f32[16,1,32,384]{3,2,1,0:T(8,128)S(1)}, u32[]{:S(2)}, u32[]{:S(2)}) %all-to-all-start.1) | async-done | bytes 786464 | tf_op jit(solution)/shard_map/all_to_all | solution.py:42
  61.6 0.1 slice_negate_fusion.4
  61.7 0.1 copy.83
  61.7 0.1 copy.72
  61.8 0.1 copy.73
  61.9 0.1 copy.74
  62.0 0.1 copy.81
  62.0 0.1 copy.82
  62.1 0.1 copy.70
  62.2 0.7 maximum_maximum_fusion.real_ref
  62.9 0.7 maximum_maximum_fusion.1.imag_ref
  63.6 14.6 %shard_map.38 = bf16[1,192,64]{2,1,0:T(8,128)(2,1)} custom-call(f32[1,96,96]{2,1,0:T(8,128)} %maximum_maximum_fusion.real_ref, f32[1,96,96]{2,1,0:T(8,128)} %maximum_maximum_fusion.1.imag_ref, f32[96,64]{1,0:T(8,128)} %bitcast.42, f32[96,64]{1,0:T(8,128)} %bitcast.41), custom_call_target="tpu_custom_call" | custom-call | tf_op jit(solution)/shard_map/pallas_call | solution.py:178
  78.3 0.9 copy.75
  79.2 15.1 %all_to_all.26 = bf16[16,1,192,64]{2,3,1,0:T(8,128)(2,1)S(1)} all-to-all(bf16[16,1,192,64]{2,3,1,0:T(8,128)(2,1)S(1)} %broadcast_in_dim.5), channel_id=1, replica_groups=mesh['dop'=8,'rng'=16] {'rng'}, dimensions={0} | all-to-all | bytes 786432 | tf_op jit(solution)/shard_map/all_to_all | solution.py:54
  94.3 0.4 copy.76
  94.7 0.1 slice_negate_fusion.1
  94.7 0.2 pad_maximum_fusion.4
  94.9 1.2 %fusion.13 = f32[16,128,512]{2,1,0:T(8,128)S(1)} fusion(bf16[16,512,64]{2,1,0:T(8,128)(2,1)S(1)} %reshape.121, bf16[16,192,64]{2,1,0:T(8,128)(2,1)S(1)} %bitcast.29, bf16[16,192,64]{2,1,0:T(8,128)(2,1)S(1)} %bitcast.32), kind=kOutput, calls=%fused_computation.31 | convolution fusion | flops 134742016 | bytes 6029312 | tf_op jit(solution)/shard_map/knj,krn->kjr/dot_general | solution.py:225
  96.1 0.8 fusion.16
  97.0 2.9 %add_add_fusion = f32[16,128,512]{2,1,0:T(8,128)} fusion(f32[16,128,512]{2,1,0:T(8,128)S(1)} %fusion.16, f32[16,128,512]{2,1,0:T(8,128)S(1)} %fusion.13, bf16[16,512,64]{1,2,0:T(8,128)(2,1)S(1)} %copy-done.3, bf16[16,192,64]{2,1,0:T(8,128)(2,1)S(1)} %bitcast.34, bf16[16,192,64]{2,1,0:T(8,128)(2,1)S(1)} %bitcast.31), kind=kOutput, calls=%fused_computation.5 | convolution fusion | flops 136839168 | bytes 14417920 | tf_op jit(solution)/shard_map/knj,krn->kjr/dot_general | solution.py:225
  (20 shorter events, 0.2 us)
Async XLA Ops:
  4.0 18.6 %all-to-all-start = ((bf16[8,16,4096]{2,1,0:T(8,128)(2,1)}), bf16[8,16,4096]{2,1,0:T(8,128)(2,1)S(1)}, u32[]{:S(2)}, u32[]{:S(2)}) async-start(bf16[8,16,4096]{2,1,0:T(8,128)(2,1)} %bitcast.37), calls=%async_computation | async-start | bytes 2097152 | tf_op jit(solution)/shard_map/all_to_all | solution.py:212
  23.4 5.8 %collective-permute-start = (bf16[1,512,64]{1,2,0:T(8,128)(2,1)S(1)}, bf16[1,512,64]{1,2,0:T(8,128)(2,1)S(1)}, u32[]{:S(2)}, u32[]{:S(2)}) collective-permute-start(bf16[1,512,64]{1,2,0:T(8,128)(2,1)S(1)} %copy.57), channel_id=1, source_target_pairs={{0,16},{16,32},{32,48},{48,64},{64,80},{80,96},{96,112},{112,0},{1... | collective-permute-start | bytes 196616 | tf_op jit(solution)/shard_map/ppermute | solution.py:26
  23.7 5.5 %collective-permute-start.1 = (bf16[1,512,64]{1,2,0:T(8,128)(2,1)S(1)}, bf16[1,512,64]{1,2,0:T(8,128)(2,1)S(1)}, u32[]{:S(2)}, u32[]{:S(2)}) collective-permute-start(bf16[1,512,64]{1,2,0:T(8,128)(2,1)S(1)} %copy.60), channel_id=1, source_target_pairs={{16,0},{32,16},{48,32},{64,48},{80,64},{96,80},{112,96},{0,112},{1... | collective-permute-start | bytes 196616 | tf_op jit(solution)/shard_map/ppermute | solution.py:29
  29.9 2.4 %copy-start = (bf16[16,512,64]{1,2,0:T(8,128)(2,1)}, bf16[16,512,64]{1,2,0:T(8,128)(2,1)S(1)}, u32[]{:S(2)}) copy-start(bf16[16,512,64]{1,2,0:T(8,128)(2,1)S(1)} %get-tuple-element.14) | copy-start | bytes 3145732
  29.9 2.4 %copy-start.2 = (bf16[16,512,64]{1,2,0:T(8,128)(2,1)}, bf16[16,512,64]{1,2,0:T(8,128)(2,1)S(1)}, u32[]{:S(2)}) copy-start(bf16[16,512,64]{1,2,0:T(8,128)(2,1)S(1)} %get-tuple-element.13) | copy-start | bytes 3145732
  34.4 11.3 %copy-start.4 = (s32[64]{0:T(128)S(1)}, s32[64]{0:T(128)}, u32[]{:S(2)}) copy-start(s32[64]{0:T(128)} %param.5) | copy-start | bytes 772
  37.8 23.7 %all-to-all-start.1 = ((f32[16,1,32,384]{3,2,1,0:T(8,128)}), f32[16,1,32,384]{3,2,1,0:T(8,128)S(1)}, u32[]{:S(2)}, u32[]{:S(2)}) async-start(f32[16,1,32,384]{3,2,1,0:T(8,128)} %maximum_bitcast_fusion), calls=%async_computation.1 | async-start | bytes 1572864 | tf_op jit(solution)/shard_map/all_to_all | solution.py:42
  94.6 1.5 %copy-start.1 = (bf16[16,512,64]{1,2,0:T(8,128)(2,1)S(1)}, bf16[16,512,64]{1,2,0:T(8,128)(2,1)}, u32[]{:S(2)}) copy-start(bf16[16,512,64]{1,2,0:T(8,128)(2,1)} %copy-done) | copy-start | bytes 3145732
  94.9 2.1 %copy-start.3 = (bf16[16,512,64]{1,2,0:T(8,128)(2,1)S(1)}, bf16[16,512,64]{1,2,0:T(8,128)(2,1)}, u32[]{:S(2)}) copy-start(bf16[16,512,64]{1,2,0:T(8,128)(2,1)} %copy-done.2) | copy-start | bytes 3145732

commit v12 on v11

--- a/solution.py
+++ b/solution.py
@@ -138,25 +138,50 @@
     wr_ref[:, gap:] = steer_re
     wi_ref[:, gap:] = steer_im
 
-    def step(j, carry):
+    def pick(values, hit):
+        return jnp.sum(jnp.where(hit, values, 0.0), axis=1, keepdims=True)
+
+    def times(a_r, a_i, b_r, b_i):
+        return a_r * b_r - a_i * b_i, a_r * b_i + a_i * b_r
+
+    def step(half, carry):
+        j = 2 * half
         cur_r = wr_ref[...]
         cur_i = wi_ref[...]
-        row_r = wr_ref[pl.ds(j, 1), :]
-        row_i = wi_ref[pl.ds(j, 1), :]
-        hit = lane_ids == j
-        col_r = jnp.sum(jnp.where(hit, cur_r, 0.0), axis=1, keepdims=True)
-        col_i = jnp.sum(jnp.where(hit, cur_i, 0.0), axis=1, keepdims=True)
-        lead_r = jnp.sum(jnp.where(hit, row_r, 0.0), axis=1, keepdims=True)
-        lead_i = jnp.sum(jnp.where(hit, row_i, 0.0), axis=1, keepdims=True)
-        norm = lead_r * lead_r + lead_i * lead_i
-        scaled_r = (row_r * lead_r + row_i * lead_i) / norm
-        scaled_i = (row_i * lead_r - row_r * lead_i) / norm
-        is_row = row_ids == j
-        wr_ref[...] = jnp.where(is_row, scaled_r, cur_r - (col_r * scaled_r - col_i * scaled_i))
-        wi_ref[...] = jnp.where(is_row, scaled_i, cur_i - (col_r * scaled_i + col_i * scaled_r))
+        top_r = wr_ref[pl.ds(j, 1), :]
+        top_i = wi_ref[pl.ds(j, 1), :]
+        low_r = wr_ref[pl.ds(j + 1, 1), :]
+        low_i = wi_ref[pl.ds(j + 1, 1), :]
+        first = lane_ids == j
+        second = lane_ids == j + 1
+        a_r, a_i = pick(top_r, first), pick(top_i, first)
+        b_r, b_i = pick(top_r, second), pick(top_i, second)
+        c_r, c_i = pick(low_r, first), pick(low_i, first)
+        d_r, d_i = pick(low_r, second), pick(low_i, second)
+        ad_r, ad_i = times(a_r, a_i, d_r, d_i)
+        bc_r, bc_i = times(b_r, b_i, c_r, c_i)
+        det_r, det_i = ad_r - bc_r, ad_i - bc_i
+        scale = 1.0 / (det_r * det_r + det_i * det_i)
+        inv_r, inv_i = det_r * scale, -det_i * scale
+        p_r, p_i = times(d_r, d_i, top_r, top_i)
+        q_r, q_i = times(b_r, b_i, low_r, low_i)
+        one_r, one_i = times(inv_r, inv_i, p_r - q_r, p_i - q_i)
+        s_r, s_i = times(a_r, a_i, low_r, low_i)
+        t_r, t_i = times(c_r, c_i, top_r, top_i)
+        two_r, two_i = times(inv_r, inv_i, s_r - t_r, s_i - t_i)
+        u_r, u_i = pick(cur_r, first), pick(cur_i, first)
+        v_r, v_i = pick(cur_r, second), pick(cur_i, second)
+        x_r, x_i = times(u_r, u_i, one_r, one_i)
+        y_r, y_i = times(v_r, v_i, two_r, two_i)
+        wr_ref[...] = cur_r - (x_r + y_r)
+        wi_ref[...] = cur_i - (x_i + y_i)
+        wr_ref[pl.ds(j, 1), :] = one_r
+        wi_ref[pl.ds(j, 1), :] = one_i
+        wr_ref[pl.ds(j + 1, 1), :] = two_r
+        wi_ref[pl.ds(j + 1, 1), :] = two_i
         return carry
 
-    lax.fori_loop(0, rows, step, 0)
+    lax.fori_loop(0, rows // 2, step, 0)
     solved_re = wr_ref[:, gap:]
     solved_im = wi_ref[:, gap:]
     root = jnp.sqrt(jnp.sum(steer_re * solved_re + steer_im * solved_im, axis=0, keepdims=True))
@@ -165,7 +190,6 @@
     for pos in range(rows // CH):
         unit_ref[0, 2 * pos * CH : (2 * pos + 1) * CH, :] = unit_re[pos * CH : (pos + 1) * CH]
         unit_ref[0, (2 * pos + 1) * CH : (2 * pos + 2) * CH, :] = unit_im[pos * CH : (pos + 1) * CH]
-
 
 def unit_vectors(same, cross, steer):
     count, size, _ = same.shape

time: 100 us -> 95.7 us (0.957)
  Pallas kernels: 17.7 us -> 13.1 us
    pallas_call x1, Pallas kernels: 14.6 us -> 10 us  [unit_vectors(): pl.pallas_call(eliminate, grid=(count,), in_specs=[matrix, matrix, vector...]
where the time goes in v12:
time: 95.7 us; the launch traced here: 95.2 us
  waiting for transfers between devices  28.1 us (29%)
  blocking collectives  15.1 us (16%)
  starting transfers between devices  14.3 us (15%)
  Pallas kernels  13.1 us (14%)
  matrix products  9.13 us (10%)
  other arithmetic  7.97 us (8%)
  local copies, waits for them, and re-layouts  7.3 us (8%)
    all_to_all x1, blocking collectives, copy_for_each(): lax.all_to_all(jnp.broadcast_to(array[None], (count, *array.shape)), axis...  15.1 us
    all_to_all x1, waiting for transfers between devices, sum_at_owner(): lax.all_to_all(blocks, axis, split_axis=0, concat_axis=0, tiled=True)  15 us
    all_to_all x1, waiting for transfers between devices, body(): lax.all_to_all(spectra, 'dop', split_axis=0, concat_axis=1, tiled=True)  13.1 us
    pallas_call x1, Pallas kernels, unit_vectors(): pl.pallas_call(eliminate, grid=(count,), in_specs=[matrix, matrix, vector...  10 us
    all_to_all x1, starting transfers between devices, sum_at_owner(): lax.all_to_all(blocks, axis, split_axis=0, concat_axis=0, tiled=True)  7.88 us
    dot_general x3, matrix products, body(): jnp.einsum('knj,krn->kjr', weights[:, position * 2 * CH:(position + 1) *...  4.9 us
    all_to_all x1, starting transfers between devices, body(): lax.all_to_all(spectra, 'dop', split_axis=0, concat_axis=1, tiled=True)  4.69 us
    dot_general x3, matrix products, upper_blocks(): jnp.einsum('krn,krm->knm', masked[:, :, left_pos * 2 * CH:left_pos * 2 *...  4.23 us
  transfers between devices with their start and end apart: 4, of which 2 were waited for; matrix products, arithmetic and copies ran while one was open for 6% of the time, Pallas kernels for 0%

profile of v12, /device:TPU:24, one launch (start us, length us, event | category | flops | bytes accessed | tf_op | source)
XLA Modules:
  0.0 95.2 jit_solution(9850132943138416974)
XLA Ops:
  0.0 0.3 sine_convert_fusion
  0.3 0.6 pad_maximum_fusion.10.twiddle_ref
  0.9 3.0 %shard_map.37 = bf16[128,4096]{1,0:T(8,128)(2,1)} custom-call(bf16[128,256]{1,0:T(8,128)(2,1)} %pad_maximum_fusion.10.twiddle_ref, bf16[64,2,32,128]{3,2,1,0:T(8,128)(2,1)} %echo_ref.1), custom_call_target="tpu_custom_call" | custom-call | tf_op jit(solution)/shard_map/pallas_call | solution.py:84
  4.0 4.7 %all-to-all-start = ((bf16[8,16,4096]{2,1,0:T(8,128)(2,1)}), bf16[8,16,4096]{2,1,0:T(8,128)(2,1)S(1)}, u32[]{:S(2)}, u32[]{:S(2)}) async-start(bf16[8,16,4096]{2,1,0:T(8,128)(2,1)} %bitcast.37), calls=%async_computation | async-start | bytes 2097152 | tf_op jit(solution)/shard_map/all_to_all | solution.py:236
  8.7 0.8 convert_element_type.20
  9.4 13.1 %all-to-all-done = bf16[8,16,4096]{2,1,0:T(8,128)(2,1)S(1)} async-done(((bf16[8,16,4096]{2,1,0:T(8,128)(2,1)}), bf16[8,16,4096]{2,1,0:T(8,128)(2,1)S(1)}, u32[]{:S(2)}, u32[]{:S(2)}) %all-to-all-start) | async-done | bytes 1048608 | tf_op jit(solution)/shard_map/all_to_all | solution.py:236
  22.5 0.6 slice_reduce_fusion
  23.1 0.2 slice.154
  23.3 0.1 copy.57
  23.4 0.0 collective-permute-start
  23.4 0.2 slice.157
  23.6 0.1 copy.60
  23.7 1.7 %collective-permute-start.1 = (bf16[1,512,64]{1,2,0:T(8,128)(2,1)S(1)}, bf16[1,512,64]{1,2,0:T(8,128)(2,1)S(1)}, u32[]{:S(2)}, u32[]{:S(2)}) collective-permute-start(bf16[1,512,64]{1,2,0:T(8,128)(2,1)S(1)} %copy.60), channel_id=1, source_target_pairs={{16,0},{32,16},{48,32},{64,48},{80,64},{96,80},{112,96},{0,112},{1... | collective-permute-start | bytes 196616 | tf_op jit(solution)/shard_map/ppermute | solution.py:29
  25.5 0.6 copy.58
  26.0 2.3 %reshape.121 = bf16[16,512,64]{2,1,0:T(8,128)(2,1)S(1)} reshape(bf16[16,8,4096]{2,1,0:T(8,128)(2,1)S(1)} %copy.58) | data formatting | bytes 2097152 | tf_op jit(solution)/shard_map/reshape | solution.py:237
  28.3 0.8 copy.59
  29.2 0.2 pad_maximum_fusion.1
  29.4 0.1 slice_negate_fusion
  29.4 0.3 fusion.7
  29.7 0.1 pad_maximum_fusion.2
  29.9 2.4 %broadcast_multiply_fusion = (bf16[16,1024,192]{1,2,0:T(8,128)(2,1)S(1)}, bf16[16,1024,192]{1,2,0:T(8,128)(2,1)S(1)}) fusion(bf16[16,1024]{1,0:T(8,128)(2,1)S(1)} %pad_maximum_fusion.11, bf16[18,512,32]{1,2,0:T(8,128)(2,1)S(1)} %get-tuple-element.12, bf16[18,512,32]{1,2,0:T(8,128)(2,1)S(1)} %get-tuple-element.11, ...), kind=kLoop, calls=%fused_computation.6 | loop fusion | flops 53477376 | bytes 19038208 | tf_op jit(solution)/shard_map/mul | solution.py:110
  32.3 2.0 %fusion.10 = f32[16,32,192]{2,1,0:T(8,128)S(1)} fusion(bf16[16,1024,192]{1,2,0:T(8,128)(2,1)S(1)} %get-tuple-element.8, bf16[16,1024,192]{1,2,0:T(8,128)(2,1)S(1)} %get-tuple-element.7), kind=kOutput, calls=%fused_computation.18 | convolution fusion | flops 201326592 | bytes 7733248 | tf_op jit(solution)/shard_map/krn,krm->knm/dot_general | solution.py:114
  34.4 1.5 %fusion.2 = f32[16,32,128]{2,1,0:T(8,128)S(1)} fusion(bf16[16,1024,192]{1,2,0:T(8,128)(2,1)S(1)} %get-tuple-element.8, bf16[16,1024,192]{1,2,0:T(8,128)(2,1)S(1)} %get-tuple-element.7), kind=kOutput, calls=%fused_computation.3 | convolution fusion | flops 134217728 | bytes 5505024 | tf_op jit(solution)/shard_map/krn,krm->knm/dot_general | solution.py:114
  35.9 0.7 fusion.4
  36.6 1.2 %maximum_bitcast_fusion = f32[16,1,32,384]{3,2,1,0:T(8,128)} fusion(f32[16,32,64]{2,1,0:T(8,128)S(1)} %fusion.4, f32[16,32,128]{2,1,0:T(8,128)S(1)} %fusion.2, f32[16,32,192]{2,1,0:T(8,128)S(1)} %fusion.10), kind=kLoop, calls=%fused_computation.22 | loop fusion | flops 393216 | bytes 1572864 | tf_op jit(solution)/shard_map/reshape | solution.py:36
  37.8 7.9 %all-to-all-start.1 = ((f32[16,1,32,384]{3,2,1,0:T(8,128)}), f32[16,1,32,384]{3,2,1,0:T(8,128)S(1)}, u32[]{:S(2)}, u32[]{:S(2)}) async-start(f32[16,1,32,384]{3,2,1,0:T(8,128)} %maximum_bitcast_fusion), calls=%async_computation.1 | async-start | bytes 1572864 | tf_op jit(solution)/shard_map/all_to_all | solution.py:42
  45.7 0.1 multiply_cosine_fusion
  45.9 0.6 fusion.30
  46.5 15.0 %all-to-all-done.1 = f32[16,1,32,384]{3,2,1,0:T(8,128)S(1)} async-done(((f32[16,1,32,384]{3,2,1,0:T(8,128)}), f32[16,1,32,384]{3,2,1,0:T(8,128)S(1)}, u32[]{:S(2)}, u32[]{:S(2)}) %all-to-all-start.1) | async-done | bytes 786464 | tf_op jit(solution)/shard_map/all_to_all | solution.py:42
  61.6 0.1 slice_negate_fusion.4
  61.7 0.1 copy.83
  61.7 0.1 copy.72
  61.8 0.1 copy.73
  61.9 0.1 copy.74
  62.0 0.1 copy.81
  62.0 0.1 copy.82
  62.1 0.1 copy.70
  62.2 0.7 maximum_maximum_fusion.real_ref
  62.9 0.7 maximum_maximum_fusion.1.imag_ref
  63.6 10.0 %shard_map.38 = bf16[1,192,64]{2,1,0:T(8,128)(2,1)} custom-call(f32[1,96,96]{2,1,0:T(8,128)} %maximum_maximum_fusion.real_ref, f32[1,96,96]{2,1,0:T(8,128)} %maximum_maximum_fusion.1.imag_ref, f32[96,64]{1,0:T(8,128)} %bitcast.42, f32[96,64]{1,0:T(8,128)} %bitcast.41), custom_call_target="tpu_custom_call" | custom-call | tf_op jit(solution)/shard_map/pallas_call | solution.py:202
  73.6 0.9 copy.75
  74.6 15.1 %all_to_all.26 = bf16[16,1,192,64]{2,3,1,0:T(8,128)(2,1)S(1)} all-to-all(bf16[16,1,192,64]{2,3,1,0:T(8,128)(2,1)S(1)} %broadcast_in_dim.5), channel_id=1, replica_groups=mesh['dop'=8,'rng'=16] {'rng'}, dimensions={0} | all-to-all | bytes 786432 | tf_op jit(solution)/shard_map/all_to_all | solution.py:54
  89.6 0.4 copy.76
  90.0 0.1 slice_negate_fusion.1
  90.1 0.2 pad_maximum_fusion.4
  90.3 1.2 %fusion.13 = f32[16,128,512]{2,1,0:T(8,128)S(1)} fusion(bf16[16,512,64]{2,1,0:T(8,128)(2,1)S(1)} %reshape.121, bf16[16,192,64]{2,1,0:T(8,128)(2,1)S(1)} %bitcast.29, bf16[16,192,64]{2,1,0:T(8,128)(2,1)S(1)} %bitcast.32), kind=kOutput, calls=%fused_computation.31 | convolution fusion | flops 134742016 | bytes 6029312 | tf_op jit(solution)/shard_map/knj,krn->kjr/dot_general | solution.py:249
  91.5 0.8 fusion.16
  92.4 2.9 %add_add_fusion = f32[16,128,512]{2,1,0:T(8,128)} fusion(f32[16,128,512]{2,1,0:T(8,128)S(1)} %fusion.16, f32[16,128,512]{2,1,0:T(8,128)S(1)} %fusion.13, bf16[16,512,64]{1,2,0:T(8,128)(2,1)S(1)} %copy-done.3, bf16[16,192,64]{2,1,0:T(8,128)(2,1)S(1)} %bitcast.34, bf16[16,192,64]{2,1,0:T(8,128)(2,1)S(1)} %bitcast.31), kind=kOutput, calls=%fused_computation.5 | convolution fusion | flops 136839168 | bytes 14417920 | tf_op jit(solution)/shard_map/knj,krn->kjr/dot_general | solution.py:249
  (20 shorter events, 0.2 us)
Async XLA Ops:
  4.0 18.6 %all-to-all-start = ((bf16[8,16,4096]{2,1,0:T(8,128)(2,1)}), bf16[8,16,4096]{2,1,0:T(8,128)(2,1)S(1)}, u32[]{:S(2)}, u32[]{:S(2)}) async-start(bf16[8,16,4096]{2,1,0:T(8,128)(2,1)} %bitcast.37), calls=%async_computation | async-start | bytes 2097152 | tf_op jit(solution)/shard_map/all_to_all | solution.py:236
  23.4 5.8 %collective-permute-start = (bf16[1,512,64]{1,2,0:T(8,128)(2,1)S(1)}, bf16[1,512,64]{1,2,0:T(8,128)(2,1)S(1)}, u32[]{:S(2)}, u32[]{:S(2)}) collective-permute-start(bf16[1,512,64]{1,2,0:T(8,128)(2,1)S(1)} %copy.57), channel_id=1, source_target_pairs={{0,16},{16,32},{32,48},{48,64},{64,80},{80,96},{96,112},{112,0},{1... | collective-permute-start | bytes 196616 | tf_op jit(solution)/shard_map/ppermute | solution.py:26
  23.7 5.5 %collective-permute-start.1 = (bf16[1,512,64]{1,2,0:T(8,128)(2,1)S(1)}, bf16[1,512,64]{1,2,0:T(8,128)(2,1)S(1)}, u32[]{:S(2)}, u32[]{:S(2)}) collective-permute-start(bf16[1,512,64]{1,2,0:T(8,128)(2,1)S(1)} %copy.60), channel_id=1, source_target_pairs={{16,0},{32,16},{48,32},{64,48},{80,64},{96,80},{112,96},{0,112},{1... | collective-permute-start | bytes 196616 | tf_op jit(solution)/shard_map/ppermute | solution.py:29
  29.9 2.4 %copy-start = (bf16[16,512,64]{1,2,0:T(8,128)(2,1)}, bf16[16,512,64]{1,2,0:T(8,128)(2,1)S(1)}, u32[]{:S(2)}) copy-start(bf16[16,512,64]{1,2,0:T(8,128)(2,1)S(1)} %get-tuple-element.14) | copy-start | bytes 3145732
  29.9 2.4 %copy-start.2 = (bf16[16,512,64]{1,2,0:T(8,128)(2,1)}, bf16[16,512,64]{1,2,0:T(8,128)(2,1)S(1)}, u32[]{:S(2)}) copy-start(bf16[16,512,64]{1,2,0:T(8,128)(2,1)S(1)} %get-tuple-element.13) | copy-start | bytes 3145732
  34.4 11.3 %copy-start.4 = (s32[64]{0:T(128)S(1)}, s32[64]{0:T(128)}, u32[]{:S(2)}) copy-start(s32[64]{0:T(128)} %param.5) | copy-start | bytes 772
  37.8 23.7 %all-to-all-start.1 = ((f32[16,1,32,384]{3,2,1,0:T(8,128)}), f32[16,1,32,384]{3,2,1,0:T(8,128)S(1)}, u32[]{:S(2)}, u32[]{:S(2)}) async-start(f32[16,1,32,384]{3,2,1,0:T(8,128)} %maximum_bitcast_fusion), calls=%async_computation.1 | async-start | bytes 1572864 | tf_op jit(solution)/shard_map/all_to_all | solution.py:42
  90.0 1.5 %copy-start.1 = (bf16[16,512,64]{1,2,0:T(8,128)(2,1)S(1)}, bf16[16,512,64]{1,2,0:T(8,128)(2,1)}, u32[]{:S(2)}) copy-start(bf16[16,512,64]{1,2,0:T(8,128)(2,1)} %copy-done) | copy-start | bytes 3145732
  90.3 2.1 %copy-start.3 = (bf16[16,512,64]{1,2,0:T(8,128)(2,1)S(1)}, bf16[16,512,64]{1,2,0:T(8,128)(2,1)}, u32[]{:S(2)}) copy-start(bf16[16,512,64]{1,2,0:T(8,128)(2,1)} %copy-done.2) | copy-start | bytes 3145732

commit v13 on v12

--- a/solution.py
+++ b/solution.py
@@ -108,16 +108,9 @@
     both = jnp.concatenate([snap, turned_snap], axis=1)
     weighting = jnp.concatenate([mask_rows, mask_rows], axis=1)[:, :, None]
     masked = both * weighting
-    pieces = []
-    for left_pos in range(3):
-        pieces.append(
-            jnp.einsum(
-                "krn,krm->knm",
-                masked[:, :, left_pos * 2 * CH : left_pos * 2 * CH + CH],
-                both[:, :, left_pos * 2 * CH :],
-                preferred_element_type=jnp.float32,
-            )
-        )
+    leading = masked.reshape(*masked.shape[:2], 3, 2, CH)[:, :, :, 0].reshape(*masked.shape[:2], 3 * CH)
+    rows = jnp.einsum("krn,krm->knm", leading, both, preferred_element_type=jnp.float32)
+    pieces = [rows[:, b * CH : (b + 1) * CH, b * 2 * CH :] for b in range(3)]
     return jnp.concatenate(pieces, axis=-1)
 
 

time: 95.7 us -> 108 us (1.13)
  local copies, waits for them, and re-layouts: 7.3 us -> 23.3 us
  other arithmetic: 7.97 us -> 5.99 us
  matrix products: 9.13 us -> 8.03 us
    concatenate x0 -> x2, local copies, waits for them, and re-layouts: none -> 14.7 us  [upper_blocks(): snap = jnp.concatenate([edged[b:b + bin_count] for b in range(3)], axis=-1)]
    mul x1, other arithmetic: 2.42 us -> 0.74 us  [upper_blocks(): masked = both * weighting]
    dot_general x3 -> x1, matrix products: 4.23 us -> 3.08 us  [upper_blocks(): jnp.einsum('krn,krm->knm', leading, both, preferred_element_type=jnp.floa...]
    unnamed x13 -> x17, local copies, waits for them, and re-layouts: 0.24 us -> 1.33 us
  transfers between devices with their start and end apart: 4 -> 4, of which waited for: 2 -> 2; matrix products, arithmetic and copies ran while one was open for 6% -> 18% of each run, Pallas kernels for 0% -> 0%
where the time goes in v13:
time: 108 us; the launch traced here: 107 us
  waiting for transfers between devices  28.3 us (26%)
  local copies, waits for them, and re-layouts  23.3 us (22%)
  starting transfers between devices  14.3 us (13%)
  blocking collectives  14.2 us (13%)
  Pallas kernels  13.1 us (12%)
  matrix products  8.03 us (7%)
  other arithmetic  5.99 us (6%)
    concatenate x2, local copies, waits for them, and re-layouts, upper_blocks(): snap = jnp.concatenate([edged[b:b + bin_count] for b in range(3)], axis=-1)  14.7 us
    all_to_all x1, waiting for transfers between devices, sum_at_owner(): lax.all_to_all(blocks, axis, split_axis=0, concat_axis=0, tiled=True)  14.4 us
    all_to_all x1, blocking collectives, copy_for_each(): lax.all_to_all(jnp.broadcast_to(array[None], (count, *array.shape)), axis...  14.2 us
    all_to_all x1, waiting for transfers between devices, body(): lax.all_to_all(spectra, 'dop', split_axis=0, concat_axis=1, tiled=True)  13.8 us
    pallas_call x1, Pallas kernels, unit_vectors(): pl.pallas_call(eliminate, grid=(count,), in_specs=[matrix, matrix, vector...  10 us
    all_to_all x1, starting transfers between devices, sum_at_owner(): lax.all_to_all(blocks, axis, split_axis=0, concat_axis=0, tiled=True)  7.88 us
    dot_general x3, matrix products, body(): jnp.einsum('knj,krn->kjr', weights[:, position * 2 * CH:(position + 1) *...  4.95 us
    all_to_all x1, starting transfers between devices, body(): lax.all_to_all(spectra, 'dop', split_axis=0, concat_axis=1, tiled=True)  4.69 us
  transfers between devices with their start and end apart: 4, of which 2 were waited for; matrix products, arithmetic and copies ran while one was open for 18% of the time, Pallas kernels for 0%

profile of v13, /device:TPU:24, one launch (start us, length us, event | category | flops | bytes accessed | tf_op | source)
XLA Modules:
  0.0 107.4 jit_solution(17475896287130003828)
XLA Ops:
  0.0 0.3 sine_convert_fusion
  0.3 0.6 pad_maximum_fusion.14.twiddle_ref
  0.9 3.0 %shard_map.37 = bf16[128,4096]{1,0:T(8,128)(2,1)} custom-call(bf16[128,256]{1,0:T(8,128)(2,1)} %pad_maximum_fusion.14.twiddle_ref, bf16[64,2,32,128]{3,2,1,0:T(8,128)(2,1)} %echo_ref.1), custom_call_target="tpu_custom_call" | custom-call | tf_op jit(solution)/shard_map/pallas_call | solution.py:84
  4.0 4.7 %all-to-all-start = ((bf16[8,16,4096]{2,1,0:T(8,128)(2,1)}), bf16[8,16,4096]{2,1,0:T(8,128)(2,1)S(1)}, u32[]{:S(2)}, u32[]{:S(2)}) async-start(bf16[8,16,4096]{2,1,0:T(8,128)(2,1)} %bitcast.48), calls=%async_computation | async-start | bytes 2097152 | tf_op jit(solution)/shard_map/all_to_all | solution.py:229
  8.7 13.8 %all-to-all-done = bf16[8,16,4096]{2,1,0:T(8,128)(2,1)S(1)} async-done(((bf16[8,16,4096]{2,1,0:T(8,128)(2,1)}), bf16[8,16,4096]{2,1,0:T(8,128)(2,1)S(1)}, u32[]{:S(2)}, u32[]{:S(2)}) %all-to-all-start) | async-done | bytes 1048608 | tf_op jit(solution)/shard_map/all_to_all | solution.py:229
  22.5 0.6 slice_reduce_fusion
  23.1 0.2 slice.151
  23.3 0.1 copy.64
  23.4 0.2 slice.154
  23.6 0.1 copy.68
  23.7 1.7 %collective-permute-start.1 = (bf16[1,512,64]{1,2,0:T(8,128)(2,1)S(1)}, bf16[1,512,64]{1,2,0:T(8,128)(2,1)S(1)}, u32[]{:S(2)}, u32[]{:S(2)}) collective-permute-start(bf16[1,512,64]{1,2,0:T(8,128)(2,1)S(1)} %copy.68), channel_id=1, source_target_pairs={{16,0},{32,16},{48,32},{64,48},{80,64},{96,80},{112,96},{0,112},{1... | collective-permute-start | bytes 196616 | tf_op jit(solution)/shard_map/ppermute | solution.py:29
  25.4 0.6 copy.65
  26.0 2.3 %reshape.128 = bf16[16,512,64]{2,1,0:T(8,128)(2,1)S(1)} reshape(bf16[16,8,4096]{2,1,0:T(8,128)(2,1)S(1)} %copy.65) | data formatting | bytes 2097152 | tf_op jit(solution)/shard_map/reshape | solution.py:230
  28.3 4.4 %concatenate.76 = bf16[16,512,1,2,32]{4,3,1,0,2:T(2,128)(2,1)} reshape(bf16[16,8,4096]{2,1,0:T(8,128)(2,1)S(1)} %copy.65) | data formatting | bytes 2097152 | tf_op jit(solution)/shard_map/concatenate | solution.py:106
  32.7 0.8 copy.66
  33.5 10.3 %copy.71 = bf16[16,512,1,2,32]{1,4,3,2,0:T(8,128)(2,1)} copy(bf16[16,512,1,2,32]{4,3,1,0,2:T(2,128)(2,1)} %concatenate.76) | data formatting | bytes 2097152 | tf_op jit(solution)/shard_map/concatenate | solution.py:106
  43.9 0.2 pad_maximum_fusion.4
  44.0 0.1 slice_negate_fusion
  44.1 0.4 fusion.14
  44.5 0.3 pad_maximum_fusion.3
  44.9 0.1 pad_maximum_fusion.6
  45.0 0.7 copy-done.4
  45.7 0.7 fusion.12
  46.5 3.1 %fusion = f32[16,96,192]{2,1,0:T(8,128)S(1)} fusion(bf16[16,1024,96]{1,2,0:T(8,128)(2,1)S(1)} %bitcast.49, bf16[16,512,64]{1,2,0:T(8,128)(2,1)S(1)} %get-tuple-element.8, bf16[16,512,64]{1,2,0:T(8,128)(2,1)S(1)} %get-tuple-element.9, bf16[16,512,64]{1,2,0:T(8,128)(2,1)S(1)} %get-tuple-element.7, bf16[16,512,64]{1,2,0:T(8,128)(2,1)S(1)} %get-tuple-element.12, ...), kind=kOutput, calls=%fused_computation | convolution fusion | flops 641728512 | bytes 10616832 | tf_op jit(solution)/shard_map/krn,krm->knm/dot_general | solution.py:112
  49.6 0.1 slice.193
  49.8 1.2 %maximum_bitcast_fusion = f32[16,1,32,384]{3,2,1,0:T(8,128)} fusion(f32[16,32,64]{2,1,0:T(8,128)S(1)} %slice.194, f32[16,32,128]{2,1,0:T(8,128)S(1)} %slice.193, f32[16,32,192]{2,1,0:T(8,128)S(1)} %slice.192), kind=kLoop, calls=%fused_computation.28 | loop fusion | flops 393216 | bytes 1572864 | tf_op jit(solution)/shard_map/reshape | solution.py:36
  51.0 7.9 %all-to-all-start.1 = ((f32[16,1,32,384]{3,2,1,0:T(8,128)}), f32[16,1,32,384]{3,2,1,0:T(8,128)S(1)}, u32[]{:S(2)}, u32[]{:S(2)}) async-start(f32[16,1,32,384]{3,2,1,0:T(8,128)} %maximum_bitcast_fusion), calls=%async_computation.1 | async-start | bytes 1572864 | tf_op jit(solution)/shard_map/all_to_all | solution.py:42
  58.9 0.1 multiply_cosine_fusion
  59.1 0.6 fusion.33
  59.7 14.4 %all-to-all-done.1 = f32[16,1,32,384]{3,2,1,0:T(8,128)S(1)} async-done(((f32[16,1,32,384]{3,2,1,0:T(8,128)}), f32[16,1,32,384]{3,2,1,0:T(8,128)S(1)}, u32[]{:S(2)}, u32[]{:S(2)}) %all-to-all-start.1) | async-done | bytes 786464 | tf_op jit(solution)/shard_map/all_to_all | solution.py:42
  74.2 0.1 slice_negate_fusion.4
  74.3 0.1 copy.92
  74.4 0.1 copy.82
  74.5 0.1 copy.83
  74.5 0.1 copy.84
  74.7 0.1 copy.91
  74.8 0.8 maximum_maximum_fusion.real_ref
  75.6 0.7 maximum_maximum_fusion.1.imag_ref
  76.3 10.0 %shard_map.38 = bf16[1,192,64]{2,1,0:T(8,128)(2,1)} custom-call(f32[1,96,96]{2,1,0:T(8,128)} %maximum_maximum_fusion.real_ref, f32[1,96,96]{2,1,0:T(8,128)} %maximum_maximum_fusion.1.imag_ref, f32[96,64]{1,0:T(8,128)} %bitcast.54, f32[96,64]{1,0:T(8,128)} %bitcast.53), custom_call_target="tpu_custom_call" | custom-call | tf_op jit(solution)/shard_map/pallas_call | solution.py:195
  86.3 0.9 copy.85
  87.2 14.2 %all_to_all.26 = bf16[16,1,192,64]{2,3,1,0:T(8,128)(2,1)S(1)} all-to-all(bf16[16,1,192,64]{2,3,1,0:T(8,128)(2,1)S(1)} %broadcast_in_dim.5), channel_id=1, replica_groups=mesh['dop'=8,'rng'=16] {'rng'}, dimensions={0} | all-to-all | bytes 786432 | tf_op jit(solution)/shard_map/all_to_all | solution.py:54
  101.4 0.4 copy.86
  101.8 0.1 slice_negate_fusion.1
  101.9 0.2 pad_maximum_fusion.8
  102.1 1.2 %fusion.16 = f32[16,128,512]{2,1,0:T(8,128)S(1)} fusion(bf16[16,512,64]{2,1,0:T(8,128)(2,1)S(1)} %reshape.128, bf16[16,192,64]{2,1,0:T(8,128)(2,1)S(1)} %bitcast.37, bf16[16,192,64]{2,1,0:T(8,128)(2,1)S(1)} %bitcast.41), kind=kOutput, calls=%fused_computation.37 | convolution fusion | flops 134742016 | bytes 6029312 | tf_op jit(solution)/shard_map/knj,krn->kjr/dot_general | solution.py:242
  103.3 0.8 fusion.19
  104.1 0.4 copy-done.3
  104.5 2.9 %add_add_fusion = f32[16,128,512]{2,1,0:T(8,128)} fusion(f32[16,128,512]{2,1,0:T(8,128)S(1)} %fusion.19, f32[16,128,512]{2,1,0:T(8,128)S(1)} %fusion.16, bf16[16,512,64]{1,2,0:T(8,128)(2,1)S(1)} %copy-done.3, bf16[16,192,64]{2,1,0:T(8,128)(2,1)S(1)} %bitcast.43, bf16[16,192,64]{2,1,0:T(8,128)(2,1)S(1)} %bitcast.39), kind=kOutput, calls=%fused_computation.12 | convolution fusion | flops 136839168 | bytes 14417920 | tf_op jit(solution)/shard_map/knj,krn->kjr/dot_general | solution.py:242
  (28 shorter events, 0.4 us)
Async XLA Ops:
  0.0 8.7 %copy-start.5 = (s32[16,512]{1,0:T(8,128)S(1)}, s32[16,512]{1,0:T(8,128)}, u32[]{:S(2)}) copy-start(s32[16,512]{1,0:T(8,128)} %param.4) | copy-start | bytes 98308
  4.0 18.6 %all-to-all-start = ((bf16[8,16,4096]{2,1,0:T(8,128)(2,1)}), bf16[8,16,4096]{2,1,0:T(8,128)(2,1)S(1)}, u32[]{:S(2)}, u32[]{:S(2)}) async-start(bf16[8,16,4096]{2,1,0:T(8,128)(2,1)} %bitcast.48), calls=%async_computation | async-start | bytes 2097152 | tf_op jit(solution)/shard_map/all_to_all | solution.py:229
  23.4 20.5 %collective-permute-start = (bf16[1,512,64]{1,2,0:T(8,128)(2,1)S(1)}, bf16[1,512,64]{1,2,0:T(8,128)(2,1)S(1)}, u32[]{:S(2)}, u32[]{:S(2)}) collective-permute-start(bf16[1,512,64]{1,2,0:T(8,128)(2,1)S(1)} %copy.64), channel_id=1, source_target_pairs={{0,16},{16,32},{32,48},{48,64},{64,80},{80,96},{96,112},{112,0},{1... | collective-permute-start | bytes 196616 | tf_op jit(solution)/shard_map/ppermute | solution.py:26
  23.7 20.2 %collective-permute-start.1 = (bf16[1,512,64]{1,2,0:T(8,128)(2,1)S(1)}, bf16[1,512,64]{1,2,0:T(8,128)(2,1)S(1)}, u32[]{:S(2)}, u32[]{:S(2)}) collective-permute-start(bf16[1,512,64]{1,2,0:T(8,128)(2,1)S(1)} %copy.68), channel_id=1, source_target_pairs={{16,0},{32,16},{48,32},{64,48},{80,64},{96,80},{112,96},{0,112},{1... | collective-permute-start | bytes 196616 | tf_op jit(solution)/shard_map/ppermute | solution.py:29
  44.5 1.2 %copy-start.4 = (bf16[16,512,1,2,32]{1,4,3,2,0:T(8,128)(2,1)S(1)}, bf16[16,512,1,2,32]{1,4,3,2,0:T(8,128)(2,1)}, u32[]{:S(2)}) copy-start(bf16[16,512,1,2,32]{1,4,3,2,0:T(8,128)(2,1)} %copy.71) | copy-start | bytes 3145732
  45.0 1.5 %copy-start = (bf16[16,512,64]{1,2,0:T(8,128)(2,1)}, bf16[16,512,64]{1,2,0:T(8,128)(2,1)S(1)}, u32[]{:S(2)}) copy-start(bf16[16,512,64]{1,2,0:T(8,128)(2,1)S(1)} %get-tuple-element.13) | copy-start | bytes 3145732
  45.0 1.5 %copy-start.2 = (bf16[16,512,64]{1,2,0:T(8,128)(2,1)}, bf16[16,512,64]{1,2,0:T(8,128)(2,1)S(1)}, u32[]{:S(2)}) copy-start(bf16[16,512,64]{1,2,0:T(8,128)(2,1)S(1)} %get-tuple-element.12) | copy-start | bytes 3145732
  49.6 9.3 %copy-start.6 = (s32[64]{0:T(128)S(1)}, s32[64]{0:T(128)}, u32[]{:S(2)}) copy-start(s32[64]{0:T(128)} %param.5) | copy-start | bytes 772
  51.0 23.1 %all-to-all-start.1 = ((f32[16,1,32,384]{3,2,1,0:T(8,128)}), f32[16,1,32,384]{3,2,1,0:T(8,128)S(1)}, u32[]{:S(2)}, u32[]{:S(2)}) async-start(f32[16,1,32,384]{3,2,1,0:T(8,128)} %maximum_bitcast_fusion), calls=%async_computation.1 | async-start | bytes 1572864 | tf_op jit(solution)/shard_map/all_to_all | solution.py:42
  102.1 1.2 %copy-start.1 = (bf16[16,512,64]{1,2,0:T(8,128)(2,1)S(1)}, bf16[16,512,64]{1,2,0:T(8,128)(2,1)}, u32[]{:S(2)}) copy-start(bf16[16,512,64]{1,2,0:T(8,128)(2,1)} %copy-done) | copy-start | bytes 3145732
  103.3 1.2 %copy-start.3 = (bf16[16,512,64]{1,2,0:T(8,128)(2,1)S(1)}, bf16[16,512,64]{1,2,0:T(8,128)(2,1)}, u32[]{:S(2)}) copy-start(bf16[16,512,64]{1,2,0:T(8,128)(2,1)} %copy-done.2) | copy-start | bytes 3145732

commit v14 on v12

--- a/solution.py
+++ b/solution.py
@@ -118,7 +118,7 @@
                 preferred_element_type=jnp.float32,
             )
         )
-    return jnp.concatenate(pieces, axis=-1)
+    return both[:, : edged.shape[1]], jnp.concatenate(pieces, axis=-1)
 
 
 def eliminate(real_ref, imag_ref, steer_re_ref, steer_im_ref, unit_ref, wr_ref, wi_ref):
@@ -237,22 +237,14 @@
     turned = turned.reshape(turned.shape[0], -1, 2 * CH)
     edged = padded(turned, (("dop", 0),), 1)
     bin_count = edged.shape[0] - 2
-    upper = upper_blocks(edged, training.astype(jnp.bfloat16))
+    snap, upper = upper_blocks(edged, training.astype(jnp.bfloat16))
     my_upper = sum_at_owner(upper, "rng", 0)
     my_unit = unit_vectors(*hermitian_parts(my_upper), steering(look_index))
     unit = gather_directly(my_unit, "rng", 0)
     shaped = unit.reshape(bin_count, 3, 2, CH, LOOKS)
     rotated = jnp.stack([-shaped[:, :, 1], shaped[:, :, 0]], axis=2).reshape(bin_count, SNAP, LOOKS)
     weights = jnp.concatenate([unit, rotated], axis=2)
-    summed = None
-    for position in range(3):
-        term = jnp.einsum(
-            "knj,krn->kjr",
-            weights[:, position * 2 * CH : (position + 1) * 2 * CH],
-            edged[position : position + bin_count],
-            preferred_element_type=jnp.float32,
-        )
-        summed = term if summed is None else summed + term
+    summed = jnp.einsum("knj,krn->kjr", weights, snap, preferred_element_type=jnp.float32)
     return summed.reshape(bin_count, 2, LOOKS, edged.shape[1])
 
 

time: 95.7 us -> 100 us (1.045)
  local copies, waits for them, and re-layouts: 7.3 us -> 11.1 us
  other arithmetic: 7.97 us -> 10.2 us
    all_to_all x1, local copies, waits for them, and re-layouts: 0.38 us -> 2.22 us  [copy_for_each(): lax.all_to_all(jnp.broadcast_to(array[None], (count, *array.shape)), axis...]
    reduce_sum x1, other arithmetic: 0.04 us -> 1.18 us  [sum_at_owner(): return arrived.sum(axis=0)]
    neg x1, other arithmetic: 0.08 us -> 1.2 us  [body(): -shaped[:, :, 1]]
    dot_general x3 -> x1, matrix products: 4.9 us -> 4.35 us  [body(): jnp.einsum('knj,krn->kjr', weights, snap, preferred_element_type=jnp.floa...]
  transfers between devices with their start and end apart: 4 -> 4, of which waited for: 2 -> 2; matrix products, arithmetic and copies ran while one was open for 6% -> 8% of each run, Pallas kernels for 0% -> 0%
where the time goes in v14:
time: 100 us; the launch traced here: 99.3 us
  waiting for transfers between devices  27.6 us (28%)
  starting transfers between devices  14.4 us (14%)
  blocking collectives  14.3 us (14%)
  Pallas kernels  13.1 us (13%)
  local copies, waits for them, and re-layouts  11.1 us (11%)
  other arithmetic  10.2 us (10%)
  matrix products  8.58 us (9%)
    all_to_all x1, waiting for transfers between devices, sum_at_owner(): lax.all_to_all(blocks, axis, split_axis=0, concat_axis=0, tiled=True)  14.5 us
    all_to_all x1, blocking collectives, copy_for_each(): lax.all_to_all(jnp.broadcast_to(array[None], (count, *array.shape)), axis...  14.3 us
    all_to_all x1, waiting for transfers between devices, body(): lax.all_to_all(spectra, 'dop', split_axis=0, concat_axis=1, tiled=True)  13.1 us
    pallas_call x1, Pallas kernels, unit_vectors(): pl.pallas_call(eliminate, grid=(count,), in_specs=[matrix, matrix, vector...  10 us
    all_to_all x1, starting transfers between devices, sum_at_owner(): lax.all_to_all(blocks, axis, split_axis=0, concat_axis=0, tiled=True)  7.92 us
    all_to_all x1, starting transfers between devices, body(): lax.all_to_all(spectra, 'dop', split_axis=0, concat_axis=1, tiled=True)  4.69 us
    dot_general x1, matrix products, body(): jnp.einsum('knj,krn->kjr', weights, snap, preferred_element_type=jnp.floa...  4.35 us
    dot_general x3, matrix products, upper_blocks(): jnp.einsum('krn,krm->knm', masked[:, :, left_pos * 2 * CH:left_pos * 2 *...  4.23 us
  transfers between devices with their start and end apart: 4, of which 2 were waited for; matrix products, arithmetic and copies ran while one was open for 8% of the time, Pallas kernels for 0%

profile of v14, /device:TPU:24, one launch (start us, length us, event | category | flops | bytes accessed | tf_op | source)
XLA Modules:
  0.0 99.3 jit_solution(1476049166405814309)
XLA Ops:
  0.0 0.3 sine_convert_fusion
  0.3 0.6 pad_maximum_fusion.6.twiddle_ref
  0.9 3.0 %shard_map.37 = bf16[128,4096]{1,0:T(8,128)(2,1)} custom-call(bf16[128,256]{1,0:T(8,128)(2,1)} %pad_maximum_fusion.6.twiddle_ref, bf16[64,2,32,128]{3,2,1,0:T(8,128)(2,1)} %echo_ref.1), custom_call_target="tpu_custom_call" | custom-call | tf_op jit(solution)/shard_map/pallas_call | solution.py:84
  4.0 4.7 %all-to-all-start = ((bf16[8,16,4096]{2,1,0:T(8,128)(2,1)}), bf16[8,16,4096]{2,1,0:T(8,128)(2,1)S(1)}, u32[]{:S(2)}, u32[]{:S(2)}) async-start(bf16[8,16,4096]{2,1,0:T(8,128)(2,1)} %bitcast.27), calls=%async_computation | async-start | bytes 2097152 | tf_op jit(solution)/shard_map/all_to_all | solution.py:236
  8.7 0.8 convert_element_type.20
  9.4 13.1 %all-to-all-done = bf16[8,16,4096]{2,1,0:T(8,128)(2,1)S(1)} async-done(((bf16[8,16,4096]{2,1,0:T(8,128)(2,1)}), bf16[8,16,4096]{2,1,0:T(8,128)(2,1)S(1)}, u32[]{:S(2)}, u32[]{:S(2)}) %all-to-all-start) | async-done | bytes 1048608 | tf_op jit(solution)/shard_map/all_to_all | solution.py:236
  22.5 0.6 slice_reduce_fusion.1
  23.1 0.2 slice.143
  23.3 0.1 copy.55
  23.4 0.0 collective-permute-start
  23.4 0.2 slice.146
  23.6 0.1 copy.58
  23.7 1.7 %collective-permute-start.1 = (bf16[1,512,64]{1,2,0:T(8,128)(2,1)S(1)}, bf16[1,512,64]{1,2,0:T(8,128)(2,1)S(1)}, u32[]{:S(2)}, u32[]{:S(2)}) collective-permute-start(bf16[1,512,64]{1,2,0:T(8,128)(2,1)S(1)} %copy.58), channel_id=1, source_target_pairs={{16,0},{32,16},{48,32},{64,48},{80,64},{96,80},{112,96},{0,112},{1... | collective-permute-start | bytes 196616 | tf_op jit(solution)/shard_map/ppermute | solution.py:29
  25.5 1.6 %copy.56 = bf16[16,8,4096]{2,1,0:T(8,128)(2,1)} copy(bf16[16,8,4096]{2,0,1:T(8,128)(2,1)S(1)} %bitcast.26) | data formatting | bytes 2097152 | tf_op jit(solution)/shard_map/all_to_all | solution.py:236
  27.0 3.3 %reshape.121 = bf16[16,512,64]{2,1,0:T(8,128)(2,1)S(1)} reshape(bf16[16,8,4096]{2,1,0:T(8,128)(2,1)} %copy.56) | data formatting | bytes 2097152 | tf_op jit(solution)/shard_map/reshape | solution.py:237
  30.3 0.8 copy.57
  31.1 0.0 collective-permute-done
  31.1 0.2 pad_maximum_fusion.1
  31.3 0.1 slice_negate_fusion
  31.4 0.3 fusion.13
  31.7 0.1 pad_maximum_fusion.3
  31.8 2.4 %broadcast_multiply_fusion = (bf16[16,1024,192]{1,2,0:T(8,128)(2,1)S(1)}, bf16[16,1024,192]{1,2,0:T(8,128)(2,1)S(1)}) fusion(bf16[16,1024]{1,0:T(8,128)(2,1)S(1)} %pad_maximum_fusion.7, bf16[18,512,32]{1,2,0:T(8,128)(2,1)S(1)} %get-tuple-element.12, bf16[18,512,32]{1,2,0:T(8,128)(2,1)S(1)} %get-tuple-element.11, ...), kind=kLoop, calls=%fused_computation.11 | loop fusion | flops 53477376 | bytes 19038208 | tf_op jit(solution)/shard_map/mul | solution.py:110
  34.2 2.0 %fusion.16 = f32[16,32,192]{2,1,0:T(8,128)S(1)} fusion(bf16[16,1024,192]{1,2,0:T(8,128)(2,1)S(1)} %get-tuple-element.8, bf16[16,1024,192]{1,2,0:T(8,128)(2,1)S(1)} %get-tuple-element.7), kind=kOutput, calls=%fused_computation.23 | convolution fusion | flops 201326592 | bytes 7733248 | tf_op jit(solution)/shard_map/krn,krm->knm/dot_general | solution.py:114
  36.3 1.5 %fusion.2 = f32[16,32,128]{2,1,0:T(8,128)S(1)} fusion(bf16[16,1024,192]{1,2,0:T(8,128)(2,1)S(1)} %get-tuple-element.8, bf16[16,1024,192]{1,2,0:T(8,128)(2,1)S(1)} %get-tuple-element.7), kind=kOutput, calls=%fused_computation.3 | convolution fusion | flops 134217728 | bytes 5505024 | tf_op jit(solution)/shard_map/krn,krm->knm/dot_general | solution.py:114
  37.8 0.7 fusion.10
  38.4 1.2 %maximum_bitcast_fusion = f32[16,1,32,384]{3,2,1,0:T(8,128)} fusion(f32[16,32,64]{2,1,0:T(8,128)S(1)} %fusion.10, f32[16,32,128]{2,1,0:T(8,128)S(1)} %fusion.2, f32[16,32,192]{2,1,0:T(8,128)S(1)} %fusion.16), kind=kLoop, calls=%fused_computation.27 | loop fusion | flops 393216 | bytes 1572864 | tf_op jit(solution)/shard_map/reshape | solution.py:36
  39.6 7.9 %all-to-all-start.1 = ((f32[16,1,32,384]{3,2,1,0:T(8,128)}), f32[16,1,32,384]{3,2,1,0:T(8,128)}, u32[]{:S(2)}, u32[]{:S(2)}) async-start(f32[16,1,32,384]{3,2,1,0:T(8,128)} %maximum_bitcast_fusion), calls=%async_computation.1 | async-start | bytes 1572864 | tf_op jit(solution)/shard_map/all_to_all | solution.py:42
  47.6 0.1 multiply_cosine_fusion
  47.7 0.7 fusion.29
  48.4 14.5 %all-to-all-done.1 = f32[16,1,32,384]{3,2,1,0:T(8,128)} async-done(((f32[16,1,32,384]{3,2,1,0:T(8,128)}), f32[16,1,32,384]{3,2,1,0:T(8,128)}, u32[]{:S(2)}, u32[]{:S(2)}) %all-to-all-start.1) | async-done | bytes 786464 | tf_op jit(solution)/shard_map/all_to_all | solution.py:42
  62.8 1.2 %reduce_sum.11 = f32[32,384]{1,0:T(8,128)S(1)} reduce(f32[16,1,32,384]{3,2,1,0:T(8,128)} %all-to-all-done.1, f32[]{:T(128)} %constant.25.clone.1), dimensions={0,1}, to_apply=%region_0.1 | reduce | flops 184320 | bytes 835588 | tf_op jit(solution)/shard_map/reduce_sum | solution.py:43
  64.0 0.1 slice_negate_fusion.4
  64.1 0.1 copy.79
  64.2 0.1 copy.70
  64.3 0.1 copy.71
  64.4 0.1 copy.72
  64.4 0.1 copy.77
  64.5 0.1 copy.78
  64.6 0.1 copy.68
  64.6 0.8 maximum_maximum_fusion.real_ref
  65.4 0.7 maximum_maximum_fusion.1.imag_ref
  66.1 10.0 %shard_map.38 = bf16[1,192,64]{2,1,0:T(8,128)(2,1)} custom-call(f32[1,96,96]{2,1,0:T(8,128)} %maximum_maximum_fusion.real_ref, f32[1,96,96]{2,1,0:T(8,128)} %maximum_maximum_fusion.1.imag_ref, f32[96,64]{1,0:T(8,128)} %bitcast.35, f32[96,64]{1,0:T(8,128)} %bitcast.34), custom_call_target="tpu_custom_call" | custom-call | tf_op jit(solution)/shard_map/pallas_call | solution.py:202
  76.1 0.9 copy.73
  77.1 14.3 %all_to_all.26 = bf16[16,1,192,64]{2,3,1,0:T(8,128)(2,1)} all-to-all(bf16[16,1,192,64]{2,3,1,0:T(8,128)(2,1)S(1)} %broadcast_in_dim.5), channel_id=1, replica_groups=mesh['dop'=8,'rng'=16] {'rng'}, dimensions={0} | all-to-all | bytes 786432 | tf_op jit(solution)/shard_map/all_to_all | solution.py:54
  91.4 2.2 %copy.74 = bf16[16,1,192,64]{3,2,0,1:T(8,128)(2,1)} copy(bf16[16,1,192,64]{2,3,1,0:T(8,128)(2,1)} %all_to_all.26) | data formatting | bytes 786432 | tf_op jit(solution)/shard_map/all_to_all | solution.py:54
  93.6 1.2 %slice_negate_fusion.1 = (bf16[16,3,1,32,64]{4,3,2,1,0:T(8,128)(2,1)S(1)}, bf16[16,3,1,32,64]{4,3,2,1,0:T(8,128)(2,1)S(1)}) fusion(bf16[16,3,2,32,64]{4,3,2,1,0:T(8,128)(2,1)} %bitcast.28), kind=kLoop, calls=%fused_computation.33 | loop fusion | flops 98304 | bytes 786432 | tf_op jit(solution)/shard_map/neg | solution.py:245
  94.8 0.2 pad_maximum_fusion.4
  95.0 4.3 %fusion.4 = f32[16,128,512]{2,1,0:T(8,128)} fusion(bf16[16,512,64]{1,2,0:T(8,128)(2,1)S(1)} %get-tuple-element.14, bf16[16,512,64]{1,2,0:T(8,128)(2,1)S(1)} %copy.57, bf16[16,512,64]{1,2,0:T(8,128)(2,1)S(1)} %get-tuple-element.13, bf16[16,192,64]{2,1,0:T(8,128)(2,1)S(1)} %bitcast.31, bf16[16,192,64]{2,1,0:T(8,128)(2,1)} %bitcast.29), kind=kOutput, calls=%fused_computation.5 | convolution fusion | flops 413663232 | bytes 8126464 | tf_op jit(solution)/shard_map/knj,krn->kjr/dot_general | solution.py:247
  (10 shorter events, 0.1 us)
Async XLA Ops:
  4.0 18.6 %all-to-all-start = ((bf16[8,16,4096]{2,1,0:T(8,128)(2,1)}), bf16[8,16,4096]{2,1,0:T(8,128)(2,1)S(1)}, u32[]{:S(2)}, u32[]{:S(2)}) async-start(bf16[8,16,4096]{2,1,0:T(8,128)(2,1)} %bitcast.27), calls=%async_computation | async-start | bytes 2097152 | tf_op jit(solution)/shard_map/all_to_all | solution.py:236
  23.4 7.7 %collective-permute-start = (bf16[1,512,64]{1,2,0:T(8,128)(2,1)S(1)}, bf16[1,512,64]{1,2,0:T(8,128)(2,1)S(1)}, u32[]{:S(2)}, u32[]{:S(2)}) collective-permute-start(bf16[1,512,64]{1,2,0:T(8,128)(2,1)S(1)} %copy.55), channel_id=1, source_target_pairs={{0,16},{16,32},{32,48},{48,64},{64,80},{80,96},{96,112},{112,0},{1... | collective-permute-start | bytes 196616 | tf_op jit(solution)/shard_map/ppermute | solution.py:26
  23.7 7.4 %collective-permute-start.1 = (bf16[1,512,64]{1,2,0:T(8,128)(2,1)S(1)}, bf16[1,512,64]{1,2,0:T(8,128)(2,1)S(1)}, u32[]{:S(2)}, u32[]{:S(2)}) collective-permute-start(bf16[1,512,64]{1,2,0:T(8,128)(2,1)S(1)} %copy.58), channel_id=1, source_target_pairs={{16,0},{32,16},{48,32},{64,48},{80,64},{96,80},{112,96},{0,112},{1... | collective-permute-start | bytes 196616 | tf_op jit(solution)/shard_map/ppermute | solution.py:29
  36.2 11.3 %copy-start = (s32[64]{0:T(128)S(1)}, s32[64]{0:T(128)}, u32[]{:S(2)}) copy-start(s32[64]{0:T(128)} %param.5) | copy-start | bytes 772
  39.6 23.2 %all-to-all-start.1 = ((f32[16,1,32,384]{3,2,1,0:T(8,128)}), f32[16,1,32,384]{3,2,1,0:T(8,128)}, u32[]{:S(2)}, u32[]{:S(2)}) async-start(f32[16,1,32,384]{3,2,1,0:T(8,128)} %maximum_bitcast_fusion), calls=%async_computation.1 | async-start | bytes 1572864 | tf_op jit(solution)/shard_map/all_to_all | solution.py:42

commit v15 on v12

--- a/solution.py
+++ b/solution.py
@@ -81,8 +81,16 @@
 def doppler_spectra(echo_rows, twiddle):
     rows = echo_rows.shape[0]
     paired = jnp.concatenate([twiddle[:PULSES], twiddle[PULSES:]], axis=1)
+    chunks = 4 if rows % 32 == 0 else 1
+    step = rows // chunks
     return pl.pallas_call(
         transform,
+        grid=(chunks,),
+        in_specs=[
+            pl.BlockSpec(paired.shape, lambda i: (0, 0)),
+            pl.BlockSpec((step, 2, CH, PULSES), lambda i: (i, 0, 0, 0)),
+        ],
+        out_specs=pl.BlockSpec((PULSES, step * 2 * CH), lambda i: (0, i)),
         out_shape=jax.ShapeDtypeStruct((PULSES, rows * 2 * CH), jnp.bfloat16),
     )(paired, echo_rows)
 

time: 95.7 us -> 96.7 us (1.010)
  no operation moved by 1% of the time
where the time goes in v15:
time: 96.7 us; the launch traced here: 96.1 us
  waiting for transfers between devices  28.1 us (29%)
  blocking collectives  15.1 us (16%)
  starting transfers between devices  14.3 us (15%)
  Pallas kernels  14 us (14%)
  matrix products  9.13 us (9%)
  other arithmetic  7.97 us (8%)
  local copies, waits for them, and re-layouts  7.3 us (8%)
    all_to_all x1, blocking collectives, copy_for_each(): lax.all_to_all(jnp.broadcast_to(array[None], (count, *array.shape)), axis...  15.1 us
    all_to_all x1, waiting for transfers between devices, sum_at_owner(): lax.all_to_all(blocks, axis, split_axis=0, concat_axis=0, tiled=True)  15 us
    all_to_all x1, waiting for transfers between devices, body(): lax.all_to_all(spectra, 'dop', split_axis=0, concat_axis=1, tiled=True)  13.1 us
    pallas_call x1, Pallas kernels, unit_vectors(): pl.pallas_call(eliminate, grid=(count,), in_specs=[matrix, matrix, vector...  10 us
    all_to_all x1, starting transfers between devices, sum_at_owner(): lax.all_to_all(blocks, axis, split_axis=0, concat_axis=0, tiled=True)  7.87 us
    dot_general x3, matrix products, body(): jnp.einsum('knj,krn->kjr', weights[:, position * 2 * CH:(position + 1) *...  4.9 us
    all_to_all x1, starting transfers between devices, body(): lax.all_to_all(spectra, 'dop', split_axis=0, concat_axis=1, tiled=True)  4.69 us
    dot_general x3, matrix products, upper_blocks(): jnp.einsum('krn,krm->knm', masked[:, :, left_pos * 2 * CH:left_pos * 2 *...  4.23 us
  transfers between devices with their start and end apart: 4, of which 2 were waited for; matrix products, arithmetic and copies ran while one was open for 6% of the time, Pallas kernels for 0%

profile of v15, /device:TPU:24, one launch (start us, length us, event | category | flops | bytes accessed | tf_op | source)
XLA Modules:
  0.0 96.1 jit_solution(6937941236554733489)
XLA Ops:
  0.0 0.3 sine_convert_fusion
  0.3 0.6 pad_maximum_fusion.10.twiddle_ref
  0.9 3.9 %shard_map.37 = bf16[128,4096]{1,0:T(8,128)(2,1)} custom-call(bf16[128,256]{1,0:T(8,128)(2,1)} %pad_maximum_fusion.10.twiddle_ref, bf16[64,2,32,128]{3,2,1,0:T(8,128)(2,1)} %echo_ref.1), custom_call_target="tpu_custom_call" | custom-call | tf_op jit(solution)/shard_map/pallas_call | solution.py:86
  4.9 4.7 %all-to-all-start = ((bf16[8,16,4096]{2,1,0:T(8,128)(2,1)}), bf16[8,16,4096]{2,1,0:T(8,128)(2,1)S(1)}, u32[]{:S(2)}, u32[]{:S(2)}) async-start(bf16[8,16,4096]{2,1,0:T(8,128)(2,1)} %bitcast.37), calls=%async_computation | async-start | bytes 2097152 | tf_op jit(solution)/shard_map/all_to_all | solution.py:244
  9.6 0.8 convert_element_type.20
  10.3 13.1 %all-to-all-done = bf16[8,16,4096]{2,1,0:T(8,128)(2,1)S(1)} async-done(((bf16[8,16,4096]{2,1,0:T(8,128)(2,1)}), bf16[8,16,4096]{2,1,0:T(8,128)(2,1)S(1)}, u32[]{:S(2)}, u32[]{:S(2)}) %all-to-all-start) | async-done | bytes 1048608 | tf_op jit(solution)/shard_map/all_to_all | solution.py:244
  23.4 0.6 slice_reduce_fusion
  24.0 0.2 slice.154
  24.2 0.1 copy.57
  24.3 0.0 collective-permute-start
  24.3 0.2 slice.157
  24.5 0.1 copy.60
  24.6 1.7 %collective-permute-start.1 = (bf16[1,512,64]{1,2,0:T(8,128)(2,1)S(1)}, bf16[1,512,64]{1,2,0:T(8,128)(2,1)S(1)}, u32[]{:S(2)}, u32[]{:S(2)}) collective-permute-start(bf16[1,512,64]{1,2,0:T(8,128)(2,1)S(1)} %copy.60), channel_id=1, source_target_pairs={{16,0},{32,16},{48,32},{64,48},{80,64},{96,80},{112,96},{0,112},{1... | collective-permute-start | bytes 196616 | tf_op jit(solution)/shard_map/ppermute | solution.py:29
  26.3 0.6 copy.58
  26.9 2.3 %reshape.121 = bf16[16,512,64]{2,1,0:T(8,128)(2,1)S(1)} reshape(bf16[16,8,4096]{2,1,0:T(8,128)(2,1)S(1)} %copy.58) | data formatting | bytes 2097152 | tf_op jit(solution)/shard_map/reshape | solution.py:245
  29.2 0.8 copy.59
  30.1 0.2 pad_maximum_fusion.1
  30.3 0.1 slice_negate_fusion
  30.3 0.3 fusion.7
  30.6 0.1 pad_maximum_fusion.2
  30.8 2.4 %broadcast_multiply_fusion = (bf16[16,1024,192]{1,2,0:T(8,128)(2,1)S(1)}, bf16[16,1024,192]{1,2,0:T(8,128)(2,1)S(1)}) fusion(bf16[16,1024]{1,0:T(8,128)(2,1)S(1)} %pad_maximum_fusion.11, bf16[18,512,32]{1,2,0:T(8,128)(2,1)S(1)} %get-tuple-element.12, bf16[18,512,32]{1,2,0:T(8,128)(2,1)S(1)} %get-tuple-element.11, ...), kind=kLoop, calls=%fused_computation.6 | loop fusion | flops 53477376 | bytes 19038208 | tf_op jit(solution)/shard_map/mul | solution.py:118
  33.2 2.0 %fusion.10 = f32[16,32,192]{2,1,0:T(8,128)S(1)} fusion(bf16[16,1024,192]{1,2,0:T(8,128)(2,1)S(1)} %get-tuple-element.8, bf16[16,1024,192]{1,2,0:T(8,128)(2,1)S(1)} %get-tuple-element.7), kind=kOutput, calls=%fused_computation.18 | convolution fusion | flops 201326592 | bytes 7733248 | tf_op jit(solution)/shard_map/krn,krm->knm/dot_general | solution.py:122
  35.3 1.5 %fusion.2 = f32[16,32,128]{2,1,0:T(8,128)S(1)} fusion(bf16[16,1024,192]{1,2,0:T(8,128)(2,1)S(1)} %get-tuple-element.8, bf16[16,1024,192]{1,2,0:T(8,128)(2,1)S(1)} %get-tuple-element.7), kind=kOutput, calls=%fused_computation.3 | convolution fusion | flops 134217728 | bytes 5505024 | tf_op jit(solution)/shard_map/krn,krm->knm/dot_general | solution.py:122
  36.8 0.7 fusion.4
  37.5 1.2 %maximum_bitcast_fusion = f32[16,1,32,384]{3,2,1,0:T(8,128)} fusion(f32[16,32,64]{2,1,0:T(8,128)S(1)} %fusion.4, f32[16,32,128]{2,1,0:T(8,128)S(1)} %fusion.2, f32[16,32,192]{2,1,0:T(8,128)S(1)} %fusion.10), kind=kLoop, calls=%fused_computation.22 | loop fusion | flops 393216 | bytes 1572864 | tf_op jit(solution)/shard_map/reshape | solution.py:36
  38.7 7.9 %all-to-all-start.1 = ((f32[16,1,32,384]{3,2,1,0:T(8,128)}), f32[16,1,32,384]{3,2,1,0:T(8,128)S(1)}, u32[]{:S(2)}, u32[]{:S(2)}) async-start(f32[16,1,32,384]{3,2,1,0:T(8,128)} %maximum_bitcast_fusion), calls=%async_computation.1 | async-start | bytes 1572864 | tf_op jit(solution)/shard_map/all_to_all | solution.py:42
  46.6 0.1 multiply_cosine_fusion
  46.8 0.6 fusion.30
  47.4 15.0 %all-to-all-done.1 = f32[16,1,32,384]{3,2,1,0:T(8,128)S(1)} async-done(((f32[16,1,32,384]{3,2,1,0:T(8,128)}), f32[16,1,32,384]{3,2,1,0:T(8,128)S(1)}, u32[]{:S(2)}, u32[]{:S(2)}) %all-to-all-start.1) | async-done | bytes 786464 | tf_op jit(solution)/shard_map/all_to_all | solution.py:42
  62.4 0.1 slice_negate_fusion.4
  62.5 0.1 copy.83
  62.6 0.1 copy.72
  62.7 0.1 copy.73
  62.8 0.1 copy.74
  62.8 0.1 copy.81
  62.9 0.1 copy.82
  63.0 0.1 copy.70
  63.1 0.7 maximum_maximum_fusion.real_ref
  63.8 0.7 maximum_maximum_fusion.1.imag_ref
  64.5 10.0 %shard_map.38 = bf16[1,192,64]{2,1,0:T(8,128)(2,1)} custom-call(f32[1,96,96]{2,1,0:T(8,128)} %maximum_maximum_fusion.real_ref, f32[1,96,96]{2,1,0:T(8,128)} %maximum_maximum_fusion.1.imag_ref, f32[96,64]{1,0:T(8,128)} %bitcast.42, f32[96,64]{1,0:T(8,128)} %bitcast.41), custom_call_target="tpu_custom_call" | custom-call | tf_op jit(solution)/shard_map/pallas_call | solution.py:210
  74.5 0.9 copy.75
  75.5 15.1 %all_to_all.26 = bf16[16,1,192,64]{2,3,1,0:T(8,128)(2,1)S(1)} all-to-all(bf16[16,1,192,64]{2,3,1,0:T(8,128)(2,1)S(1)} %broadcast_in_dim.5), channel_id=1, replica_groups=mesh['dop'=8,'rng'=16] {'rng'}, dimensions={0} | all-to-all | bytes 786432 | tf_op jit(solution)/shard_map/all_to_all | solution.py:54
  90.5 0.4 copy.76
  90.9 0.1 slice_negate_fusion.1
  91.0 0.2 pad_maximum_fusion.4
  91.2 1.2 %fusion.13 = f32[16,128,512]{2,1,0:T(8,128)S(1)} fusion(bf16[16,512,64]{2,1,0:T(8,128)(2,1)S(1)} %reshape.121, bf16[16,192,64]{2,1,0:T(8,128)(2,1)S(1)} %bitcast.29, bf16[16,192,64]{2,1,0:T(8,128)(2,1)S(1)} %bitcast.32), kind=kOutput, calls=%fused_computation.31 | convolution fusion | flops 134742016 | bytes 6029312 | tf_op jit(solution)/shard_map/knj,krn->kjr/dot_general | solution.py:257
  92.4 0.8 fusion.16
  93.3 2.9 %add_add_fusion = f32[16,128,512]{2,1,0:T(8,128)} fusion(f32[16,128,512]{2,1,0:T(8,128)S(1)} %fusion.16, f32[16,128,512]{2,1,0:T(8,128)S(1)} %fusion.13, bf16[16,512,64]{1,2,0:T(8,128)(2,1)S(1)} %copy-done.3, bf16[16,192,64]{2,1,0:T(8,128)(2,1)S(1)} %bitcast.34, bf16[16,192,64]{2,1,0:T(8,128)(2,1)S(1)} %bitcast.31), kind=kOutput, calls=%fused_computation.5 | convolution fusion | flops 136839168 | bytes 14417920 | tf_op jit(solution)/shard_map/knj,krn->kjr/dot_general | solution.py:257
  (20 shorter events, 0.2 us)
Async XLA Ops:
  4.9 18.6 %all-to-all-start = ((bf16[8,16,4096]{2,1,0:T(8,128)(2,1)}), bf16[8,16,4096]{2,1,0:T(8,128)(2,1)S(1)}, u32[]{:S(2)}, u32[]{:S(2)}) async-start(bf16[8,16,4096]{2,1,0:T(8,128)(2,1)} %bitcast.37), calls=%async_computation | async-start | bytes 2097152 | tf_op jit(solution)/shard_map/all_to_all | solution.py:244
  24.3 5.8 %collective-permute-start = (bf16[1,512,64]{1,2,0:T(8,128)(2,1)S(1)}, bf16[1,512,64]{1,2,0:T(8,128)(2,1)S(1)}, u32[]{:S(2)}, u32[]{:S(2)}) collective-permute-start(bf16[1,512,64]{1,2,0:T(8,128)(2,1)S(1)} %copy.57), channel_id=1, source_target_pairs={{0,16},{16,32},{32,48},{48,64},{64,80},{80,96},{96,112},{112,0},{1... | collective-permute-start | bytes 196616 | tf_op jit(solution)/shard_map/ppermute | solution.py:26
  24.6 5.5 %collective-permute-start.1 = (bf16[1,512,64]{1,2,0:T(8,128)(2,1)S(1)}, bf16[1,512,64]{1,2,0:T(8,128)(2,1)S(1)}, u32[]{:S(2)}, u32[]{:S(2)}) collective-permute-start(bf16[1,512,64]{1,2,0:T(8,128)(2,1)S(1)} %copy.60), channel_id=1, source_target_pairs={{16,0},{32,16},{48,32},{64,48},{80,64},{96,80},{112,96},{0,112},{1... | collective-permute-start | bytes 196616 | tf_op jit(solution)/shard_map/ppermute | solution.py:29
  30.8 2.4 %copy-start = (bf16[16,512,64]{1,2,0:T(8,128)(2,1)}, bf16[16,512,64]{1,2,0:T(8,128)(2,1)S(1)}, u32[]{:S(2)}) copy-start(bf16[16,512,64]{1,2,0:T(8,128)(2,1)S(1)} %get-tuple-element.14) | copy-start | bytes 3145732
  30.8 2.4 %copy-start.2 = (bf16[16,512,64]{1,2,0:T(8,128)(2,1)}, bf16[16,512,64]{1,2,0:T(8,128)(2,1)S(1)}, u32[]{:S(2)}) copy-start(bf16[16,512,64]{1,2,0:T(8,128)(2,1)S(1)} %get-tuple-element.13) | copy-start | bytes 3145732
  35.3 11.3 %copy-start.4 = (s32[64]{0:T(128)S(1)}, s32[64]{0:T(128)}, u32[]{:S(2)}) copy-start(s32[64]{0:T(128)} %param.5) | copy-start | bytes 772
  38.7 23.7 %all-to-all-start.1 = ((f32[16,1,32,384]{3,2,1,0:T(8,128)}), f32[16,1,32,384]{3,2,1,0:T(8,128)S(1)}, u32[]{:S(2)}, u32[]{:S(2)}) async-start(f32[16,1,32,384]{3,2,1,0:T(8,128)} %maximum_bitcast_fusion), calls=%async_computation.1 | async-start | bytes 1572864 | tf_op jit(solution)/shard_map/all_to_all | solution.py:42
  90.9 1.5 %copy-start.1 = (bf16[16,512,64]{1,2,0:T(8,128)(2,1)S(1)}, bf16[16,512,64]{1,2,0:T(8,128)(2,1)}, u32[]{:S(2)}) copy-start(bf16[16,512,64]{1,2,0:T(8,128)(2,1)} %copy-done) | copy-start | bytes 3145732
  91.2 2.1 %copy-start.3 = (bf16[16,512,64]{1,2,0:T(8,128)(2,1)S(1)}, bf16[16,512,64]{1,2,0:T(8,128)(2,1)}, u32[]{:S(2)}) copy-start(bf16[16,512,64]{1,2,0:T(8,128)(2,1)} %copy-done.2) | copy-start | bytes 3145732

commit v16 on v12

--- a/solution.py
+++ b/solution.py
@@ -67,24 +67,24 @@
     return jnp.concatenate([jnp.cos(angles), jnp.sin(angles)], axis=0).astype(jnp.bfloat16)
 
 
-def transform(twiddle_ref, echo_ref, out_ref):
+def transform(cosine_ref, sine_ref, echo_ref, out_ref):
     rows = echo_ref.shape[0]
     echoes = echo_ref[...]
     swapped = jnp.stack([echoes[:, 1], -echoes[:, 0]], axis=1)
     stacked = jnp.concatenate(
         [echoes.reshape(rows * 2 * CH, PULSES), swapped.reshape(rows * 2 * CH, PULSES)], axis=1
     )
+    paired = jnp.concatenate([cosine_ref[...], sine_ref[...]], axis=1)
     out_ref[...] = lax.dot_general(
-        twiddle_ref[...], stacked, (((1,), (1,)), ((), ())), preferred_element_type=jnp.float32
+        paired, stacked, (((1,), (1,)), ((), ())), preferred_element_type=jnp.float32
     ).astype(out_ref.dtype)
 
 def doppler_spectra(echo_rows, twiddle):
     rows = echo_rows.shape[0]
-    paired = jnp.concatenate([twiddle[:PULSES], twiddle[PULSES:]], axis=1)
     return pl.pallas_call(
         transform,
         out_shape=jax.ShapeDtypeStruct((PULSES, rows * 2 * CH), jnp.bfloat16),
-    )(paired, echo_rows)
+    )(twiddle[:PULSES], twiddle[PULSES:], echo_rows)
 
 def steering(look_index):
     sines = -1.0 + (2.0 * look_index.astype(jnp.float32) + 1.0) / ANGLES

time: 95.7 us -> 95.7 us (level)
  no operation moved by 1% of the time
where the time goes in v16:
time: 95.7 us; the launch traced here: 95.2 us
  waiting for transfers between devices  28.1 us (29%)
  blocking collectives  15.1 us (16%)
  starting transfers between devices  14.3 us (15%)
  Pallas kernels  13.1 us (14%)
  matrix products  9.13 us (10%)
  other arithmetic  7.96 us (8%)
  local copies, waits for them, and re-layouts  7.3 us (8%)
    all_to_all x1, blocking collectives, copy_for_each(): lax.all_to_all(jnp.broadcast_to(array[None], (count, *array.shape)), axis...  15.1 us
    all_to_all x1, waiting for transfers between devices, sum_at_owner(): lax.all_to_all(blocks, axis, split_axis=0, concat_axis=0, tiled=True)  15 us
    all_to_all x1, waiting for transfers between devices, body(): lax.all_to_all(spectra, 'dop', split_axis=0, concat_axis=1, tiled=True)  13.1 us
    pallas_call x1, Pallas kernels, unit_vectors(): pl.pallas_call(eliminate, grid=(count,), in_specs=[matrix, matrix, vector...  10 us
    all_to_all x1, starting transfers between devices, sum_at_owner(): lax.all_to_all(blocks, axis, split_axis=0, concat_axis=0, tiled=True)  7.88 us
    dot_general x3, matrix products, body(): jnp.einsum('knj,krn->kjr', weights[:, position * 2 * CH:(position + 1) *...  4.9 us
    all_to_all x1, starting transfers between devices, body(): lax.all_to_all(spectra, 'dop', split_axis=0, concat_axis=1, tiled=True)  4.69 us
    dot_general x3, matrix products, upper_blocks(): jnp.einsum('krn,krm->knm', masked[:, :, left_pos * 2 * CH:left_pos * 2 *...  4.23 us
  transfers between devices with their start and end apart: 4, of which 2 were waited for; matrix products, arithmetic and copies ran while one was open for 6% of the time, Pallas kernels for 0%

profile of v16, /device:TPU:24, one launch (start us, length us, event | category | flops | bytes accessed | tf_op | source)
XLA Modules:
  0.0 95.2 jit_solution(17984685817080354421)
XLA Ops:
  0.0 0.9 sine_convert_fusion
  0.9 3.0 %shard_map.37 = bf16[128,4096]{1,0:T(8,128)(2,1)} custom-call(bf16[128,128]{1,0:T(8,128)(2,1)} %get-tuple-element.37.cosine_ref, bf16[128,128]{1,0:T(8,128)(2,1)} %get-tuple-element.36.sine_ref, bf16[64,2,32,128]{3,2,1,0:T(8,128)(2,1)} %echo_ref.1), custom_call_target="tpu_custom_call" | custom-call | tf_op jit(solution)/shard_map/pallas_call | solution.py:84
  4.0 4.7 %all-to-all-start = ((bf16[8,16,4096]{2,1,0:T(8,128)(2,1)}), bf16[8,16,4096]{2,1,0:T(8,128)(2,1)S(1)}, u32[]{:S(2)}, u32[]{:S(2)}) async-start(bf16[8,16,4096]{2,1,0:T(8,128)(2,1)} %bitcast.37), calls=%async_computation | async-start | bytes 2097152 | tf_op jit(solution)/shard_map/all_to_all | solution.py:236
  8.7 0.8 convert_element_type.20
  9.4 13.1 %all-to-all-done = bf16[8,16,4096]{2,1,0:T(8,128)(2,1)S(1)} async-done(((bf16[8,16,4096]{2,1,0:T(8,128)(2,1)}), bf16[8,16,4096]{2,1,0:T(8,128)(2,1)S(1)}, u32[]{:S(2)}, u32[]{:S(2)}) %all-to-all-start) | async-done | bytes 1048608 | tf_op jit(solution)/shard_map/all_to_all | solution.py:236
  22.5 0.6 slice_reduce_fusion
  23.1 0.2 slice.154
  23.3 0.1 copy.57
  23.4 0.0 collective-permute-start
  23.4 0.2 slice.157
  23.6 0.1 copy.60
  23.7 1.7 %collective-permute-start.1 = (bf16[1,512,64]{1,2,0:T(8,128)(2,1)S(1)}, bf16[1,512,64]{1,2,0:T(8,128)(2,1)S(1)}, u32[]{:S(2)}, u32[]{:S(2)}) collective-permute-start(bf16[1,512,64]{1,2,0:T(8,128)(2,1)S(1)} %copy.60), channel_id=1, source_target_pairs={{16,0},{32,16},{48,32},{64,48},{80,64},{96,80},{112,96},{0,112},{1... | collective-permute-start | bytes 196616 | tf_op jit(solution)/shard_map/ppermute | solution.py:29
  25.4 0.6 copy.58
  26.0 2.3 %reshape.121 = bf16[16,512,64]{2,1,0:T(8,128)(2,1)S(1)} reshape(bf16[16,8,4096]{2,1,0:T(8,128)(2,1)S(1)} %copy.58) | data formatting | bytes 2097152 | tf_op jit(solution)/shard_map/reshape | solution.py:237
  28.3 0.8 copy.59
  29.2 0.2 pad_maximum_fusion.1
  29.3 0.1 slice_negate_fusion
  29.4 0.3 fusion.7
  29.7 0.1 pad_maximum_fusion.2
  29.9 0.0 copy-start
  29.9 2.4 %broadcast_multiply_fusion = (bf16[16,1024,192]{1,2,0:T(8,128)(2,1)S(1)}, bf16[16,1024,192]{1,2,0:T(8,128)(2,1)S(1)}) fusion(bf16[16,1024]{1,0:T(8,128)(2,1)S(1)} %pad_maximum_fusion.10, bf16[18,512,32]{1,2,0:T(8,128)(2,1)S(1)} %get-tuple-element.12, bf16[18,512,32]{1,2,0:T(8,128)(2,1)S(1)} %get-tuple-element.11, ...), kind=kLoop, calls=%fused_computation.6 | loop fusion | flops 53477376 | bytes 19038208 | tf_op jit(solution)/shard_map/mul | solution.py:110
  32.3 2.0 %fusion.10 = f32[16,32,192]{2,1,0:T(8,128)S(1)} fusion(bf16[16,1024,192]{1,2,0:T(8,128)(2,1)S(1)} %get-tuple-element.8, bf16[16,1024,192]{1,2,0:T(8,128)(2,1)S(1)} %get-tuple-element.7), kind=kOutput, calls=%fused_computation.18 | convolution fusion | flops 201326592 | bytes 7733248 | tf_op jit(solution)/shard_map/krn,krm->knm/dot_general | solution.py:114
  34.4 1.5 %fusion.2 = f32[16,32,128]{2,1,0:T(8,128)S(1)} fusion(bf16[16,1024,192]{1,2,0:T(8,128)(2,1)S(1)} %get-tuple-element.8, bf16[16,1024,192]{1,2,0:T(8,128)(2,1)S(1)} %get-tuple-element.7), kind=kOutput, calls=%fused_computation.3 | convolution fusion | flops 134217728 | bytes 5505024 | tf_op jit(solution)/shard_map/krn,krm->knm/dot_general | solution.py:114
  35.9 0.7 fusion.4
  36.6 1.2 %maximum_bitcast_fusion = f32[16,1,32,384]{3,2,1,0:T(8,128)} fusion(f32[16,32,64]{2,1,0:T(8,128)S(1)} %fusion.4, f32[16,32,128]{2,1,0:T(8,128)S(1)} %fusion.2, f32[16,32,192]{2,1,0:T(8,128)S(1)} %fusion.10), kind=kLoop, calls=%fused_computation.22 | loop fusion | flops 393216 | bytes 1572864 | tf_op jit(solution)/shard_map/reshape | solution.py:36
  37.8 7.9 %all-to-all-start.1 = ((f32[16,1,32,384]{3,2,1,0:T(8,128)}), f32[16,1,32,384]{3,2,1,0:T(8,128)S(1)}, u32[]{:S(2)}, u32[]{:S(2)}) async-start(f32[16,1,32,384]{3,2,1,0:T(8,128)} %maximum_bitcast_fusion), calls=%async_computation.1 | async-start | bytes 1572864 | tf_op jit(solution)/shard_map/all_to_all | solution.py:42
  45.7 0.1 multiply_cosine_fusion
  45.9 0.6 fusion.30
  46.5 15.0 %all-to-all-done.1 = f32[16,1,32,384]{3,2,1,0:T(8,128)S(1)} async-done(((f32[16,1,32,384]{3,2,1,0:T(8,128)}), f32[16,1,32,384]{3,2,1,0:T(8,128)S(1)}, u32[]{:S(2)}, u32[]{:S(2)}) %all-to-all-start.1) | async-done | bytes 786464 | tf_op jit(solution)/shard_map/all_to_all | solution.py:42
  61.5 0.1 slice_negate_fusion.4
  61.6 0.1 copy.83
  61.7 0.1 copy.72
  61.8 0.1 copy.73
  61.9 0.1 copy.74
  61.9 0.1 copy.81
  62.0 0.1 copy.82
  62.1 0.1 copy.70
  62.2 0.7 maximum_maximum_fusion.real_ref
  62.9 0.7 maximum_maximum_fusion.1.imag_ref
  63.6 10.0 %shard_map.38 = bf16[1,192,64]{2,1,0:T(8,128)(2,1)} custom-call(f32[1,96,96]{2,1,0:T(8,128)} %maximum_maximum_fusion.real_ref, f32[1,96,96]{2,1,0:T(8,128)} %maximum_maximum_fusion.1.imag_ref, f32[96,64]{1,0:T(8,128)} %bitcast.42, f32[96,64]{1,0:T(8,128)} %bitcast.41), custom_call_target="tpu_custom_call" | custom-call | tf_op jit(solution)/shard_map/pallas_call | solution.py:202
  73.6 0.9 copy.75
  74.6 15.1 %all_to_all.26 = bf16[16,1,192,64]{2,3,1,0:T(8,128)(2,1)S(1)} all-to-all(bf16[16,1,192,64]{2,3,1,0:T(8,128)(2,1)S(1)} %broadcast_in_dim.5), channel_id=1, replica_groups=mesh['dop'=8,'rng'=16] {'rng'}, dimensions={0} | all-to-all | bytes 786432 | tf_op jit(solution)/shard_map/all_to_all | solution.py:54
  89.6 0.4 copy.76
  90.0 0.1 slice_negate_fusion.1
  90.1 0.2 pad_maximum_fusion.4
  90.3 1.2 %fusion.13 = f32[16,128,512]{2,1,0:T(8,128)S(1)} fusion(bf16[16,512,64]{2,1,0:T(8,128)(2,1)S(1)} %reshape.121, bf16[16,192,64]{2,1,0:T(8,128)(2,1)S(1)} %bitcast.29, bf16[16,192,64]{2,1,0:T(8,128)(2,1)S(1)} %bitcast.32), kind=kOutput, calls=%fused_computation.31 | convolution fusion | flops 134742016 | bytes 6029312 | tf_op jit(solution)/shard_map/knj,krn->kjr/dot_general | solution.py:249
  91.5 0.8 fusion.16
  92.4 2.9 %add_add_fusion = f32[16,128,512]{2,1,0:T(8,128)} fusion(f32[16,128,512]{2,1,0:T(8,128)S(1)} %fusion.16, f32[16,128,512]{2,1,0:T(8,128)S(1)} %fusion.13, bf16[16,512,64]{1,2,0:T(8,128)(2,1)S(1)} %copy-done.3, bf16[16,192,64]{2,1,0:T(8,128)(2,1)S(1)} %bitcast.34, bf16[16,192,64]{2,1,0:T(8,128)(2,1)S(1)} %bitcast.31), kind=kOutput, calls=%fused_computation.5 | convolution fusion | flops 136839168 | bytes 14417920 | tf_op jit(solution)/shard_map/knj,krn->kjr/dot_general | solution.py:249
  (19 shorter events, 0.2 us)
Async XLA Ops:
  4.0 18.6 %all-to-all-start = ((bf16[8,16,4096]{2,1,0:T(8,128)(2,1)}), bf16[8,16,4096]{2,1,0:T(8,128)(2,1)S(1)}, u32[]{:S(2)}, u32[]{:S(2)}) async-start(bf16[8,16,4096]{2,1,0:T(8,128)(2,1)} %bitcast.37), calls=%async_computation | async-start | bytes 2097152 | tf_op jit(solution)/shard_map/all_to_all | solution.py:236
  23.4 5.8 %collective-permute-start = (bf16[1,512,64]{1,2,0:T(8,128)(2,1)S(1)}, bf16[1,512,64]{1,2,0:T(8,128)(2,1)S(1)}, u32[]{:S(2)}, u32[]{:S(2)}) collective-permute-start(bf16[1,512,64]{1,2,0:T(8,128)(2,1)S(1)} %copy.57), channel_id=1, source_target_pairs={{0,16},{16,32},{32,48},{48,64},{64,80},{80,96},{96,112},{112,0},{1... | collective-permute-start | bytes 196616 | tf_op jit(solution)/shard_map/ppermute | solution.py:26
  23.7 5.5 %collective-permute-start.1 = (bf16[1,512,64]{1,2,0:T(8,128)(2,1)S(1)}, bf16[1,512,64]{1,2,0:T(8,128)(2,1)S(1)}, u32[]{:S(2)}, u32[]{:S(2)}) collective-permute-start(bf16[1,512,64]{1,2,0:T(8,128)(2,1)S(1)} %copy.60), channel_id=1, source_target_pairs={{16,0},{32,16},{48,32},{64,48},{80,64},{96,80},{112,96},{0,112},{1... | collective-permute-start | bytes 196616 | tf_op jit(solution)/shard_map/ppermute | solution.py:29
  29.9 2.4 %copy-start = (bf16[16,512,64]{1,2,0:T(8,128)(2,1)}, bf16[16,512,64]{1,2,0:T(8,128)(2,1)S(1)}, u32[]{:S(2)}) copy-start(bf16[16,512,64]{1,2,0:T(8,128)(2,1)S(1)} %get-tuple-element.14) | copy-start | bytes 3145732
  29.9 2.4 %copy-start.2 = (bf16[16,512,64]{1,2,0:T(8,128)(2,1)}, bf16[16,512,64]{1,2,0:T(8,128)(2,1)S(1)}, u32[]{:S(2)}) copy-start(bf16[16,512,64]{1,2,0:T(8,128)(2,1)S(1)} %get-tuple-element.13) | copy-start | bytes 3145732
  34.4 11.3 %copy-start.4 = (s32[64]{0:T(128)S(1)}, s32[64]{0:T(128)}, u32[]{:S(2)}) copy-start(s32[64]{0:T(128)} %param.5) | copy-start | bytes 772
  37.8 23.7 %all-to-all-start.1 = ((f32[16,1,32,384]{3,2,1,0:T(8,128)}), f32[16,1,32,384]{3,2,1,0:T(8,128)S(1)}, u32[]{:S(2)}, u32[]{:S(2)}) async-start(f32[16,1,32,384]{3,2,1,0:T(8,128)} %maximum_bitcast_fusion), calls=%async_computation.1 | async-start | bytes 1572864 | tf_op jit(solution)/shard_map/all_to_all | solution.py:42
  90.0 1.5 %copy-start.1 = (bf16[16,512,64]{1,2,0:T(8,128)(2,1)S(1)}, bf16[16,512,64]{1,2,0:T(8,128)(2,1)}, u32[]{:S(2)}) copy-start(bf16[16,512,64]{1,2,0:T(8,128)(2,1)} %copy-done) | copy-start | bytes 3145732
  90.3 2.1 %copy-start.3 = (bf16[16,512,64]{1,2,0:T(8,128)(2,1)S(1)}, bf16[16,512,64]{1,2,0:T(8,128)(2,1)}, u32[]{:S(2)}) copy-start(bf16[16,512,64]{1,2,0:T(8,128)(2,1)} %copy-done.2) | copy-start | bytes 3145732

commit v17 on v16

--- a/solution.py
+++ b/solution.py
@@ -121,20 +121,20 @@
     return jnp.concatenate(pieces, axis=-1)
 
 
-def eliminate(real_ref, imag_ref, steer_re_ref, steer_im_ref, unit_ref, wr_ref, wi_ref):
+def eliminate(parts_ref, steer_re_ref, steer_im_ref, unit_ref, wr_ref, wi_ref):
     rows, cols = wr_ref.shape
     gap = cols - LOOKS
     lane_ids = lax.broadcasted_iota(jnp.int32, (1, cols), 1)
     row_ids = lax.broadcasted_iota(jnp.int32, (rows, 1), 0)
     diagonal = row_ids == lax.broadcasted_iota(jnp.int32, (1, rows), 1)
-    same = real_ref[0]
+    same = parts_ref[0, 0]
     power = 2.0 * jnp.sum(jnp.where(diagonal, same, 0.0)) / SNAP + epsilon
     steer_re = steer_re_ref[...]
     steer_im = steer_im_ref[...]
     wr_ref[...] = jnp.zeros(wr_ref.shape, jnp.float32)
     wi_ref[...] = jnp.zeros(wi_ref.shape, jnp.float32)
     wr_ref[:, :rows] = same / power + jnp.where(diagonal, loading, 0.0)
-    wi_ref[:, :rows] = imag_ref[0] / power
+    wi_ref[:, :rows] = parts_ref[0, 1] / power
     wr_ref[:, gap:] = steer_re
     wi_ref[:, gap:] = steer_im
 
@@ -193,20 +193,20 @@
 
 def unit_vectors(same, cross, steer):
     count, size, _ = same.shape
-    parts = steer.reshape(size // CH, 2, CH, LOOKS)
-    steer_re = parts[:, 0].reshape(size, LOOKS)
-    steer_im = parts[:, 1].reshape(size, LOOKS)
+    parts = jnp.stack([same, cross], axis=1)
+    halves = steer.reshape(size // CH, 2, CH, LOOKS)
+    steer_re = halves[:, 0].reshape(size, LOOKS)
+    steer_im = halves[:, 1].reshape(size, LOOKS)
     width = ((size + 127) // 128) * 128 + LOOKS
-    matrix = pl.BlockSpec((1, size, size), lambda i: (i, 0, 0))
     vector = pl.BlockSpec((size, LOOKS), lambda i: (0, 0))
     return pl.pallas_call(
         eliminate,
         grid=(count,),
-        in_specs=[matrix, matrix, vector, vector],
+        in_specs=[pl.BlockSpec((1, 2, size, size), lambda i: (i, 0, 0, 0)), vector, vector],
         out_specs=pl.BlockSpec((1, 2 * size, LOOKS), lambda i: (i, 0, 0)),
         out_shape=jax.ShapeDtypeStruct((count, 2 * size, LOOKS), jnp.bfloat16),
         scratch_shapes=[pltpu.VMEM((size, width), jnp.float32)] * 2,
-    )(same, cross, steer_re, steer_im)
+    )(parts, steer_re, steer_im)
 
 
 def hermitian_parts(upper):

time: 95.7 us -> 95.2 us (level)
    concatenate x2 -> x0, other arithmetic: 1.45 us -> none  [assemble(): return jnp.concatenate(rows, 1)]
where the time goes in v17:
time: 95.2 us; the launch traced here: 94.7 us
  waiting for transfers between devices  28.1 us (30%)
  blocking collectives  15.1 us (16%)
  starting transfers between devices  14.3 us (15%)
  Pallas kernels  13.1 us (14%)
  matrix products  9.14 us (10%)
  other arithmetic  7.36 us (8%)
  local copies, waits for them, and re-layouts  7.31 us (8%)
    all_to_all x1, blocking collectives, copy_for_each(): lax.all_to_all(jnp.broadcast_to(array[None], (count, *array.shape)), axis...  15.1 us
    all_to_all x1, waiting for transfers between devices, sum_at_owner(): lax.all_to_all(blocks, axis, split_axis=0, concat_axis=0, tiled=True)  15 us
    all_to_all x1, waiting for transfers between devices, body(): lax.all_to_all(spectra, 'dop', split_axis=0, concat_axis=1, tiled=True)  13.1 us
    pallas_call x1, Pallas kernels, unit_vectors(): pl.pallas_call(eliminate, grid=(count,), in_specs=[pl.BlockSpec((1, 2, si...  10.1 us
    all_to_all x1, starting transfers between devices, sum_at_owner(): lax.all_to_all(blocks, axis, split_axis=0, concat_axis=0, tiled=True)  7.88 us
    dot_general x3, matrix products, body(): jnp.einsum('knj,krn->kjr', weights[:, position * 2 * CH:(position + 1) *...  4.91 us
    all_to_all x1, starting transfers between devices, body(): lax.all_to_all(spectra, 'dop', split_axis=0, concat_axis=1, tiled=True)  4.69 us
    dot_general x3, matrix products, upper_blocks(): jnp.einsum('krn,krm->knm', masked[:, :, left_pos * 2 * CH:left_pos * 2 *...  4.23 us
  transfers between devices with their start and end apart: 4, of which 2 were waited for; matrix products, arithmetic and copies ran while one was open for 6% of the time, Pallas kernels for 0%

profile of v17, /device:TPU:24, one launch (start us, length us, event | category | flops | bytes accessed | tf_op | source)
XLA Modules:
  0.0 94.7 jit_solution(15032094953939946272)
XLA Ops:
  0.0 0.9 sine_convert_fusion
  0.9 3.0 %shard_map.37 = bf16[128,4096]{1,0:T(8,128)(2,1)} custom-call(bf16[128,128]{1,0:T(8,128)(2,1)} %get-tuple-element.37.cosine_ref, bf16[128,128]{1,0:T(8,128)(2,1)} %get-tuple-element.36.sine_ref, bf16[64,2,32,128]{3,2,1,0:T(8,128)(2,1)} %echo_ref.1), custom_call_target="tpu_custom_call" | custom-call | tf_op jit(solution)/shard_map/pallas_call | solution.py:84
  4.0 4.7 %all-to-all-start = ((bf16[8,16,4096]{2,1,0:T(8,128)(2,1)}), bf16[8,16,4096]{2,1,0:T(8,128)(2,1)S(1)}, u32[]{:S(2)}, u32[]{:S(2)}) async-start(bf16[8,16,4096]{2,1,0:T(8,128)(2,1)} %bitcast.41), calls=%async_computation | async-start | bytes 2097152 | tf_op jit(solution)/shard_map/all_to_all | solution.py:236
  8.7 0.8 convert_element_type.20
  9.4 13.1 %all-to-all-done = bf16[8,16,4096]{2,1,0:T(8,128)(2,1)S(1)} async-done(((bf16[8,16,4096]{2,1,0:T(8,128)(2,1)}), bf16[8,16,4096]{2,1,0:T(8,128)(2,1)S(1)}, u32[]{:S(2)}, u32[]{:S(2)}) %all-to-all-start) | async-done | bytes 1048608 | tf_op jit(solution)/shard_map/all_to_all | solution.py:236
  22.5 0.6 slice_reduce_fusion
  23.1 0.2 slice.154
  23.3 0.1 copy.57
  23.4 0.0 collective-permute-start
  23.4 0.2 slice.157
  23.6 0.1 copy.60
  23.7 1.7 %collective-permute-start.1 = (bf16[1,512,64]{1,2,0:T(8,128)(2,1)S(1)}, bf16[1,512,64]{1,2,0:T(8,128)(2,1)S(1)}, u32[]{:S(2)}, u32[]{:S(2)}) collective-permute-start(bf16[1,512,64]{1,2,0:T(8,128)(2,1)S(1)} %copy.60), channel_id=1, source_target_pairs={{16,0},{32,16},{48,32},{64,48},{80,64},{96,80},{112,96},{0,112},{1... | collective-permute-start | bytes 196616 | tf_op jit(solution)/shard_map/ppermute | solution.py:29
  25.4 0.6 copy.58
  26.0 2.3 %reshape.121 = bf16[16,512,64]{2,1,0:T(8,128)(2,1)S(1)} reshape(bf16[16,8,4096]{2,1,0:T(8,128)(2,1)S(1)} %copy.58) | data formatting | bytes 2097152 | tf_op jit(solution)/shard_map/reshape | solution.py:237
  28.3 0.8 copy.59
  29.2 0.2 pad_maximum_fusion.1
  29.3 0.1 slice_negate_fusion
  29.4 0.3 fusion.7
  29.7 0.1 pad_maximum_fusion.2
  29.9 2.4 %broadcast_multiply_fusion = (bf16[16,1024,192]{1,2,0:T(8,128)(2,1)S(1)}, bf16[16,1024,192]{1,2,0:T(8,128)(2,1)S(1)}) fusion(bf16[16,1024]{1,0:T(8,128)(2,1)S(1)} %pad_maximum_fusion.11, bf16[18,512,32]{1,2,0:T(8,128)(2,1)S(1)} %get-tuple-element.12, bf16[18,512,32]{1,2,0:T(8,128)(2,1)S(1)} %get-tuple-element.11, ...), kind=kLoop, calls=%fused_computation.6 | loop fusion | flops 53477376 | bytes 19038208 | tf_op jit(solution)/shard_map/mul | solution.py:110
  32.3 2.0 %fusion.10 = f32[16,32,192]{2,1,0:T(8,128)S(1)} fusion(bf16[16,1024,192]{1,2,0:T(8,128)(2,1)S(1)} %get-tuple-element.8, bf16[16,1024,192]{1,2,0:T(8,128)(2,1)S(1)} %get-tuple-element.7), kind=kOutput, calls=%fused_computation.18 | convolution fusion | flops 201326592 | bytes 7733248 | tf_op jit(solution)/shard_map/krn,krm->knm/dot_general | solution.py:114
  34.4 1.5 %fusion.2 = f32[16,32,128]{2,1,0:T(8,128)S(1)} fusion(bf16[16,1024,192]{1,2,0:T(8,128)(2,1)S(1)} %get-tuple-element.8, bf16[16,1024,192]{1,2,0:T(8,128)(2,1)S(1)} %get-tuple-element.7), kind=kOutput, calls=%fused_computation.3 | convolution fusion | flops 134217728 | bytes 5505024 | tf_op jit(solution)/shard_map/krn,krm->knm/dot_general | solution.py:114
  35.9 0.7 fusion.4
  36.6 1.2 %maximum_bitcast_fusion = f32[16,1,32,384]{3,2,1,0:T(8,128)} fusion(f32[16,32,64]{2,1,0:T(8,128)S(1)} %fusion.4, f32[16,32,128]{2,1,0:T(8,128)S(1)} %fusion.2, f32[16,32,192]{2,1,0:T(8,128)S(1)} %fusion.10), kind=kLoop, calls=%fused_computation.22 | loop fusion | flops 393216 | bytes 1572864 | tf_op jit(solution)/shard_map/reshape | solution.py:36
  37.8 7.9 %all-to-all-start.1 = ((f32[16,1,32,384]{3,2,1,0:T(8,128)}), f32[16,1,32,384]{3,2,1,0:T(8,128)S(1)}, u32[]{:S(2)}, u32[]{:S(2)}) async-start(f32[16,1,32,384]{3,2,1,0:T(8,128)} %maximum_bitcast_fusion), calls=%async_computation.1 | async-start | bytes 1572864 | tf_op jit(solution)/shard_map/all_to_all | solution.py:42
  45.7 0.1 multiply_cosine_fusion
  45.9 0.6 fusion.30
  46.5 15.0 %all-to-all-done.1 = f32[16,1,32,384]{3,2,1,0:T(8,128)S(1)} async-done(((f32[16,1,32,384]{3,2,1,0:T(8,128)}), f32[16,1,32,384]{3,2,1,0:T(8,128)S(1)}, u32[]{:S(2)}, u32[]{:S(2)}) %all-to-all-start.1) | async-done | bytes 786464 | tf_op jit(solution)/shard_map/all_to_all | solution.py:42
  61.5 0.1 fusion.31
  61.6 0.1 copy.81
  61.7 0.1 copy.82
  61.8 0.1 copy.70
  61.9 0.1 copy.83
  61.9 0.1 copy.72
  62.0 0.1 copy.73
  62.1 0.1 copy.74
  62.2 0.1 maximum_bitcast_fusion.1
  62.3 0.1 maximum_bitcast_fusion.2
  62.4 0.6 pad_maximum_fusion.9.parts_ref
  63.0 10.1 %shard_map.38 = bf16[1,192,64]{2,1,0:T(8,128)(2,1)} custom-call(f32[1,2,96,96]{3,2,1,0:T(8,128)} %pad_maximum_fusion.9.parts_ref, f32[96,64]{1,0:T(8,128)} %bitcast.46, f32[96,64]{1,0:T(8,128)} %bitcast.45), custom_call_target="tpu_custom_call" | custom-call | tf_op jit(solution)/shard_map/pallas_call | solution.py:202
  73.1 0.9 copy.75
  74.1 15.1 %all_to_all.26 = bf16[16,1,192,64]{2,3,1,0:T(8,128)(2,1)S(1)} all-to-all(bf16[16,1,192,64]{2,3,1,0:T(8,128)(2,1)S(1)} %broadcast_in_dim.5), channel_id=1, replica_groups=mesh['dop'=8,'rng'=16] {'rng'}, dimensions={0} | all-to-all | bytes 786432 | tf_op jit(solution)/shard_map/all_to_all | solution.py:54
  89.1 0.4 copy.76
  89.5 0.1 slice_negate_fusion.1
  89.6 0.2 pad_maximum_fusion.4
  89.8 1.2 %fusion.13 = f32[16,128,512]{2,1,0:T(8,128)S(1)} fusion(bf16[16,512,64]{2,1,0:T(8,128)(2,1)S(1)} %reshape.121, bf16[16,192,64]{2,1,0:T(8,128)(2,1)S(1)} %bitcast.33, bf16[16,192,64]{2,1,0:T(8,128)(2,1)S(1)} %bitcast.36), kind=kOutput, calls=%fused_computation.31 | convolution fusion | flops 134742016 | bytes 6029312 | tf_op jit(solution)/shard_map/knj,krn->kjr/dot_general | solution.py:249
  91.0 0.8 fusion.16
  91.8 2.9 %add_add_fusion = f32[16,128,512]{2,1,0:T(8,128)} fusion(f32[16,128,512]{2,1,0:T(8,128)S(1)} %fusion.16, f32[16,128,512]{2,1,0:T(8,128)S(1)} %fusion.13, bf16[16,512,64]{1,2,0:T(8,128)(2,1)S(1)} %copy-done.3, bf16[16,192,64]{2,1,0:T(8,128)(2,1)S(1)} %bitcast.38, bf16[16,192,64]{2,1,0:T(8,128)(2,1)S(1)} %bitcast.35), kind=kOutput, calls=%fused_computation.5 | convolution fusion | flops 136839168 | bytes 14417920 | tf_op jit(solution)/shard_map/knj,krn->kjr/dot_general | solution.py:249
  (20 shorter events, 0.2 us)
Async XLA Ops:
  4.0 18.6 %all-to-all-start = ((bf16[8,16,4096]{2,1,0:T(8,128)(2,1)}), bf16[8,16,4096]{2,1,0:T(8,128)(2,1)S(1)}, u32[]{:S(2)}, u32[]{:S(2)}) async-start(bf16[8,16,4096]{2,1,0:T(8,128)(2,1)} %bitcast.41), calls=%async_computation | async-start | bytes 2097152 | tf_op jit(solution)/shard_map/all_to_all | solution.py:236
  23.4 5.8 %collective-permute-start = (bf16[1,512,64]{1,2,0:T(8,128)(2,1)S(1)}, bf16[1,512,64]{1,2,0:T(8,128)(2,1)S(1)}, u32[]{:S(2)}, u32[]{:S(2)}) collective-permute-start(bf16[1,512,64]{1,2,0:T(8,128)(2,1)S(1)} %copy.57), channel_id=1, source_target_pairs={{0,16},{16,32},{32,48},{48,64},{64,80},{80,96},{96,112},{112,0},{1... | collective-permute-start | bytes 196616 | tf_op jit(solution)/shard_map/ppermute | solution.py:26
  23.7 5.5 %collective-permute-start.1 = (bf16[1,512,64]{1,2,0:T(8,128)(2,1)S(1)}, bf16[1,512,64]{1,2,0:T(8,128)(2,1)S(1)}, u32[]{:S(2)}, u32[]{:S(2)}) collective-permute-start(bf16[1,512,64]{1,2,0:T(8,128)(2,1)S(1)} %copy.60), channel_id=1, source_target_pairs={{16,0},{32,16},{48,32},{64,48},{80,64},{96,80},{112,96},{0,112},{1... | collective-permute-start | bytes 196616 | tf_op jit(solution)/shard_map/ppermute | solution.py:29
  29.9 2.4 %copy-start = (bf16[16,512,64]{1,2,0:T(8,128)(2,1)}, bf16[16,512,64]{1,2,0:T(8,128)(2,1)S(1)}, u32[]{:S(2)}) copy-start(bf16[16,512,64]{1,2,0:T(8,128)(2,1)S(1)} %get-tuple-element.14) | copy-start | bytes 3145732
  29.9 2.4 %copy-start.2 = (bf16[16,512,64]{1,2,0:T(8,128)(2,1)}, bf16[16,512,64]{1,2,0:T(8,128)(2,1)S(1)}, u32[]{:S(2)}) copy-start(bf16[16,512,64]{1,2,0:T(8,128)(2,1)S(1)} %get-tuple-element.13) | copy-start | bytes 3145732
  34.4 11.3 %copy-start.4 = (s32[64]{0:T(128)S(1)}, s32[64]{0:T(128)}, u32[]{:S(2)}) copy-start(s32[64]{0:T(128)} %param.5) | copy-start | bytes 772
  37.8 23.7 %all-to-all-start.1 = ((f32[16,1,32,384]{3,2,1,0:T(8,128)}), f32[16,1,32,384]{3,2,1,0:T(8,128)S(1)}, u32[]{:S(2)}, u32[]{:S(2)}) async-start(f32[16,1,32,384]{3,2,1,0:T(8,128)} %maximum_bitcast_fusion), calls=%async_computation.1 | async-start | bytes 1572864 | tf_op jit(solution)/shard_map/all_to_all | solution.py:42
  89.5 1.5 %copy-start.1 = (bf16[16,512,64]{1,2,0:T(8,128)(2,1)S(1)}, bf16[16,512,64]{1,2,0:T(8,128)(2,1)}, u32[]{:S(2)}) copy-start(bf16[16,512,64]{1,2,0:T(8,128)(2,1)} %copy-done) | copy-start | bytes 3145732
  89.8 2.1 %copy-start.3 = (bf16[16,512,64]{1,2,0:T(8,128)(2,1)S(1)}, bf16[16,512,64]{1,2,0:T(8,128)(2,1)}, u32[]{:S(2)}) copy-start(bf16[16,512,64]{1,2,0:T(8,128)(2,1)} %copy-done.2) | copy-start | bytes 3145732

commit v18 on v17

--- a/solution.py
+++ b/solution.py
@@ -121,7 +121,7 @@
     return jnp.concatenate(pieces, axis=-1)
 
 
-def eliminate(parts_ref, steer_re_ref, steer_im_ref, unit_ref, wr_ref, wi_ref):
+def eliminate(parts_ref, steer_ref, unit_ref, wr_ref, wi_ref):
     rows, cols = wr_ref.shape
     gap = cols - LOOKS
     lane_ids = lax.broadcasted_iota(jnp.int32, (1, cols), 1)
@@ -129,8 +129,9 @@
     diagonal = row_ids == lax.broadcasted_iota(jnp.int32, (1, rows), 1)
     same = parts_ref[0, 0]
     power = 2.0 * jnp.sum(jnp.where(diagonal, same, 0.0)) / SNAP + epsilon
-    steer_re = steer_re_ref[...]
-    steer_im = steer_im_ref[...]
+    steer = steer_ref[...]
+    steer_re = jnp.concatenate([steer[2 * b * CH : (2 * b + 1) * CH] for b in range(rows // CH)], 0)
+    steer_im = jnp.concatenate([steer[(2 * b + 1) * CH : (2 * b + 2) * CH] for b in range(rows // CH)], 0)
     wr_ref[...] = jnp.zeros(wr_ref.shape, jnp.float32)
     wi_ref[...] = jnp.zeros(wi_ref.shape, jnp.float32)
     wr_ref[:, :rows] = same / power + jnp.where(diagonal, loading, 0.0)
@@ -194,19 +195,16 @@
 def unit_vectors(same, cross, steer):
     count, size, _ = same.shape
     parts = jnp.stack([same, cross], axis=1)
-    halves = steer.reshape(size // CH, 2, CH, LOOKS)
-    steer_re = halves[:, 0].reshape(size, LOOKS)
-    steer_im = halves[:, 1].reshape(size, LOOKS)
     width = ((size + 127) // 128) * 128 + LOOKS
-    vector = pl.BlockSpec((size, LOOKS), lambda i: (0, 0))
+    vector = pl.BlockSpec((2 * size, LOOKS), lambda i: (0, 0))
     return pl.pallas_call(
         eliminate,
         grid=(count,),
-        in_specs=[pl.BlockSpec((1, 2, size, size), lambda i: (i, 0, 0, 0)), vector, vector],
+        in_specs=[pl.BlockSpec((1, 2, size, size), lambda i: (i, 0, 0, 0)), vector],
         out_specs=pl.BlockSpec((1, 2 * size, LOOKS), lambda i: (i, 0, 0)),
         out_shape=jax.ShapeDtypeStruct((count, 2 * size, LOOKS), jnp.bfloat16),
         scratch_shapes=[pltpu.VMEM((size, width), jnp.float32)] * 2,
-    )(parts, steer_re, steer_im)
+    )(parts, steer)
 
 
 def hermitian_parts(upper):

time: 95.2 us -> 95.2 us (level)
  no operation moved by 1% of the time
where the time goes in v18:
time: 95.2 us; the launch traced here: 94.7 us
  waiting for transfers between devices  28.1 us (30%)
  blocking collectives  15 us (16%)
  starting transfers between devices  14.3 us (15%)
  Pallas kernels  13.1 us (14%)
  matrix products  9.14 us (10%)
  other arithmetic  7.98 us (8%)
  local copies, waits for them, and re-layouts  6.67 us (7%)
    all_to_all x1, blocking collectives, copy_for_each(): lax.all_to_all(jnp.broadcast_to(array[None], (count, *array.shape)), axis...  15 us
    all_to_all x1, waiting for transfers between devices, sum_at_owner(): lax.all_to_all(blocks, axis, split_axis=0, concat_axis=0, tiled=True)  15 us
    all_to_all x1, waiting for transfers between devices, body(): lax.all_to_all(spectra, 'dop', split_axis=0, concat_axis=1, tiled=True)  13.1 us
    pallas_call x1, Pallas kernels, unit_vectors(): pl.pallas_call(eliminate, grid=(count,), in_specs=[pl.BlockSpec((1, 2, si...  10.1 us
    all_to_all x1, starting transfers between devices, sum_at_owner(): lax.all_to_all(blocks, axis, split_axis=0, concat_axis=0, tiled=True)  7.88 us
    dot_general x3, matrix products, body(): jnp.einsum('knj,krn->kjr', weights[:, position * 2 * CH:(position + 1) *...  4.91 us
    all_to_all x1, starting transfers between devices, body(): lax.all_to_all(spectra, 'dop', split_axis=0, concat_axis=1, tiled=True)  4.69 us
    dot_general x3, matrix products, upper_blocks(): jnp.einsum('krn,krm->knm', masked[:, :, left_pos * 2 * CH:left_pos * 2 *...  4.23 us
  transfers between devices with their start and end apart: 4, of which 2 were waited for; matrix products, arithmetic and copies ran while one was open for 6% of the time, Pallas kernels for 0%

profile of v18, /device:TPU:24, one launch (start us, length us, event | category | flops | bytes accessed | tf_op | source)
XLA Modules:
  0.0 94.7 jit_solution(15010185884319012912)
XLA Ops:
  0.0 0.9 sine_convert_fusion
  0.9 3.0 %shard_map.37 = bf16[128,4096]{1,0:T(8,128)(2,1)} custom-call(bf16[128,128]{1,0:T(8,128)(2,1)} %get-tuple-element.35.cosine_ref, bf16[128,128]{1,0:T(8,128)(2,1)} %get-tuple-element.34.sine_ref, bf16[64,2,32,128]{3,2,1,0:T(8,128)(2,1)} %echo_ref.1), custom_call_target="tpu_custom_call" | custom-call | tf_op jit(solution)/shard_map/pallas_call | solution.py:84
  3.9 4.7 %all-to-all-start = ((bf16[8,16,4096]{2,1,0:T(8,128)(2,1)}), bf16[8,16,4096]{2,1,0:T(8,128)(2,1)S(1)}, u32[]{:S(2)}, u32[]{:S(2)}) async-start(bf16[8,16,4096]{2,1,0:T(8,128)(2,1)} %bitcast.39), calls=%async_computation | async-start | bytes 2097152 | tf_op jit(solution)/shard_map/all_to_all | solution.py:234
  8.6 0.8 convert_element_type.20
  9.4 13.1 %all-to-all-done = bf16[8,16,4096]{2,1,0:T(8,128)(2,1)S(1)} async-done(((bf16[8,16,4096]{2,1,0:T(8,128)(2,1)}), bf16[8,16,4096]{2,1,0:T(8,128)(2,1)S(1)}, u32[]{:S(2)}, u32[]{:S(2)}) %all-to-all-start) | async-done | bytes 1048608 | tf_op jit(solution)/shard_map/all_to_all | solution.py:234
  22.5 0.6 slice_reduce_fusion
  23.1 0.2 slice.148
  23.3 0.1 copy.57
  23.4 0.0 collective-permute-start
  23.4 0.2 slice.151
  23.6 0.1 copy.60
  23.7 1.7 %collective-permute-start.1 = (bf16[1,512,64]{1,2,0:T(8,128)(2,1)S(1)}, bf16[1,512,64]{1,2,0:T(8,128)(2,1)S(1)}, u32[]{:S(2)}, u32[]{:S(2)}) collective-permute-start(bf16[1,512,64]{1,2,0:T(8,128)(2,1)S(1)} %copy.60), channel_id=1, source_target_pairs={{16,0},{32,16},{48,32},{64,48},{80,64},{96,80},{112,96},{0,112},{1... | collective-permute-start | bytes 196616 | tf_op jit(solution)/shard_map/ppermute | solution.py:29
  25.4 0.6 copy.58
  26.0 2.3 %reshape.124 = bf16[16,512,64]{2,1,0:T(8,128)(2,1)S(1)} reshape(bf16[16,8,4096]{2,1,0:T(8,128)(2,1)S(1)} %copy.58) | data formatting | bytes 2097152 | tf_op jit(solution)/shard_map/reshape | solution.py:235
  28.3 0.8 copy.59
  29.2 0.2 pad_maximum_fusion.1
  29.3 0.1 slice_negate_fusion
  29.4 0.3 fusion.7
  29.7 0.1 pad_maximum_fusion.2
  29.9 2.4 %broadcast_multiply_fusion = (bf16[16,1024,192]{1,2,0:T(8,128)(2,1)S(1)}, bf16[16,1024,192]{1,2,0:T(8,128)(2,1)S(1)}) fusion(bf16[16,1024]{1,0:T(8,128)(2,1)S(1)} %pad_maximum_fusion.11, bf16[18,512,32]{1,2,0:T(8,128)(2,1)S(1)} %get-tuple-element.12, bf16[18,512,32]{1,2,0:T(8,128)(2,1)S(1)} %get-tuple-element.11, ...), kind=kLoop, calls=%fused_computation.6 | loop fusion | flops 53477376 | bytes 19038208 | tf_op jit(solution)/shard_map/mul | solution.py:110
  32.3 2.0 %fusion.10 = f32[16,32,192]{2,1,0:T(8,128)S(1)} fusion(bf16[16,1024,192]{1,2,0:T(8,128)(2,1)S(1)} %get-tuple-element.8, bf16[16,1024,192]{1,2,0:T(8,128)(2,1)S(1)} %get-tuple-element.7), kind=kOutput, calls=%fused_computation.18 | convolution fusion | flops 201326592 | bytes 7733248 | tf_op jit(solution)/shard_map/krn,krm->knm/dot_general | solution.py:114
  34.4 1.5 %fusion.2 = f32[16,32,128]{2,1,0:T(8,128)S(1)} fusion(bf16[16,1024,192]{1,2,0:T(8,128)(2,1)S(1)} %get-tuple-element.8, bf16[16,1024,192]{1,2,0:T(8,128)(2,1)S(1)} %get-tuple-element.7), kind=kOutput, calls=%fused_computation.3 | convolution fusion | flops 134217728 | bytes 5505024 | tf_op jit(solution)/shard_map/krn,krm->knm/dot_general | solution.py:114
  35.9 0.7 fusion.4
  36.6 1.2 %maximum_bitcast_fusion = f32[16,1,32,384]{3,2,1,0:T(8,128)} fusion(f32[16,32,64]{2,1,0:T(8,128)S(1)} %fusion.4, f32[16,32,128]{2,1,0:T(8,128)S(1)} %fusion.2, f32[16,32,192]{2,1,0:T(8,128)S(1)} %fusion.10), kind=kLoop, calls=%fused_computation.22 | loop fusion | flops 393216 | bytes 1572864 | tf_op jit(solution)/shard_map/reshape | solution.py:36
  37.8 7.9 %all-to-all-start.1 = ((f32[16,1,32,384]{3,2,1,0:T(8,128)}), f32[16,1,32,384]{3,2,1,0:T(8,128)S(1)}, u32[]{:S(2)}, u32[]{:S(2)}) async-start(f32[16,1,32,384]{3,2,1,0:T(8,128)} %maximum_bitcast_fusion), calls=%async_computation.1 | async-start | bytes 1572864 | tf_op jit(solution)/shard_map/all_to_all | solution.py:42
  45.7 0.1 multiply_cosine_fusion
  45.9 0.6 pad_maximum_fusion.10
  46.5 15.0 %all-to-all-done.1 = f32[16,1,32,384]{3,2,1,0:T(8,128)S(1)} async-done(((f32[16,1,32,384]{3,2,1,0:T(8,128)}), f32[16,1,32,384]{3,2,1,0:T(8,128)S(1)}, u32[]{:S(2)}, u32[]{:S(2)}) %all-to-all-start.1) | async-done | bytes 786464 | tf_op jit(solution)/shard_map/all_to_all | solution.py:42
  61.6 0.1 fusion.30
  61.7 0.1 copy.81
  61.7 0.1 copy.82
  61.8 0.1 copy.70
  61.9 0.1 copy.83
  62.0 0.1 copy.72
  62.0 0.1 copy.73
  62.1 0.1 copy.74
  62.2 0.1 maximum_bitcast_fusion.1
  62.3 0.1 maximum_bitcast_fusion.2
  62.4 0.6 pad_maximum_fusion.9.parts_ref
  63.1 10.1 %shard_map.38 = bf16[1,192,64]{2,1,0:T(8,128)(2,1)} custom-call(f32[1,2,96,96]{3,2,1,0:T(8,128)} %pad_maximum_fusion.9.parts_ref, f32[192,64]{1,0:T(8,128)} %bitcast.41), custom_call_target="tpu_custom_call" | custom-call | tf_op jit(solution)/shard_map/pallas_call | solution.py:200
  73.2 0.9 copy.75
  74.1 15.0 %all_to_all.26 = bf16[16,1,192,64]{2,3,1,0:T(8,128)(2,1)S(1)} all-to-all(bf16[16,1,192,64]{2,3,1,0:T(8,128)(2,1)S(1)} %broadcast_in_dim.5), channel_id=1, replica_groups=mesh['dop'=8,'rng'=16] {'rng'}, dimensions={0} | all-to-all | bytes 786432 | tf_op jit(solution)/shard_map/all_to_all | solution.py:54
  89.1 0.4 copy.76
  89.5 0.1 slice_negate_fusion.1
  89.6 0.2 pad_maximum_fusion.4
  89.8 1.2 %fusion.13 = f32[16,128,512]{2,1,0:T(8,128)S(1)} fusion(bf16[16,512,64]{2,1,0:T(8,128)(2,1)S(1)} %reshape.124, bf16[16,192,64]{2,1,0:T(8,128)(2,1)S(1)} %bitcast.31, bf16[16,192,64]{2,1,0:T(8,128)(2,1)S(1)} %bitcast.34), kind=kOutput, calls=%fused_computation.31 | convolution fusion | flops 134742016 | bytes 6029312 | tf_op jit(solution)/shard_map/knj,krn->kjr/dot_general | solution.py:247
  91.0 0.8 fusion.16
  91.9 2.9 %add_add_fusion = f32[16,128,512]{2,1,0:T(8,128)} fusion(f32[16,128,512]{2,1,0:T(8,128)S(1)} %fusion.16, f32[16,128,512]{2,1,0:T(8,128)S(1)} %fusion.13, bf16[16,512,64]{1,2,0:T(8,128)(2,1)S(1)} %copy-done.3, bf16[16,192,64]{2,1,0:T(8,128)(2,1)S(1)} %bitcast.36, bf16[16,192,64]{2,1,0:T(8,128)(2,1)S(1)} %bitcast.33), kind=kOutput, calls=%fused_computation.5 | convolution fusion | flops 136839168 | bytes 14417920 | tf_op jit(solution)/shard_map/knj,krn->kjr/dot_general | solution.py:247
  (19 shorter events, 0.1 us)
Async XLA Ops:
  3.9 18.6 %all-to-all-start = ((bf16[8,16,4096]{2,1,0:T(8,128)(2,1)}), bf16[8,16,4096]{2,1,0:T(8,128)(2,1)S(1)}, u32[]{:S(2)}, u32[]{:S(2)}) async-start(bf16[8,16,4096]{2,1,0:T(8,128)(2,1)} %bitcast.39), calls=%async_computation | async-start | bytes 2097152 | tf_op jit(solution)/shard_map/all_to_all | solution.py:234
  23.4 5.8 %collective-permute-start = (bf16[1,512,64]{1,2,0:T(8,128)(2,1)S(1)}, bf16[1,512,64]{1,2,0:T(8,128)(2,1)S(1)}, u32[]{:S(2)}, u32[]{:S(2)}) collective-permute-start(bf16[1,512,64]{1,2,0:T(8,128)(2,1)S(1)} %copy.57), channel_id=1, source_target_pairs={{0,16},{16,32},{32,48},{48,64},{64,80},{80,96},{96,112},{112,0},{1... | collective-permute-start | bytes 196616 | tf_op jit(solution)/shard_map/ppermute | solution.py:26
  23.7 5.5 %collective-permute-start.1 = (bf16[1,512,64]{1,2,0:T(8,128)(2,1)S(1)}, bf16[1,512,64]{1,2,0:T(8,128)(2,1)S(1)}, u32[]{:S(2)}, u32[]{:S(2)}) collective-permute-start(bf16[1,512,64]{1,2,0:T(8,128)(2,1)S(1)} %copy.60), channel_id=1, source_target_pairs={{16,0},{32,16},{48,32},{64,48},{80,64},{96,80},{112,96},{0,112},{1... | collective-permute-start | bytes 196616 | tf_op jit(solution)/shard_map/ppermute | solution.py:29
  29.8 2.4 %copy-start = (bf16[16,512,64]{1,2,0:T(8,128)(2,1)}, bf16[16,512,64]{1,2,0:T(8,128)(2,1)S(1)}, u32[]{:S(2)}) copy-start(bf16[16,512,64]{1,2,0:T(8,128)(2,1)S(1)} %get-tuple-element.14) | copy-start | bytes 3145732
  29.9 2.4 %copy-start.2 = (bf16[16,512,64]{1,2,0:T(8,128)(2,1)}, bf16[16,512,64]{1,2,0:T(8,128)(2,1)S(1)}, u32[]{:S(2)}) copy-start(bf16[16,512,64]{1,2,0:T(8,128)(2,1)S(1)} %get-tuple-element.13) | copy-start | bytes 3145732
  34.4 11.3 %copy-start.4 = (s32[64]{0:T(128)S(1)}, s32[64]{0:T(128)}, u32[]{:S(2)}) copy-start(s32[64]{0:T(128)} %param.5) | copy-start | bytes 772
  37.8 23.7 %all-to-all-start.1 = ((f32[16,1,32,384]{3,2,1,0:T(8,128)}), f32[16,1,32,384]{3,2,1,0:T(8,128)S(1)}, u32[]{:S(2)}, u32[]{:S(2)}) async-start(f32[16,1,32,384]{3,2,1,0:T(8,128)} %maximum_bitcast_fusion), calls=%async_computation.1 | async-start | bytes 1572864 | tf_op jit(solution)/shard_map/all_to_all | solution.py:42
  89.5 1.5 %copy-start.1 = (bf16[16,512,64]{1,2,0:T(8,128)(2,1)S(1)}, bf16[16,512,64]{1,2,0:T(8,128)(2,1)}, u32[]{:S(2)}) copy-start(bf16[16,512,64]{1,2,0:T(8,128)(2,1)} %copy-done) | copy-start | bytes 3145732
  89.8 2.1 %copy-start.3 = (bf16[16,512,64]{1,2,0:T(8,128)(2,1)S(1)}, bf16[16,512,64]{1,2,0:T(8,128)(2,1)}, u32[]{:S(2)}) copy-start(bf16[16,512,64]{1,2,0:T(8,128)(2,1)} %copy-done.2) | copy-start | bytes 3145732
